TPU v7x, 256 devices: a whole 4x4x8 slice. The times are simulated.
256 devices in a mesh: along: 32 (over y_hi, z, core), across: 8 (over x, y_lo).
Axes of the slice: x: 4, y: 4 (y_hi: 2, y_lo: 2; y = y_hi * 2 + y_lo), z: 8, core: 2. Of those that a mesh axis runs over, the one named last changes fastest.
Arguments:
- disp: float32 [2, 4096, 4096], P(None, 'along', 'across'), may hold values from -0.1 to 0.1
- velocity: float32 [2, 4096, 4096], P(None, 'along', 'across'), may hold values from -6 to 6
- bond_bits: int32 [2, 4096, 4096], P(None, 'along', 'across'), may hold values from 0 to 16383
- panel_pos: float32 [2048, 2], P('along'), as said below
- contact_list: int32 [32, 4], P('along'), may hold values from 0 to 255, as said below
Outputs:
- new_disp: float32 [2, 4096, 4096], P(None, 'along', 'across')
- new_velocity: float32 [2, 4096, 4096], P(None, 'along', 'across')
- damage: float32 [4096, 4096], P('along', 'across')
- panel_force: float32 [2048, 2], P('along')
Inputs may be any that keep to these rules, and one draw needn't show every extreme that they name: `contact_list`: each row lists 4 different tiles. `panel_pos`: every panel lies inside some tile of its block's contact list.
All inputs are finite; a program needn't handle non-finite values.
Results may differ from a plain program's by a relative error of at most 0.0003.
Values sent between devices are 32-bit elements; how exact they have to be, the bound alone decides.
No kernel may reach another device: no remote copies, remote signals or barrier semaphores. Data moves between devices by JAX's collectives and lax.ppermute only.
A program may use at most 64 MiB of HBM per device.

v0:
```python
import jax
import jax.numpy as jnp
from jax import lax
from jax.experimental import pallas as pl
from jax.experimental.pallas import tpu as pltpu
from jax.sharding import PartitionSpec as P

PAN_DEV = 64


offsets = [(rr, cc) for rr in range(-3, 4) for cc in range(-3, 4) if 0 < rr * rr + cc * cc <= 9]


def xor_pairs(count, bit):
    return [(i, i ^ (1 << bit)) for i in range(count)]


def contact_kernel(meta_ref, win_ref, pos_ref, xr_ref, xc_ref, out_ref):
    out_ref[...] = jnp.zeros_like(out_ref)
    panels = out_ref.shape[2]

    def per_block(k, carry):
        block = meta_ref[1 + k]

        def per_panel(j, carry):
            slot = block * panels + j
            centre_row = pos_ref[2 * slot]
            centre_col = pos_ref[2 * slot + 1]
            first_row = win_ref[4 * slot]
            row_groups = win_ref[4 * slot + 1]
            first_col = win_ref[4 * slot + 2]
            col_groups = win_ref[4 * slot + 3]

            def per_row(r, accs):
                row = pl.multiple_of((first_row + r) * 8, 8)

                def per_col(c, accs):
                    col = pl.multiple_of((first_col + c) * 128, 128)
                    delta_row = centre_row - xr_ref[pl.ds(row, 8), pl.ds(col, 128)]
                    delta_col = centre_col - xc_ref[pl.ds(row, 8), pl.ds(col, 128)]
                    push = 0.5 * jnp.maximum(
                        4.0 - delta_row * delta_row - delta_col * delta_col, 0.0
                    )
                    return (accs[0] + push * delta_row, accs[1] + push * delta_col)

                return lax.fori_loop(0, col_groups, per_col, accs)

            zero = jnp.zeros((8, 128), jnp.float32)
            acc_row, acc_col = lax.fori_loop(0, row_groups, per_row, (zero, zero))
            out_ref[block, 0, pl.ds(j, 1), :] = jnp.sum(acc_row, axis=0, keepdims=True)
            out_ref[block, 1, pl.ds(j, 1), :] = jnp.sum(acc_col, axis=0, keepdims=True)
            return carry

        return lax.fori_loop(0, panels, per_panel, carry)

    lax.fori_loop(0, meta_ref[0], per_block, 0)


def contact_sums(meta, windows, positions, rows_x, cols_x):
    blocks = meta.shape[0] - 1
    smem = pl.BlockSpec(memory_space=pltpu.SMEM)
    vmem = pl.BlockSpec(memory_space=pltpu.VMEM)
    return pl.pallas_call(
        contact_kernel,
        out_shape=jax.ShapeDtypeStruct((blocks, 2, PAN_DEV, 128), jnp.float32),
        in_specs=[smem, smem, smem, vmem, vmem],
        out_specs=vmem,
    )(meta, windows, positions, rows_x, cols_x)


def with_halo(block, sides, width):
    for axis, dim in sides:
        count = lax.axis_size(axis)
        forward = [(i, i + 1) for i in range(count - 1)]
        backward = [(target, source) for source, target in forward]
        low = lax.ppermute(
            lax.slice_in_dim(block, block.shape[dim] - width, None, axis=dim), axis, forward
        )
        high = lax.ppermute(lax.slice_in_dim(block, 0, width, axis=dim), axis, backward)
        block = jnp.concatenate([low, block, high], axis=dim)
    return block


def forces(padded, bits, present_pad, rows, cols):
    centre = padded[:, 3 : 3 + rows, 3 : 3 + cols]
    total_row = jnp.zeros((rows, cols), jnp.float32)
    total_col = jnp.zeros((rows, cols), jnp.float32)
    kept_sum = jnp.zeros((rows, cols), jnp.float32)
    exist_sum = jnp.zeros((rows, cols), jnp.float32)
    for index, (row_off, col_off) in enumerate(offsets):
        other = padded[:, 3 + row_off : 3 + row_off + rows, 3 + col_off : 3 + col_off + cols]
        present = present_pad[3 + row_off : 3 + row_off + rows, 3 + col_off : 3 + col_off + cols]
        flag = jnp.bitwise_and(jnp.right_shift(bits[index // 14], index % 14), 1).astype(
            jnp.float32
        )
        keep = flag * present
        row_part = row_off + (other[0] - centre[0])
        col_part = col_off + (other[1] - centre[1])
        length = jnp.sqrt(row_part * row_part + col_part * col_part)
        rest = float((row_off * row_off + col_off * col_off) ** 0.5)
        coeff = keep * (length - rest) / (rest * length)
        total_row = total_row + coeff * row_part
        total_col = total_col + coeff * col_part
        kept_sum = kept_sum + keep
        exist_sum = exist_sum + present
    return (jnp.stack([total_row, total_col]), kept_sum, exist_sum)


def body(disp, velocity, bond_bits, panel_pos, contact_list):
    rows, cols = (disp.shape[1], disp.shape[2])
    along_count = lax.axis_size("along")
    across_count = lax.axis_size("across")
    total_rows = rows * along_count
    total_cols = cols * across_count
    row_base = lax.axis_index("along") * rows
    col_base = lax.axis_index("across") * cols
    state_u, state_v = (disp, velocity)
    damage = None
    for step in range(2):
        padded = with_halo(state_u, (("along", 1), ("across", 2)), 3)
        grid_row = row_base - 3 + jnp.arange(rows + 2 * 3, dtype=jnp.int32)
        grid_col = col_base - 3 + jnp.arange(cols + 2 * 3, dtype=jnp.int32)
        inside_row = (grid_row >= 0) & (grid_row < total_rows)
        inside_col = (grid_col >= 0) & (grid_col < total_cols)
        force, kept_sum, exist_sum = forces(
            padded,
            bond_bits,
            (inside_row[:, None] & inside_col[None, :]).astype(jnp.float32),
            rows,
            cols,
        )
        if step == 0:
            damage = 1.0 - kept_sum / exist_sum
        state_v = state_v + 10.0 * force
        state_u = state_u + 0.05 * state_v
    block_count = lax.axis_size("along")
    packed = jnp.concatenate(
        [panel_pos.reshape(1, -1), contact_list.astype(jnp.float32).reshape(1, -1)], axis=1
    )
    gathered = lax.all_to_all(
        jnp.broadcast_to(packed[None], (block_count,) + packed.shape), "along", 0, 0, tiled=True
    ).reshape(block_count, -1)
    all_pos = gathered[:, : 2 * PAN_DEV].reshape(block_count, PAN_DEV, 2)
    all_lists = gathered[:, 2 * PAN_DEV :].astype(jnp.int32)
    my_tile = lax.axis_index("along") * across_count + lax.axis_index("across")
    listed = jnp.any(all_lists == my_tile, axis=1).astype(jnp.int32)
    prefix = jnp.cumsum(listed)
    n_listed = prefix[-1]
    slots = jnp.arange(block_count, dtype=jnp.int32)
    listed_blocks = jnp.sum((prefix[None, :] <= slots[:, None]).astype(jnp.int32), axis=1)
    rows_x = (row_base + jnp.arange(rows, dtype=jnp.int32)).astype(jnp.float32)[:, None] + state_u[0]
    cols_x = (col_base + jnp.arange(cols, dtype=jnp.int32)).astype(jnp.float32)[None, :] + state_u[1]
    reach_row = 3.0 + jnp.max(jnp.abs(state_u[0]))
    reach_col = 3.0 + jnp.max(jnp.abs(state_u[1]))
    local_row = all_pos[:, :, 0] - row_base.astype(jnp.float32)
    local_col = all_pos[:, :, 1] - col_base.astype(jnp.float32)
    row_lo = jnp.clip(jnp.floor(local_row - reach_row), 0, rows).astype(jnp.int32)
    row_hi = jnp.clip(jnp.floor(local_row + reach_row) + 1, 0, rows).astype(jnp.int32)
    col_lo = jnp.clip(jnp.floor(local_col - reach_col), 0, cols).astype(jnp.int32)
    col_hi = jnp.clip(jnp.floor(local_col + reach_col) + 1, 0, cols).astype(jnp.int32)
    first_row = row_lo // 8
    row_groups = jnp.maximum((row_hi + 7) // 8 - first_row, 0)
    first_col = col_lo // 128
    col_groups = jnp.maximum((col_hi + 127) // 128 - first_col, 0)
    windows = jnp.stack([first_row, row_groups, first_col, col_groups], axis=-1).reshape(-1)
    meta = jnp.concatenate([n_listed[None], listed_blocks])
    sums = contact_sums(meta, windows, all_pos.reshape(-1), rows_x, cols_x)
    partials = jnp.transpose(jnp.sum(sums, axis=-1), (0, 2, 1))
    arrived = lax.all_to_all(
        partials.reshape(block_count, 1, 2 * PAN_DEV), "along", 0, 0, tiled=True
    )
    share = jnp.sum(arrived, axis=0)
    for k in range(across_count.bit_length() - 1):
        share = share + lax.ppermute(share, "across", xor_pairs(across_count, k))
    panel_force = share.reshape(PAN_DEV, 2)
    return (state_u, state_v, damage, panel_force)


def solution(mesh):
    return jax.shard_map(
        body,
        mesh=mesh,
        in_specs=(
            P(None, "along", "across"),
            P(None, "along", "across"),
            P(None, "along", "across"),
            P("along", None),
            P("along", None),
        ),
        out_specs=(
            P(None, "along", "across"),
            P(None, "along", "across"),
            P("along", "across"),
            P("along", None),
        ),
        check_vma=False,
    )
```

profile of v0, /device:TPU:12, one launch (start us, length us, event | category | flops | bytes accessed | tf_op | source)
XLA Modules:
  0.0 140.0 jit_solution(7753673321368067288)
XLA Ops:
  0.6 1.4 fusion.245
  2.0 1.7 %collective-permute-start = (f32[2,3,512]{2,1,0:T(4,128)}, f32[2,3,512]{2,1,0:T(4,128)S(1)}, u32[]{:S(2)}, u32[]{:S(2)}) collective-permute-start(f32[2,3,512]{2,1,0:T(4,128)} %get-tuple-element.93), channel_id=1, source_target_pairs={{0,8},{8,16},{16,24},{24,32},{32,40},{40,48},{48,56},{56,64},{64,7... | collective-permute-start | bytes 36872 | tf_op jit(solution)/shard_map/ppermute | solution.py:76
  3.8 1.3 collective-permute-start.1
  7.3 14.5 %all-to-all-start = ((f32[32,1,132]{2,1,0:T(1,128)}), f32[32,1,132]{2,1,0:T(1,128)}, u32[]{:S(2)}, u32[]{:S(2)}) async-start(f32[32,1,132]{2,1,0:T(1,128)} %broadcast_in_dim.5), calls=%async_computation | async-start | bytes 65536 | tf_op jit(solution)/shard_map/all_to_all | solution.py:140
  21.9 3.7 %divide_subtract_fusion = (f32[128,512]{1,0:T(8,128)}, f32[128,512]{1,0:T(8,128)S(1)}, f32[128,512]{1,0:T(8,128)S(1)}, f32[128,512]{1,0:T(8,128)S(1)}, f32[128,5...) fusion(f32[134,518]{1,0:T(8,128)S(1)} %and_convert_fusion, ...), kind=kLoop, calls=%fused_computation.403 | loop fusion | flops 11010048 | bytes 14417920 | tf_op jit(solution)/shard_map/sub | solution.py:133
  25.8 1.2 pad_maximum_fusion.8
  27.0 3.9 %collective-permute-start.2 = (f32[2,134,3]{2,1,0:T(8,128)S(1)}, f32[2,134,3]{2,1,0:T(8,128)S(1)}, u32[]{:S(2)}, u32[]{:S(2)}) collective-permute-start(f32[2,134,3]{2,1,0:T(8,128)S(1)} %get-tuple-element.86), channel_id=1, source_target_pairs={{0,1},{1,2},{2,3},{3,4},{4,5},{5,6},{6,7},{8,9},{9,10},{10,11},{11... | collective-permute-start | bytes 9656 | tf_op jit(solution)/shard_map/ppermute | solution.py:76
  30.9 2.0 %collective-permute-start.3 = (f32[2,134,3]{2,1,0:T(8,128)S(1)}, f32[2,134,3]{2,1,0:T(8,128)S(1)}, u32[]{:S(2)}, u32[]{:S(2)}) collective-permute-start(f32[2,134,3]{2,1,0:T(8,128)S(1)} %get-tuple-element.85), channel_id=1, source_target_pairs={{1,0},{2,1},{3,2},{4,3},{5,4},{6,5},{7,6},{9,8},{10,9},{11,10},{12... | collective-permute-start | bytes 9656 | tf_op jit(solution)/shard_map/ppermute | solution.py:79
  33.6 1.1 collective-permute-done.2
  34.6 4.5 %collective-permute-done.3 = f32[2,134,3]{2,1,0:T(8,128)S(1)} collective-permute-done((f32[2,134,3]{2,1,0:T(8,128)S(1)}, f32[2,134,3]{2,1,0:T(8,128)S(1)}, u32[]{:S(2)}, u32[]{:S(2)}) %collective-permute-start.3) | collective-permute-done | bytes 3248 | tf_op jit(solution)/shard_map/ppermute | solution.py:79
  39.2 1.1 pad_maximum_fusion
  40.3 6.5 %add_bitcast_fusion.3 = (f32[1,128,512]{2,1,0:T(8,128)S(1)}, f32[128,512]{1,0:T(8,128)S(1)}, f32[128,512]{1,0:T(8,128)S(1)}, f32[128,512]{1,0:T(8,128)S(1)}, f32...) fusion(f32[128,512]{1,0:T(8,128)S(1)} %get-tuple-element.51, ...), kind=kLoop, calls=%fused_computation.435 | loop fusion | flops 24182784 | bytes 24395776 | tf_op jit(solution)/shard_map/stack | solution.py:106
  46.9 5.1 %add_bitcast_fusion.2 = f32[1,128,512]{2,1,0:T(8,128)S(1)} fusion(f32[128,512]{1,0:T(8,128)S(1)} %get-tuple-element.78, f32[128,512]{1,0:T(8,128)S(1)} %get-tuple-element.77, f32[128,512]{1,0:T(8,128)S(1)} %get-tuple-element.76, f32[128,512]{1,0:T(8,128)S(1)} %get-tuple-element.75, f32[128,512]{1,0:T(8,128)S(1)} %get-tuple-element.74, ...), kind=kLoop, calls=%fused_computation.434 | loop fusion | flops 19136512 | bytes 20201472 | tf_op jit(solution)/shard_map/stack | solution.py:106
  52.8 1.4 %collective-permute-start.4 = (f32[2,3,512]{2,1,0:T(4,128)S(1)}, f32[2,3,512]{2,1,0:T(4,128)S(1)}, u32[]{:S(2)}, u32[]{:S(2)}) collective-permute-start(f32[2,3,512]{2,1,0:T(4,128)S(1)} %get-tuple-element.91), channel_id=1, source_target_pairs={{0,8},{8,16},{16,24},{24,32},{32,40},{40,48},{48,56},{56,64},{64,7... | collective-permute-start | bytes 36872 | tf_op jit(solution)/shard_map/ppermute | solution.py:76
  54.2 1.3 collective-permute-start.5
  55.6 3.7 %collective-permute-done.5 = f32[2,3,512]{2,1,0:T(4,128)S(1)} collective-permute-done((f32[2,3,512]{2,1,0:T(4,128)S(1)}, f32[2,3,512]{2,1,0:T(4,128)S(1)}, u32[]{:S(2)}, u32[]{:S(2)}) %collective-permute-start.5) | collective-permute-done | bytes 12320 | tf_op jit(solution)/shard_map/ppermute | solution.py:79
  60.0 3.2 %collective-permute-start.6 = (f32[2,134,3]{2,1,0:T(8,128)}, f32[2,134,3]{2,1,0:T(8,128)}, u32[]{:S(2)}, u32[]{:S(2)}) collective-permute-start(f32[2,134,3]{2,1,0:T(8,128)} %get-tuple-element.82), channel_id=1, source_target_pairs={{0,1},{1,2},{2,3},{3,4},{4,5},{5,6},{6,7},{8,9},{9,10},{10,11},{11... | collective-permute-start | bytes 9656 | tf_op jit(solution)/shard_map/ppermute | solution.py:76
  63.3 2.8 %collective-permute-start.7 = (f32[2,134,3]{2,1,0:T(8,128)}, f32[2,134,3]{2,1,0:T(8,128)}, u32[]{:S(2)}, u32[]{:S(2)}) collective-permute-start(f32[2,134,3]{2,1,0:T(8,128)} %get-tuple-element.81), channel_id=1, source_target_pairs={{1,0},{2,1},{3,2},{4,3},{5,4},{6,5},{7,6},{9,8},{10,9},{11,10},{12... | collective-permute-start | bytes 9656 | tf_op jit(solution)/shard_map/ppermute | solution.py:79
  66.1 1.1 collective-permute-done.6
  67.3 4.4 %collective-permute-done.7 = f32[2,134,3]{2,1,0:T(8,128)} collective-permute-done((f32[2,134,3]{2,1,0:T(8,128)}, f32[2,134,3]{2,1,0:T(8,128)}, u32[]{:S(2)}, u32[]{:S(2)}) %collective-permute-start.7) | collective-permute-done | bytes 3248 | tf_op jit(solution)/shard_map/ppermute | solution.py:79
  71.7 1.3 pad_maximum_fusion.1
  73.0 8.1 %add_bitcast_fusion.1 = (f32[1,128,512]{2,1,0:T(8,128)S(1)}, f32[128,512]{1,0:T(8,128)S(1)}, f32[128,512]{1,0:T(8,128)S(1)}, f32[128,512]{1,0:T(8,128)S(1)}, f32...) fusion(f32[128,512]{1,0:T(8,128)S(1)} %copy-done.10, ...), kind=kLoop, calls=%fused_computation.405 | loop fusion | flops 24576000 | bytes 23887872 | tf_op jit(solution)/shard_map/stack | solution.py:106
  81.1 4.5 %add_bitcast_fusion = f32[1,128,512]{2,1,0:T(8,128)S(1)} fusion(f32[128,512]{1,0:T(8,128)S(1)} %get-tuple-element.69, f32[128,512]{1,0:T(8,128)S(1)} %get-tuple-element.68, f32[128,512]{1,0:T(8,128)S(1)} %get-tuple-element.67, f32[128,512]{1,0:T(8,128)S(1)} %get-tuple-element.66, f32[128,512]{1,0:T(8,128)S(1)} %get-tuple-element.65, ...), kind=kLoop, calls=%fused_computation.404 | loop fusion | flops 16711680 | bytes 17072128 | tf_op jit(solution)/shard_map/stack | solution.py:106
  86.7 1.6 %fusion.236 = (f32[128,512]{1,0:T(8,128)}, f32[128,512]{1,0:T(8,128)}, f32[]{:T(128)}, f32[]{:T(128)}) fusion(f32[2,128,512]{2,1,0:T(8,128)S(1)} %get-tuple-element.55, f32[512]{0:T(512)S(1)} %add_convert_fusion, f32[128]{0:T(128)S(1)} %add_convert_fusion.1), kind=kLoop, calls=%fused_computation.465 | loop fusion | flops 393214 | bytes 1051144 | tf_op jit(solution)/shard_map/add | solution.py:152
  94.0 1.3 reshape.499.win_ref
  95.3 1.3 pad_add_fusion.1.meta_ref
  96.6 15.0 %shard_map.84 = f32[32,2,64,128]{3,2,1,0:T(8,128)} custom-call(s32[33]{0:T(128)} %pad_add_fusion.1.meta_ref, s32[8192]{0:T(1024)} %reshape.499.win_ref, f32[4096]{0:T(1024)} %get-tuple-element.97.pos_ref, f32[128,512]{1,0:T(8,128)} %get-tuple-element.88.xr_ref, f32[128,512]{1,0:T(8,128)} %get-tuple-element.87.xc_ref), custom_call_target="tpu_custom_call" | custom-call | tf_op jit(solution)/shard_map/pallas_call | solution.py:63
  111.7 2.2 %reduce_sum.30 = f32[32,2,64]{2,1,0:T(2,128)S(1)} reduce(f32[32,2,64,128]{3,2,1,0:T(8,128)} %shard_map.84, f32[]{:T(128)} %constant.180.clone.1), dimensions={3}, to_apply=%region_5.6 | reduce | flops 520192 | bytes 2113540 | tf_op jit(solution)/shard_map/reduce_sum | solution.py:168
  114.0 12.9 %all_to_all.10 = f32[32,1,128]{2,1,0:T(1,128)S(1)} all-to-all(f32[32,1,128]{2,1,0:T(1,128)S(1)} %copy.33), channel_id=1, replica_groups=mesh['along'=32,'across'=8] {'along'}, dimensions={0} | all-to-all | bytes 32768 | tf_op jit(solution)/shard_map/all_to_all | solution.py:169
  127.1 3.5 %collective-permute-done.8 = f32[1,128]{1,0:T(1,128)S(1)} collective-permute-done((f32[1,128]{1,0:T(1,128)S(1)}, f32[1,128]{1,0:T(1,128)S(1)}, u32[]{:S(2)}, u32[]{:S(2)}) %collective-permute-start.8) | collective-permute-done | bytes 544 | tf_op jit(solution)/shard_map/ppermute | solution.py:174
  130.6 3.5 %collective-permute-done.9 = f32[1,128]{1,0:T(1,128)S(1)} collective-permute-done((f32[1,128]{1,0:T(1,128)S(1)}, f32[1,128]{1,0:T(1,128)S(1)}, u32[]{:S(2)}, u32[]{:S(2)}) %collective-permute-start.9) | collective-permute-done | bytes 544 | tf_op jit(solution)/shard_map/ppermute | solution.py:174
  134.1 5.0 %collective-permute-done.10 = f32[1,128]{1,0:T(1,128)S(1)} collective-permute-done((f32[1,128]{1,0:T(1,128)S(1)}, f32[1,128]{1,0:T(1,128)S(1)}, u32[]{:S(2)}, u32[]{:S(2)}) %collective-permute-start.10) | collective-permute-done | bytes 544 | tf_op jit(solution)/shard_map/ppermute | solution.py:174
  (112 shorter events, 11.3 us)
Async XLA Ops:
  2.0 23.8 %collective-permute-start = (f32[2,3,512]{2,1,0:T(4,128)}, f32[2,3,512]{2,1,0:T(4,128)S(1)}, u32[]{:S(2)}, u32[]{:S(2)}) collective-permute-start(f32[2,3,512]{2,1,0:T(4,128)} %get-tuple-element.93), channel_id=1, source_target_pairs={{0,8},{8,16},{16,24},{24,32},{32,40},{40,48},{48,56},{56,64},{64,7... | collective-permute-start | bytes 36872 | tf_op jit(solution)/shard_map/ppermute | solution.py:76
  3.8 22.0 %collective-permute-start.1 = (f32[2,3,512]{2,1,0:T(4,128)}, f32[2,3,512]{2,1,0:T(4,128)}, u32[]{:S(2)}, u32[]{:S(2)}) collective-permute-start(f32[2,3,512]{2,1,0:T(4,128)} %get-tuple-element.94), channel_id=1, source_target_pairs={{8,0},{16,8},{24,16},{32,24},{40,32},{48,40},{56,48},{64,56},{72,6... | collective-permute-start | bytes 36872 | tf_op jit(solution)/shard_map/ppermute | solution.py:79
  7.3 82.3 %all-to-all-start = ((f32[32,1,132]{2,1,0:T(1,128)}), f32[32,1,132]{2,1,0:T(1,128)}, u32[]{:S(2)}, u32[]{:S(2)}) async-start(f32[32,1,132]{2,1,0:T(1,128)} %broadcast_in_dim.5), calls=%async_computation | async-start | bytes 65536 | tf_op jit(solution)/shard_map/all_to_all | solution.py:140
  25.6 14.7 %copy-start.13 = (f32[128,512]{1,0:T(8,128)}, f32[128,512]{1,0:T(8,128)S(1)}, u32[]{:S(2)}) copy-start(f32[128,512]{1,0:T(8,128)S(1)} %get-tuple-element.52) | copy-start | bytes 786436
  25.6 14.7 %copy-start.15 = (f32[128,512]{1,0:T(8,128)}, f32[128,512]{1,0:T(8,128)S(1)}, u32[]{:S(2)}) copy-start(f32[128,512]{1,0:T(8,128)S(1)} %get-tuple-element.53) | copy-start | bytes 786436
  25.6 14.7 %copy-start.17 = (f32[128,512]{1,0:T(8,128)}, f32[128,512]{1,0:T(8,128)S(1)}, u32[]{:S(2)}) copy-start(f32[128,512]{1,0:T(8,128)S(1)} %get-tuple-element.54) | copy-start | bytes 786436
  25.6 21.2 %copy-start.1 = (f32[128,512]{1,0:T(8,128)}, f32[128,512]{1,0:T(8,128)S(1)}, u32[]{:S(2)}) copy-start(f32[128,512]{1,0:T(8,128)S(1)} %get-tuple-element.47) | copy-start | bytes 786436
  25.6 21.2 %copy-start.3 = (f32[128,512]{1,0:T(8,128)}, f32[128,512]{1,0:T(8,128)S(1)}, u32[]{:S(2)}) copy-start(f32[128,512]{1,0:T(8,128)S(1)} %get-tuple-element.48) | copy-start | bytes 786436
  25.6 21.2 %copy-start.5 = (f32[128,512]{1,0:T(8,128)}, f32[128,512]{1,0:T(8,128)S(1)}, u32[]{:S(2)}) copy-start(f32[128,512]{1,0:T(8,128)S(1)} %get-tuple-element.49) | copy-start | bytes 786436
  25.6 21.2 %copy-start.7 = (f32[128,512]{1,0:T(8,128)}, f32[128,512]{1,0:T(8,128)S(1)}, u32[]{:S(2)}) copy-start(f32[128,512]{1,0:T(8,128)S(1)} %get-tuple-element.50) | copy-start | bytes 786436
  25.6 21.2 %copy-start.9 = (f32[128,512]{1,0:T(8,128)}, f32[128,512]{1,0:T(8,128)S(1)}, u32[]{:S(2)}) copy-start(f32[128,512]{1,0:T(8,128)S(1)} %get-tuple-element.51) | copy-start | bytes 786436
  25.6 21.2 %copy-start.19 = (f32[128,512]{1,0:T(8,128)}, f32[128,512]{1,0:T(8,128)S(1)}, u32[]{:S(2)}) copy-start(f32[128,512]{1,0:T(8,128)S(1)} %get-tuple-element.38) | copy-start | bytes 786436
  25.7 21.2 %copy-start.20 = (f32[128,512]{1,0:T(8,128)}, f32[128,512]{1,0:T(8,128)S(1)}, u32[]{:S(2)}) copy-start(f32[128,512]{1,0:T(8,128)S(1)} %get-tuple-element.39) | copy-start | bytes 786436
  25.7 21.2 %copy-start.21 = (f32[128,512]{1,0:T(8,128)}, f32[128,512]{1,0:T(8,128)S(1)}, u32[]{:S(2)}) copy-start(f32[128,512]{1,0:T(8,128)S(1)} %get-tuple-element.40) | copy-start | bytes 786436
  25.7 21.2 %copy-start.22 = (f32[128,512]{1,0:T(8,128)}, f32[128,512]{1,0:T(8,128)S(1)}, u32[]{:S(2)}) copy-start(f32[128,512]{1,0:T(8,128)S(1)} %get-tuple-element.41) | copy-start | bytes 786436
  25.7 21.2 %copy-start.23 = (f32[128,512]{1,0:T(8,128)}, f32[128,512]{1,0:T(8,128)S(1)}, u32[]{:S(2)}) copy-start(f32[128,512]{1,0:T(8,128)S(1)} %get-tuple-element.42) | copy-start | bytes 786436
  25.7 21.2 %copy-start.24 = (f32[128,512]{1,0:T(8,128)}, f32[128,512]{1,0:T(8,128)S(1)}, u32[]{:S(2)}) copy-start(f32[128,512]{1,0:T(8,128)S(1)} %get-tuple-element.43) | copy-start | bytes 786436
  25.7 21.2 %copy-start.25 = (f32[128,512]{1,0:T(8,128)}, f32[128,512]{1,0:T(8,128)S(1)}, u32[]{:S(2)}) copy-start(f32[128,512]{1,0:T(8,128)S(1)} %get-tuple-element.44) | copy-start | bytes 786436
  25.7 21.2 %copy-start.26 = (f32[128,512]{1,0:T(8,128)}, f32[128,512]{1,0:T(8,128)S(1)}, u32[]{:S(2)}) copy-start(f32[128,512]{1,0:T(8,128)S(1)} %get-tuple-element.45) | copy-start | bytes 786436
  25.7 14.6 %copy-start.11 = (s32[2,128,512]{2,1,0:T(8,128)S(1)}, s32[2,128,512]{2,1,0:T(8,128)}, u32[]{:S(2)}) copy-start(s32[2,128,512]{2,1,0:T(8,128)} %param.7) | copy-start | bytes 1572868
  27.0 7.7 %collective-permute-start.2 = (f32[2,134,3]{2,1,0:T(8,128)S(1)}, f32[2,134,3]{2,1,0:T(8,128)S(1)}, u32[]{:S(2)}, u32[]{:S(2)}) collective-permute-start(f32[2,134,3]{2,1,0:T(8,128)S(1)} %get-tuple-element.86), channel_id=1, source_target_pairs={{0,1},{1,2},{2,3},{3,4},{4,5},{5,6},{6,7},{8,9},{9,10},{10,11},{11... | collective-permute-start | bytes 9656 | tf_op jit(solution)/shard_map/ppermute | solution.py:76
  30.9 8.3 %collective-permute-start.3 = (f32[2,134,3]{2,1,0:T(8,128)S(1)}, f32[2,134,3]{2,1,0:T(8,128)S(1)}, u32[]{:S(2)}, u32[]{:S(2)}) collective-permute-start(f32[2,134,3]{2,1,0:T(8,128)S(1)} %get-tuple-element.85), channel_id=1, source_target_pairs={{1,0},{2,1},{3,2},{4,3},{5,4},{6,5},{7,6},{9,8},{10,9},{11,10},{12... | collective-permute-start | bytes 9656 | tf_op jit(solution)/shard_map/ppermute | solution.py:79
  52.8 20.1 %copy-start.2 = (f32[128,512]{1,0:T(8,128)S(1)}, f32[128,512]{1,0:T(8,128)}, u32[]{:S(2)}) copy-start(f32[128,512]{1,0:T(8,128)} %copy-done.1) | copy-start | bytes 786436
  52.8 20.1 %copy-start.4 = (f32[128,512]{1,0:T(8,128)S(1)}, f32[128,512]{1,0:T(8,128)}, u32[]{:S(2)}) copy-start(f32[128,512]{1,0:T(8,128)} %copy-done.3) | copy-start | bytes 786436
  52.8 2.7 %collective-permute-start.4 = (f32[2,3,512]{2,1,0:T(4,128)S(1)}, f32[2,3,512]{2,1,0:T(4,128)S(1)}, u32[]{:S(2)}, u32[]{:S(2)}) collective-permute-start(f32[2,3,512]{2,1,0:T(4,128)S(1)} %get-tuple-element.91), channel_id=1, source_target_pairs={{0,8},{8,16},{16,24},{24,32},{32,40},{40,48},{48,56},{56,64},{64,7... | collective-permute-start | bytes 36872 | tf_op jit(solution)/shard_map/ppermute | solution.py:76
  54.2 5.0 %collective-permute-start.5 = (f32[2,3,512]{2,1,0:T(4,128)S(1)}, f32[2,3,512]{2,1,0:T(4,128)S(1)}, u32[]{:S(2)}, u32[]{:S(2)}) collective-permute-start(f32[2,3,512]{2,1,0:T(4,128)S(1)} %get-tuple-element.92), channel_id=1, source_target_pairs={{8,0},{16,8},{24,16},{32,24},{40,32},{48,40},{56,48},{64,56},{72,6... | collective-permute-start | bytes 36872 | tf_op jit(solution)/shard_map/ppermute | solution.py:79
  60.0 7.3 %collective-permute-start.6 = (f32[2,134,3]{2,1,0:T(8,128)}, f32[2,134,3]{2,1,0:T(8,128)}, u32[]{:S(2)}, u32[]{:S(2)}) collective-permute-start(f32[2,134,3]{2,1,0:T(8,128)} %get-tuple-element.82), channel_id=1, source_target_pairs={{0,1},{1,2},{2,3},{3,4},{4,5},{5,6},{6,7},{8,9},{9,10},{10,11},{11... | collective-permute-start | bytes 9656 | tf_op jit(solution)/shard_map/ppermute | solution.py:76
  63.3 8.4 %collective-permute-start.7 = (f32[2,134,3]{2,1,0:T(8,128)}, f32[2,134,3]{2,1,0:T(8,128)}, u32[]{:S(2)}, u32[]{:S(2)}) collective-permute-start(f32[2,134,3]{2,1,0:T(8,128)} %get-tuple-element.81), channel_id=1, source_target_pairs={{1,0},{2,1},{3,2},{4,3},{5,4},{6,5},{7,6},{9,8},{10,9},{11,10},{12... | collective-permute-start | bytes 9656 | tf_op jit(solution)/shard_map/ppermute | solution.py:79
  86.7 24.9 %copy-start.31 = (f32[2,128,512]{2,1,0:T(8,128)}, f32[2,128,512]{2,1,0:T(8,128)S(1)}, u32[]{:S(2)}) copy-start(f32[2,128,512]{2,1,0:T(8,128)S(1)} %get-tuple-element.55) | copy-start | bytes 1572868
  127.0 3.6 %collective-permute-start.8 = (f32[1,128]{1,0:T(1,128)S(1)}, f32[1,128]{1,0:T(1,128)S(1)}, u32[]{:S(2)}, u32[]{:S(2)}) collective-permute-start(f32[1,128]{1,0:T(1,128)S(1)} %bitcast.955), channel_id=1, source_target_pairs={{0,1},{1,0},{2,3},{3,2},{4,5},{5,4},{6,7},{7,6},{8,9},{9,8},{10,11... | collective-permute-start | bytes 1544 | tf_op jit(solution)/shard_map/ppermute | solution.py:174
  130.6 3.5 %collective-permute-start.9 = (f32[1,128]{1,0:T(1,128)S(1)}, f32[1,128]{1,0:T(1,128)S(1)}, u32[]{:S(2)}, u32[]{:S(2)}) collective-permute-start(f32[1,128]{1,0:T(1,128)S(1)} %bitcast_add_fusion), channel_id=1, source_target_pairs={{0,2},{1,3},{2,0},{3,1},{4,6},{5,7},{6,4},{7,5},{8,10},{9,11},{10,... | collective-permute-start | bytes 1544 | tf_op jit(solution)/shard_map/ppermute | solution.py:174
  134.1 5.0 %collective-permute-start.10 = (f32[1,128]{1,0:T(1,128)S(1)}, f32[1,128]{1,0:T(1,128)S(1)}, u32[]{:S(2)}, u32[]{:S(2)}) collective-permute-start(f32[1,128]{1,0:T(1,128)S(1)} %add.1788), channel_id=1, source_target_pairs={{0,4},{1,5},{2,6},{3,7},{4,0},{5,1},{6,2},{7,3},{8,12},{9,13},{10,... | collective-permute-start | bytes 1544 | tf_op jit(solution)/shard_map/ppermute | solution.py:174
  (14 other events, 76.9 us)
where the time goes:
time: 140 us
  other arithmetic  40.8 us (29%)
  starting transfers between devices  32.1 us (23%)
  waiting for transfers between devices  26.9 us (19%)
  Pallas kernels  15 us (11%)
  blocking collectives  12.9 us (9%)
  local copies, waits for them, and re-layouts  9.6 us (7%)
  between operations  2.66 us (2%)
    another operation x4, other arithmetic, forces(): return (jnp.stack([total_row, total_col]), kept_sum, exist_sum)  24.2 us
    pallas_call x1, Pallas kernels, contact_sums(): pl.pallas_call(contact_kernel, out_shape=jax.ShapeDtypeStruct((blocks, 2,...  15 us
    all_to_all x1, starting transfers between devices, body(): lax.all_to_all(jnp.broadcast_to(packed[None], (block_count,) + packed.sha...  14.5 us
    all_to_all x1, blocking collectives, body(): lax.all_to_all(partials.reshape(block_count, 1, 2 * PAN_DEV), 'along', 0,...  12.9 us
    ppermute x4, waiting for transfers between devices, with_halo(): lax.ppermute(lax.slice_in_dim(block, 0, width, axis=dim), axis, backward)  12.6 us
    ppermute x3, waiting for transfers between devices, body(): share = share + lax.ppermute(share, 'across', xor_pairs(across_count, k))  12.1 us
    ppermute x4, starting transfers between devices, with_halo(): lax.ppermute(lax.slice_in_dim(block, block.shape[dim] - width, None, axis...  10.3 us
    ppermute x4, starting transfers between devices, with_halo(): lax.ppermute(lax.slice_in_dim(block, 0, width, axis=dim), axis, backward)  7.3 us
  transfers between devices with their start and end apart: 12, of which 8 were waited for; matrix products, arithmetic and copies ran while one was open for 27% of the time, Pallas kernels for 0%

commit v1 on v0

--- a/solution.py
+++ b/solution.py
@@ -9,10 +9,6 @@
 
 
 offsets = [(rr, cc) for rr in range(-3, 4) for cc in range(-3, 4) if 0 < rr * rr + cc * cc <= 9]
-
-
-def xor_pairs(count, bit):
-    return [(i, i ^ (1 << bit)) for i in range(count)]
 
 
 def contact_kernel(meta_ref, win_ref, pos_ref, xr_ref, xc_ref, out_ref):
@@ -114,25 +110,24 @@
     total_cols = cols * across_count
     row_base = lax.axis_index("along") * rows
     col_base = lax.axis_index("across") * cols
-    state_u, state_v = (disp, velocity)
-    damage = None
-    for step in range(2):
-        padded = with_halo(state_u, (("along", 1), ("across", 2)), 3)
-        grid_row = row_base - 3 + jnp.arange(rows + 2 * 3, dtype=jnp.int32)
-        grid_col = col_base - 3 + jnp.arange(cols + 2 * 3, dtype=jnp.int32)
-        inside_row = (grid_row >= 0) & (grid_row < total_rows)
-        inside_col = (grid_col >= 0) & (grid_col < total_cols)
-        force, kept_sum, exist_sum = forces(
-            padded,
-            bond_bits,
-            (inside_row[:, None] & inside_col[None, :]).astype(jnp.float32),
-            rows,
-            cols,
-        )
-        if step == 0:
-            damage = 1.0 - kept_sum / exist_sum
-        state_v = state_v + 10.0 * force
-        state_u = state_u + 0.05 * state_v
+    stacked = jnp.concatenate([disp, velocity, bond_bits.astype(jnp.float32)], axis=0)
+    ext = with_halo(stacked, (("along", 1), ("across", 2)), 6)
+    grid_row = row_base - 6 + jnp.arange(rows + 12, dtype=jnp.int32)
+    grid_col = col_base - 6 + jnp.arange(cols + 12, dtype=jnp.int32)
+    inside_row = (grid_row >= 0) & (grid_row < total_rows)
+    inside_col = (grid_col >= 0) & (grid_col < total_cols)
+    present_wide = (inside_row[:, None] & inside_col[None, :]).astype(jnp.float32)
+    present_ring = present_wide[3:-3, 3:-3]
+    force, kept_sum, exist_sum = forces(
+        ext[0:2], ext[4:6, 3:-3, 3:-3].astype(jnp.int32), present_wide, rows + 6, cols + 6
+    )
+    damage = 1.0 - kept_sum[3:-3, 3:-3] / exist_sum[3:-3, 3:-3]
+    ring_v = ext[2:4, 3:-3, 3:-3] + 10.0 * force
+    ring_u = ext[0:2, 3:-3, 3:-3] + 0.05 * ring_v
+    ring_u = jnp.where(present_ring[None] > 0.0, ring_u, 0.0)
+    force, _, _ = forces(ring_u, bond_bits, present_ring, rows, cols)
+    state_v = ring_v[:, 3:-3, 3:-3] + 10.0 * force
+    state_u = ring_u[:, 3:-3, 3:-3] + 0.05 * state_v
     block_count = lax.axis_size("along")
     packed = jnp.concatenate(
         [panel_pos.reshape(1, -1), contact_list.astype(jnp.float32).reshape(1, -1)], axis=1
@@ -166,13 +161,12 @@
     meta = jnp.concatenate([n_listed[None], listed_blocks])
     sums = contact_sums(meta, windows, all_pos.reshape(-1), rows_x, cols_x)
     partials = jnp.transpose(jnp.sum(sums, axis=-1), (0, 2, 1))
-    arrived = lax.all_to_all(
-        partials.reshape(block_count, 1, 2 * PAN_DEV), "along", 0, 0, tiled=True
-    )
-    share = jnp.sum(arrived, axis=0)
-    for k in range(across_count.bit_length() - 1):
-        share = share + lax.ppermute(share, "across", xor_pairs(across_count, k))
-    panel_force = share.reshape(PAN_DEV, 2)
+    spread = jnp.broadcast_to(
+        partials.reshape(block_count, 1, 1, 2 * PAN_DEV),
+        (block_count, across_count, 1, 2 * PAN_DEV),
+    ).reshape(block_count * across_count, 1, 2 * PAN_DEV)
+    arrived = lax.all_to_all(spread, ("along", "across"), 0, 0, tiled=True)
+    panel_force = jnp.sum(arrived, axis=0).reshape(PAN_DEV, 2)
     return (state_u, state_v, damage, panel_force)
 
 

time: 140 us -> 139 us (level)
  the two profiles are of different devices: /device:TPU:12 before, /device:TPU:1 now
where the time goes in v1:
time: 139 us
  other arithmetic  53.5 us (38%)
  starting transfers between devices  41.2 us (30%)
  waiting for transfers between devices  28 us (20%)
  local copies, waits for them, and re-layouts  9.19 us (7%)
  Pallas kernels  4.65 us (3%)
  between operations  2.39 us (2%)
    another operation x4, other arithmetic, forces(): return (jnp.stack([total_row, total_col]), kept_sum, exist_sum)  31.1 us
    all_to_all x1, starting transfers between devices, body(): arrived = lax.all_to_all(spread, ('along', 'across'), 0, 0, tiled=True)  18 us
    ppermute x2, waiting for transfers between devices, with_halo(): lax.ppermute(lax.slice_in_dim(block, block.shape[dim] - width, None, axis...  15 us
    all_to_all x1, starting transfers between devices, body(): lax.all_to_all(jnp.broadcast_to(packed[None], (block_count,) + packed.sha...  12.7 us
    all_to_all x1, waiting for transfers between devices, body(): arrived = lax.all_to_all(spread, ('along', 'across'), 0, 0, tiled=True)  9.11 us
    ppermute x2, starting transfers between devices, with_halo(): lax.ppermute(lax.slice_in_dim(block, block.shape[dim] - width, None, axis...  7.25 us
    pallas_call x1, Pallas kernels, contact_sums(): pl.pallas_call(contact_kernel, out_shape=jax.ShapeDtypeStruct((blocks, 2,...  4.65 us
    all_to_all x1, waiting for transfers between devices, body(): lax.all_to_all(jnp.broadcast_to(packed[None], (block_count,) + packed.sha...  3.81 us
  transfers between devices with their start and end apart: 6, of which 3 were waited for; matrix products, arithmetic and copies ran while one was open for 10% of the time, Pallas kernels for 0%

profile of v1, /device:TPU:1, one launch (start us, length us, event | category | flops | bytes accessed | tf_op | source)
XLA Modules:
  0.0 138.8 jit_solution(7508661068765818807)
XLA Ops:
  0.7 1.1 convert_element_type.416
  1.7 0.8 pad_maximum_fusion.18
  2.6 4.9 %collective-permute-start = (f32[6,6,512]{2,1,0:T(8,128)S(1)}, f32[6,6,512]{2,1,0:T(8,128)S(1)}, u32[]{:S(2)}, u32[]{:S(2)}) collective-permute-start(f32[6,6,512]{2,1,0:T(8,128)S(1)} %get-tuple-element.84), channel_id=1, source_target_pairs={{0,8},{8,16},{16,24},{24,32},{32,40},{40,48},{48,56},{56,64},{64,7... | collective-permute-start | bytes 221192 | tf_op jit(solution)/shard_map/ppermute | solution.py:72
  7.5 1.9 %collective-permute-start.1 = (f32[6,6,512]{2,1,0:T(8,128)S(1)}, f32[6,6,512]{2,1,0:T(8,128)S(1)}, u32[]{:S(2)}, u32[]{:S(2)}) collective-permute-start(f32[6,6,512]{2,1,0:T(8,128)S(1)} %get-tuple-element.85), channel_id=1, source_target_pairs={{8,0},{16,8},{24,16},{32,24},{40,32},{48,40},{56,48},{64,56},{72,6... | collective-permute-start | bytes 221192 | tf_op jit(solution)/shard_map/ppermute | solution.py:75
  10.4 12.7 %all-to-all-start = ((f32[32,1,132]{2,1,0:T(1,128)}), f32[32,1,132]{2,1,0:T(1,128)S(1)}, u32[]{:S(2)}, u32[]{:S(2)}) async-start(f32[32,1,132]{2,1,0:T(1,128)} %broadcast_in_dim.39), calls=%async_computation | async-start | bytes 65536 | tf_op jit(solution)/shard_map/all_to_all | solution.py:135
  23.2 0.8 slice_compare_fusion
  24.0 1.9 %fusion.300 = (f32[134,518]{1,0:T(8,128)}, f32[134,518]{1,0:T(8,128)}, f32[134,518]{1,0:T(8,128)}, f32[134,518]{1,0:T(8,128)}, f32[134,518]{1,0:T(8,128)}, /*index=5*/f32[134,518]{1,0:T(8,128)}) fusion(f32[140,524]{1,0:T(8,128)S(1)} %and_convert_fusion), kind=kLoop, calls=%fused_computation.545 | loop fusion | bytes 3331776 | tf_op jit(solution)/shard_map/slice | solution.py:88
  26.0 2.7 %add_add_fusion = f32[134,518]{1,0:T(8,128)} fusion(f32[140,524]{1,0:T(8,128)S(1)} %and_convert_fusion), kind=kLoop, calls=%fused_computation.210 | loop fusion | flops 1457652 | bytes 6385904 | tf_op jit(solution)/shard_map/add | solution.py:101
  28.7 3.8 %all-to-all-done = f32[32,1,132]{2,1,0:T(1,128)S(1)} async-done(((f32[32,1,132]{2,1,0:T(1,128)}), f32[32,1,132]{2,1,0:T(1,128)S(1)}, u32[]{:S(2)}, u32[]{:S(2)}) %all-to-all-start) | async-done | bytes 16928 | tf_op jit(solution)/shard_map/all_to_all | solution.py:135
  34.2 1.0 pad_maximum_fusion.5
  35.1 2.3 %collective-permute-start.2 = (f32[6,140,6]{2,1,0:T(8,128)}, f32[6,140,6]{2,1,0:T(8,128)S(1)}, u32[]{:S(2)}, u32[]{:S(2)}) collective-permute-start(f32[6,140,6]{2,1,0:T(8,128)} %get-tuple-element.82), channel_id=1, source_target_pairs={{0,1},{1,2},{2,3},{3,4},{4,5},{5,6},{6,7},{8,9},{9,10},{10,11},{11... | collective-permute-start | bytes 60488 | tf_op jit(solution)/shard_map/ppermute | solution.py:72
  37.5 1.3 collective-permute-start.3
  38.8 1.3 pad_add_fusion.1.meta_ref
  40.0 0.7 copy.32
  40.8 15.0 %collective-permute-done.2 = f32[6,140,6]{2,1,0:T(8,128)S(1)} collective-permute-done((f32[6,140,6]{2,1,0:T(8,128)}, f32[6,140,6]{2,1,0:T(8,128)S(1)}, u32[]{:S(2)}, u32[]{:S(2)}) %collective-permute-start.2) | collective-permute-done | bytes 20192 | tf_op jit(solution)/shard_map/ppermute | solution.py:72
  55.8 0.9 pad_maximum_fusion
  57.0 2.7 %add_add_fusion.1 = f32[134,518]{1,0:T(8,128)} fusion(f32[140,524]{1,0:T(8,128)S(1)} %and_convert_fusion, s32[2,134,518]{2,1,0:T(8,128)S(1)} %slice_convert_fusion), kind=kLoop, calls=%fused_computation.211 | loop fusion | flops 7565908 | bytes 6941200 | tf_op jit(solution)/shard_map/add | solution.py:100
  59.7 12.8 %add_bitcast_fusion.1 = (f32[1,134,518]{2,1,0:T(8,128)}, f32[134,518]{1,0:T(8,128)S(1)}, f32[134,518]{1,0:T(8,128)S(1)}, f32[134,518]{1,0:T(8,128)S(1)}, f32[134...) fusion(f32[6,140,524]{2,1,0:T(8,128)S(1)} %pad_maximum_fusion, ...), kind=kLoop, calls=%fused_computation.213 | loop fusion | flops 33248348 | bytes 30358384 | tf_op jit(solution)/shard_map/stack | solution.py:102
  72.5 8.6 %add_bitcast_fusion = f32[1,134,518]{2,1,0:T(8,128)S(1)} fusion(f32[134,518]{1,0:T(8,128)} %get-tuple-element.80, f32[134,518]{1,0:T(8,128)} %get-tuple-element.78, f32[134,518]{1,0:T(8,128)} %get-tuple-element.76, f32[134,518]{1,0:T(8,128)S(1)} %get-tuple-element.74, f32[134,518]{1,0:T(8,128)S(1)} %get-tuple-element.73, ...), kind=kLoop, calls=%fused_computation.212 | loop fusion | flops 23738904 | bytes 22489488 | tf_op jit(solution)/shard_map/stack | solution.py:102
  82.1 7.7 %add_bitcast_fusion.3 = (f32[1,128,512]{2,1,0:T(8,128)S(1)}, f32[128,512]{1,0:T(8,128)S(1)}, f32[128,512]{1,0:T(8,128)S(1)}, f32[128,512]{1,0:T(8,128)S(1)}, f32...) fusion(f32[2,134,518]{2,1,0:T(8,128)S(1)} %get-tuple-element.61, ...), kind=kLoop, calls=%fused_computation.501 | loop fusion | flops 30081024 | bytes 30670848 | tf_op jit(solution)/shard_map/stack | solution.py:102
  89.8 2.0 %add_bitcast_fusion.2 = f32[1,128,512]{2,1,0:T(8,128)S(1)} fusion(f32[128,512]{1,0:T(8,128)S(1)} %get-tuple-element.60, f32[128,512]{1,0:T(8,128)S(1)} %get-tuple-element.59, f32[128,512]{1,0:T(8,128)S(1)} %get-tuple-element.58, f32[128,512]{1,0:T(8,128)S(1)} %get-tuple-element.57, f32[128,512]{1,0:T(8,128)S(1)} %get-tuple-element.56, ...), kind=kLoop, calls=%fused_computation.500 | loop fusion | flops 6881280 | bytes 15204352 | tf_op jit(solution)/shard_map/stack | solution.py:102
  91.9 1.2 slice_add_fusion.3
  93.0 1.6 %fusion.262 = (f32[128,512]{1,0:T(8,128)}, f32[128,512]{1,0:T(8,128)}, f32[]{:T(128)}, f32[]{:T(128)}) fusion(f32[2,128,512]{2,1,0:T(8,128)S(1)} %get-tuple-element.30, f32[512]{0:T(512)S(1)} %add_convert_fusion, f32[128]{0:T(128)S(1)} %add_convert_fusion.1), kind=kLoop, calls=%fused_computation.503 | loop fusion | flops 393214 | bytes 1051144 | tf_op jit(solution)/shard_map/add | solution.py:147
  96.0 0.9 subtract_maximum_fusion.1
  97.0 1.0 copy.33
  98.0 1.3 reshape.647.win_ref
  99.3 4.6 %shard_map.84 = f32[32,2,64,128]{3,2,1,0:T(8,128)} custom-call(s32[33]{0:T(128)} %pad_add_fusion.1.meta_ref, s32[8192]{0:T(1024)} %reshape.647.win_ref, f32[4096]{0:T(1024)} %get-tuple-element.98.pos_ref, f32[128,512]{1,0:T(8,128)} %get-tuple-element.87.xr_ref, f32[128,512]{1,0:T(8,128)} %get-tuple-element.86.xc_ref), custom_call_target="tpu_custom_call" | custom-call | tf_op jit(solution)/shard_map/pallas_call | solution.py:59
  103.9 2.2 %reduce_sum.28 = f32[32,2,64]{2,1,0:T(2,128)S(1)} reduce(f32[32,2,64,128]{3,2,1,0:T(8,128)} %shard_map.84, f32[]{:T(128)} %constant.178.clone.1), dimensions={3}, to_apply=%region_5.6 | reduce | flops 520192 | bytes 2113540 | tf_op jit(solution)/shard_map/reduce_sum | solution.py:163
  106.3 0.7 broadcast_in_dim.41
  107.0 18.0 %all-to-all-start.1 = ((f32[256,1,128]{2,1,0:T(1,128)}), f32[256,1,128]{2,1,0:T(1,128)S(1)}, u32[]{:S(2)}, u32[]{:S(2)}) async-start(f32[256,1,128]{2,1,0:T(1,128)} %bitcast.181), calls=%async_computation.1 | async-start | bytes 262144 | tf_op jit(solution)/shard_map/all_to_all | solution.py:168
  125.1 3.6 %fusion.104 = f32[128,512]{1,0:T(8,128)} fusion(f32[134,518]{1,0:T(8,128)} %get-tuple-element.92, f32[134,518]{1,0:T(8,128)S(1)} %copy-done.10, f32[134,518]{1,0:T(8,128)} %get-tuple-element.93, f32[134,518]{1,0:T(8,128)} %get-tuple-element.95, f32[134,518]{1,0:T(8,128)} %get-tuple-element.94, f32[134,518]{1,0:T(8,128)S(1)} %copy-done.9, ...), kind=kLoop, calls=%fused_computation.246 | loop fusion | flops 917504 | bytes 3932160 | tf_op jit(solution)/shard_map/sub | solution.py:124
  128.6 9.1 %all-to-all-done.1 = f32[256,1,128]{2,1,0:T(1,128)S(1)} async-done(((f32[256,1,128]{2,1,0:T(1,128)}), f32[256,1,128]{2,1,0:T(1,128)S(1)}, u32[]{:S(2)}, u32[]{:S(2)}) %all-to-all-start.1) | async-done | bytes 131104 | tf_op jit(solution)/shard_map/all_to_all | solution.py:168
  (68 shorter events, 5.3 us)
Async XLA Ops:
  0.6 8.8 %copy-start.17 = (f32[64,2]{0,1:T(2,128)S(1)}, f32[64,2]{0,1:T(2,128)}, u32[]{:S(2)}) copy-start(f32[64,2]{0,1:T(2,128)} %param.8) | copy-start | bytes 1540
  0.6 9.1 %copy-start.18 = (s32[1,4]{1,0:T(1,128)S(1)}, s32[1,4]{1,0:T(1,128)}, u32[]{:S(2)}) copy-start(s32[1,4]{1,0:T(1,128)} %param.9) | copy-start | bytes 52
  2.6 31.5 %collective-permute-start = (f32[6,6,512]{2,1,0:T(8,128)S(1)}, f32[6,6,512]{2,1,0:T(8,128)S(1)}, u32[]{:S(2)}, u32[]{:S(2)}) collective-permute-start(f32[6,6,512]{2,1,0:T(8,128)S(1)} %get-tuple-element.84), channel_id=1, source_target_pairs={{0,8},{8,16},{16,24},{24,32},{32,40},{40,48},{48,56},{56,64},{64,7... | collective-permute-start | bytes 221192 | tf_op jit(solution)/shard_map/ppermute | solution.py:72
  7.5 26.6 %collective-permute-start.1 = (f32[6,6,512]{2,1,0:T(8,128)S(1)}, f32[6,6,512]{2,1,0:T(8,128)S(1)}, u32[]{:S(2)}, u32[]{:S(2)}) collective-permute-start(f32[6,6,512]{2,1,0:T(8,128)S(1)} %get-tuple-element.85), channel_id=1, source_target_pairs={{8,0},{16,8},{24,16},{32,24},{40,32},{48,40},{56,48},{64,56},{72,6... | collective-permute-start | bytes 221192 | tf_op jit(solution)/shard_map/ppermute | solution.py:75
  10.4 22.1 %all-to-all-start = ((f32[32,1,132]{2,1,0:T(1,128)}), f32[32,1,132]{2,1,0:T(1,128)S(1)}, u32[]{:S(2)}, u32[]{:S(2)}) async-start(f32[32,1,132]{2,1,0:T(1,128)} %broadcast_in_dim.39), calls=%async_computation | async-start | bytes 65536 | tf_op jit(solution)/shard_map/all_to_all | solution.py:135
  26.0 8.2 %copy-start = (f32[2,128,512]{2,1,0:T(8,128)S(1)}, f32[2,128,512]{2,1,0:T(8,128)}, u32[]{:S(2)}) copy-start(f32[2,128,512]{2,1,0:T(8,128)} %param.6) | copy-start | bytes 1572868
  26.0 8.2 %copy-start.1 = (f32[2,128,512]{2,1,0:T(8,128)S(1)}, f32[2,128,512]{2,1,0:T(8,128)}, u32[]{:S(2)}) copy-start(f32[2,128,512]{2,1,0:T(8,128)} %param.5) | copy-start | bytes 1572868
  34.1 22.6 %copy-start.11 = (f32[6,6,512]{2,1,0:T(8,128)}, f32[6,6,512]{2,1,0:T(8,128)S(1)}, u32[]{:S(2)}) copy-start(f32[6,6,512]{2,1,0:T(8,128)S(1)} %collective-permute-done) | copy-start | bytes 221188
  34.2 22.6 %copy-start.13 = (f32[6,6,512]{2,1,0:T(8,128)}, f32[6,6,512]{2,1,0:T(8,128)S(1)}, u32[]{:S(2)}) copy-start(f32[6,6,512]{2,1,0:T(8,128)S(1)} %collective-permute-done.1) | copy-start | bytes 221188
  35.1 20.6 %collective-permute-start.2 = (f32[6,140,6]{2,1,0:T(8,128)}, f32[6,140,6]{2,1,0:T(8,128)S(1)}, u32[]{:S(2)}, u32[]{:S(2)}) collective-permute-start(f32[6,140,6]{2,1,0:T(8,128)} %get-tuple-element.82), channel_id=1, source_target_pairs={{0,1},{1,2},{2,3},{3,4},{4,5},{5,6},{6,7},{8,9},{9,10},{10,11},{11... | collective-permute-start | bytes 60488 | tf_op jit(solution)/shard_map/ppermute | solution.py:72
  37.5 18.3 %collective-permute-start.3 = (f32[6,140,6]{2,1,0:T(8,128)S(1)}, f32[6,140,6]{2,1,0:T(8,128)S(1)}, u32[]{:S(2)}, u32[]{:S(2)}) collective-permute-start(f32[6,140,6]{2,1,0:T(8,128)S(1)} %get-tuple-element.83), channel_id=1, source_target_pairs={{1,0},{2,1},{3,2},{4,3},{5,4},{6,5},{7,6},{9,8},{10,9},{11,10},{12... | collective-permute-start | bytes 60488 | tf_op jit(solution)/shard_map/ppermute | solution.py:75
  57.0 2.7 %copy-start.12 = (f32[6,6,512]{2,1,0:T(8,128)S(1)}, f32[6,6,512]{2,1,0:T(8,128)}, u32[]{:S(2)}) copy-start(f32[6,6,512]{2,1,0:T(8,128)} %copy-done.11) | copy-start | bytes 221188
  57.0 2.7 %copy-start.14 = (f32[6,6,512]{2,1,0:T(8,128)S(1)}, f32[6,6,512]{2,1,0:T(8,128)}, u32[]{:S(2)}) copy-start(f32[6,6,512]{2,1,0:T(8,128)} %copy-done.13) | copy-start | bytes 221188
  72.5 8.6 %copy-start.4 = (f32[1,134,518]{2,1,0:T(8,128)S(1)}, f32[1,134,518]{2,1,0:T(8,128)}, u32[]{:S(2)}) copy-start(f32[1,134,518]{2,1,0:T(8,128)} %get-tuple-element.63) | copy-start | bytes 832948
  72.5 8.6 %copy-start.15 = (pred[134,518]{1,0:T(8,128)(4,1)S(1)}, pred[134,518]{1,0:T(8,128)(4,1)}, u32[]{:S(2)}) copy-start(pred[134,518]{1,0:T(8,128)(4,1)} %slice_compare_fusion) | copy-start | bytes 208240
  81.1 1.0 copy-start.3
  91.8 4.1 %copy-start.16 = (f32[32,128]{0,1:T(8,128)S(1)}, f32[32,128]{0,1:T(8,128)}, u32[]{:S(2)}) copy-start(f32[32,128]{0,1:T(8,128)} %copy.32) | copy-start | bytes 49156
  93.0 10.9 %copy-start.2 = (f32[2,128,512]{2,1,0:T(8,128)}, f32[2,128,512]{2,1,0:T(8,128)S(1)}, u32[]{:S(2)}) copy-start(f32[2,128,512]{2,1,0:T(8,128)S(1)} %get-tuple-element.30) | copy-start | bytes 1572868
  99.2 25.8 %copy-start.5 = (f32[134,518]{1,0:T(8,128)S(1)}, f32[134,518]{1,0:T(8,128)}, u32[]{:S(2)}) copy-start(f32[134,518]{1,0:T(8,128)} %get-tuple-element.75) | copy-start | bytes 832948
  99.2 25.8 %copy-start.6 = (f32[134,518]{1,0:T(8,128)S(1)}, f32[134,518]{1,0:T(8,128)}, u32[]{:S(2)}) copy-start(f32[134,518]{1,0:T(8,128)} %get-tuple-element.77) | copy-start | bytes 832948
  99.2 25.8 %copy-start.7 = (f32[134,518]{1,0:T(8,128)S(1)}, f32[134,518]{1,0:T(8,128)}, u32[]{:S(2)}) copy-start(f32[134,518]{1,0:T(8,128)} %get-tuple-element.79) | copy-start | bytes 832948
  99.2 25.8 %copy-start.8 = (f32[134,518]{1,0:T(8,128)S(1)}, f32[134,518]{1,0:T(8,128)}, u32[]{:S(2)}) copy-start(f32[134,518]{1,0:T(8,128)} %get-tuple-element.81) | copy-start | bytes 832948
  99.3 25.8 %copy-start.9 = (f32[134,518]{1,0:T(8,128)S(1)}, f32[134,518]{1,0:T(8,128)}, u32[]{:S(2)}) copy-start(f32[134,518]{1,0:T(8,128)} %get-tuple-element.90) | copy-start | bytes 832948
  99.3 25.8 %copy-start.10 = (f32[134,518]{1,0:T(8,128)S(1)}, f32[134,518]{1,0:T(8,128)}, u32[]{:S(2)}) copy-start(f32[134,518]{1,0:T(8,128)} %get-tuple-element.91) | copy-start | bytes 832948
  107.0 30.8 %all-to-all-start.1 = ((f32[256,1,128]{2,1,0:T(1,128)}), f32[256,1,128]{2,1,0:T(1,128)S(1)}, u32[]{:S(2)}, u32[]{:S(2)}) async-start(f32[256,1,128]{2,1,0:T(1,128)} %bitcast.181), calls=%async_computation.1 | async-start | bytes 262144 | tf_op jit(solution)/shard_map/all_to_all | solution.py:168

commit v2 on v1

--- a/solution.py
+++ b/solution.py
@@ -69,10 +69,14 @@
         count = lax.axis_size(axis)
         forward = [(i, i + 1) for i in range(count - 1)]
         backward = [(target, source) for source, target in forward]
-        low = lax.ppermute(
-            lax.slice_in_dim(block, block.shape[dim] - width, None, axis=dim), axis, forward
-        )
-        high = lax.ppermute(lax.slice_in_dim(block, 0, width, axis=dim), axis, backward)
+        narrow = dim == block.ndim - 1
+        low = lax.slice_in_dim(block, block.shape[dim] - width, None, axis=dim)
+        high = lax.slice_in_dim(block, 0, width, axis=dim)
+        strip = low.shape
+        if narrow:
+            low, high = low.reshape(-1), high.reshape(-1)
+        low = lax.ppermute(low, axis, forward).reshape(strip)
+        high = lax.ppermute(high, axis, backward).reshape(strip)
         block = jnp.concatenate([low, block, high], axis=dim)
     return block
 

time: 139 us -> 122 us (0.88)
  waiting for transfers between devices: 28 us -> 14.5 us
  starting transfers between devices: 41.2 us -> 31 us
  Pallas kernels: 4.65 us -> 10.7 us
    ppermute x4, waiting for transfers between devices: 15 us -> 1.59 us  [the longest x2 1.58 us: with_halo(): high = lax.ppermute(high, axis, backward).reshape(strip)]
    all_to_all x1, starting transfers between devices: 18 us -> 7.9 us  [body(): arrived = lax.all_to_all(spread, ('along', 'across'), 0, 0, tiled=True)]
    pallas_call x1, Pallas kernels: 4.65 us -> 10.7 us  [contact_sums(): pl.pallas_call(contact_kernel, out_shape=jax.ShapeDtypeStruct((blocks, 2,...]
  transfers between devices with their start and end apart: 6 -> 6, of which waited for: 3 -> 3; matrix products, arithmetic and copies ran while one was open for 10% -> 12% of each run, Pallas kernels for 0% -> 0%
where the time goes in v2:
time: 122 us; the launch traced here: 121 us
  other arithmetic  52.7 us (43%)
  starting transfers between devices  31 us (25%)
  waiting for transfers between devices  14.5 us (12%)
  Pallas kernels  10.7 us (9%)
  local copies, waits for them, and re-layouts  10.1 us (8%)
  between operations  2.41 us (2%)
    another operation x4, other arithmetic, forces(): return (jnp.stack([total_row, total_col]), kept_sum, exist_sum)  31 us
    all_to_all x1, starting transfers between devices, body(): lax.all_to_all(jnp.broadcast_to(packed[None], (block_count,) + packed.sha...  12.7 us
    pallas_call x1, Pallas kernels, contact_sums(): pl.pallas_call(contact_kernel, out_shape=jax.ShapeDtypeStruct((blocks, 2,...  10.7 us
    all_to_all x1, waiting for transfers between devices, body(): arrived = lax.all_to_all(spread, ('along', 'across'), 0, 0, tiled=True)  9.11 us
    all_to_all x1, starting transfers between devices, body(): arrived = lax.all_to_all(spread, ('along', 'across'), 0, 0, tiled=True)  7.9 us
    ppermute x2, starting transfers between devices, with_halo(): low = lax.ppermute(low, axis, forward).reshape(strip)  7.24 us
    all_to_all x1, waiting for transfers between devices, body(): lax.all_to_all(jnp.broadcast_to(packed[None], (block_count,) + packed.sha...  3.81 us
    sub x1, other arithmetic, body(): damage = 1.0 - kept_sum[3:-3, 3:-3] / exist_sum[3:-3, 3:-3]  3.56 us
  transfers between devices with their start and end apart: 6, of which 3 were waited for; matrix products, arithmetic and copies ran while one was open for 12% of the time, Pallas kernels for 0%

profile of v2, /device:TPU:1, one launch (start us, length us, event | category | flops | bytes accessed | tf_op | source)
XLA Modules:
  0.0 121.4 jit_solution(6383419383652378319)
XLA Ops:
  0.7 1.1 convert_element_type.416
  1.7 0.8 pad_maximum_fusion.18
  2.6 4.9 %collective-permute-start = (f32[6,6,512]{2,1,0:T(8,128)S(1)}, f32[6,6,512]{2,1,0:T(8,128)S(1)}, u32[]{:S(2)}, u32[]{:S(2)}) collective-permute-start(f32[6,6,512]{2,1,0:T(8,128)S(1)} %get-tuple-element.84), channel_id=1, source_target_pairs={{0,8},{8,16},{16,24},{24,32},{32,40},{40,48},{48,56},{56,64},{64,7... | collective-permute-start | bytes 221192 | tf_op jit(solution)/shard_map/ppermute | solution.py:78
  7.5 1.9 %collective-permute-start.1 = (f32[6,6,512]{2,1,0:T(8,128)S(1)}, f32[6,6,512]{2,1,0:T(8,128)S(1)}, u32[]{:S(2)}, u32[]{:S(2)}) collective-permute-start(f32[6,6,512]{2,1,0:T(8,128)S(1)} %get-tuple-element.85), channel_id=1, source_target_pairs={{8,0},{16,8},{24,16},{32,24},{40,32},{48,40},{56,48},{64,56},{72,6... | collective-permute-start | bytes 221192 | tf_op jit(solution)/shard_map/ppermute | solution.py:79
  10.4 12.7 %all-to-all-start = ((f32[32,1,132]{2,1,0:T(1,128)}), f32[32,1,132]{2,1,0:T(1,128)S(1)}, u32[]{:S(2)}, u32[]{:S(2)}) async-start(f32[32,1,132]{2,1,0:T(1,128)} %broadcast_in_dim.39), calls=%async_computation | async-start | bytes 65536 | tf_op jit(solution)/shard_map/all_to_all | solution.py:139
  23.2 0.8 slice_compare_fusion
  24.0 1.9 %fusion.300 = (f32[134,518]{1,0:T(8,128)}, f32[134,518]{1,0:T(8,128)}, f32[134,518]{1,0:T(8,128)}, f32[134,518]{1,0:T(8,128)}, f32[134,518]{1,0:T(8,128)}, /*index=5*/f32[134,518]{1,0:T(8,128)}) fusion(f32[140,524]{1,0:T(8,128)S(1)} %and_convert_fusion), kind=kLoop, calls=%fused_computation.545 | loop fusion | bytes 3331776 | tf_op jit(solution)/shard_map/slice | solution.py:92
  26.0 2.7 %add_add_fusion = f32[134,518]{1,0:T(8,128)} fusion(f32[140,524]{1,0:T(8,128)S(1)} %and_convert_fusion), kind=kLoop, calls=%fused_computation.210 | loop fusion | flops 1457652 | bytes 6385904 | tf_op jit(solution)/shard_map/add | solution.py:105
  28.7 3.8 %all-to-all-done = f32[32,1,132]{2,1,0:T(1,128)S(1)} async-done(((f32[32,1,132]{2,1,0:T(1,128)}), f32[32,1,132]{2,1,0:T(1,128)S(1)}, u32[]{:S(2)}, u32[]{:S(2)}) %all-to-all-start) | async-done | bytes 16928 | tf_op jit(solution)/shard_map/all_to_all | solution.py:139
  34.6 2.3 %collective-permute-start.2 = (f32[5040]{0:T(1024)S(1)}, f32[5040]{0:T(1024)S(1)}, u32[]{:S(2)}, u32[]{:S(2)}) collective-permute-start(f32[5040]{0:T(1024)S(1)} %reshape.656), channel_id=1, source_target_pairs={{0,1},{1,2},{2,3},{3,4},{4,5},{5,6},{6,7},{8,9},{9,10},{10,11},{11... | collective-permute-start | bytes 60488 | tf_op jit(solution)/shard_map/ppermute | solution.py:78
  37.2 1.3 %collective-permute-start.3 = (f32[5040]{0:T(1024)S(1)}, f32[5040]{0:T(1024)S(1)}, u32[]{:S(2)}, u32[]{:S(2)}) collective-permute-start(f32[5040]{0:T(1024)S(1)} %reshape.658), channel_id=1, source_target_pairs={{1,0},{2,1},{3,2},{4,3},{5,4},{6,5},{7,6},{9,8},{10,9},{11,10},{12... | collective-permute-start | bytes 60488 | tf_op jit(solution)/shard_map/ppermute | solution.py:79
  38.5 1.3 %pad_add_fusion.1.meta_ref = s32[33]{0:T(128)} fusion(s32[32]{0:T(128)S(1)} %convert_reduce_fusion, s32[1]{0:T(128)} %bitcast.174), kind=kLoop, calls=%fused_computation.541 | loop fusion | flops 33 | bytes 264 | tf_op jit(solution)/shard_map/concatenate | solution.py:165
  39.7 0.7 copy.32
  40.7 1.6 %collective-permute-done.3 = f32[5040]{0:T(1024)S(1)} collective-permute-done((f32[5040]{0:T(1024)S(1)}, f32[5040]{0:T(1024)S(1)}, u32[]{:S(2)}, u32[]{:S(2)}) %collective-permute-start.3) | collective-permute-done | bytes 20192 | tf_op jit(solution)/shard_map/ppermute | solution.py:79
  42.5 0.9 pad_maximum_fusion
  43.7 2.7 %add_add_fusion.1 = f32[134,518]{1,0:T(8,128)} fusion(f32[140,524]{1,0:T(8,128)S(1)} %and_convert_fusion, s32[2,134,518]{2,1,0:T(8,128)S(1)} %slice_convert_fusion), kind=kLoop, calls=%fused_computation.211 | loop fusion | flops 7565908 | bytes 6941200 | tf_op jit(solution)/shard_map/add | solution.py:104
  46.4 12.8 %add_bitcast_fusion.1 = (f32[1,134,518]{2,1,0:T(8,128)}, f32[134,518]{1,0:T(8,128)S(1)}, f32[134,518]{1,0:T(8,128)S(1)}, f32[134,518]{1,0:T(8,128)S(1)}, f32[134...) fusion(f32[6,140,524]{2,1,0:T(8,128)S(1)} %pad_maximum_fusion, ...), kind=kLoop, calls=%fused_computation.213 | loop fusion | flops 33248348 | bytes 30358384 | tf_op jit(solution)/shard_map/stack | solution.py:106
  59.2 8.6 %add_bitcast_fusion = f32[1,134,518]{2,1,0:T(8,128)S(1)} fusion(f32[134,518]{1,0:T(8,128)} %get-tuple-element.80, f32[134,518]{1,0:T(8,128)} %get-tuple-element.78, f32[134,518]{1,0:T(8,128)} %get-tuple-element.76, f32[134,518]{1,0:T(8,128)S(1)} %get-tuple-element.74, f32[134,518]{1,0:T(8,128)S(1)} %get-tuple-element.73, ...), kind=kLoop, calls=%fused_computation.212 | loop fusion | flops 23738904 | bytes 22489488 | tf_op jit(solution)/shard_map/stack | solution.py:106
  68.8 7.7 %add_bitcast_fusion.3 = (f32[1,128,512]{2,1,0:T(8,128)S(1)}, f32[128,512]{1,0:T(8,128)S(1)}, f32[128,512]{1,0:T(8,128)S(1)}, f32[128,512]{1,0:T(8,128)S(1)}, f32...) fusion(f32[2,134,518]{2,1,0:T(8,128)S(1)} %get-tuple-element.61, ...), kind=kLoop, calls=%fused_computation.501 | loop fusion | flops 30081024 | bytes 30670848 | tf_op jit(solution)/shard_map/stack | solution.py:106
  76.5 2.0 %add_bitcast_fusion.2 = f32[1,128,512]{2,1,0:T(8,128)S(1)} fusion(f32[128,512]{1,0:T(8,128)S(1)} %get-tuple-element.60, f32[128,512]{1,0:T(8,128)S(1)} %get-tuple-element.59, f32[128,512]{1,0:T(8,128)S(1)} %get-tuple-element.58, f32[128,512]{1,0:T(8,128)S(1)} %get-tuple-element.57, f32[128,512]{1,0:T(8,128)S(1)} %get-tuple-element.56, ...), kind=kLoop, calls=%fused_computation.500 | loop fusion | flops 6881280 | bytes 15204352 | tf_op jit(solution)/shard_map/stack | solution.py:106
  78.5 1.2 slice_add_fusion.3
  79.7 1.6 %fusion.262 = (f32[128,512]{1,0:T(8,128)}, f32[128,512]{1,0:T(8,128)}, f32[]{:T(128)}, f32[]{:T(128)}) fusion(f32[2,128,512]{2,1,0:T(8,128)S(1)} %get-tuple-element.30, f32[512]{0:T(512)S(1)} %add_convert_fusion, f32[128]{0:T(128)S(1)} %add_convert_fusion.1), kind=kLoop, calls=%fused_computation.503 | loop fusion | flops 393214 | bytes 1051144 | tf_op jit(solution)/shard_map/add | solution.py:151
  82.6 0.9 subtract_maximum_fusion.1
  83.6 1.0 copy.33
  84.6 1.3 %reshape.663.win_ref = s32[8192]{0:T(1024)} reshape(s32[32,64,4]{2,1,0:T(8,128)S(1)} %copy.33) | data formatting | bytes 65536 | tf_op jit(solution)/shard_map/reshape | solution.py:164
  85.9 10.7 %shard_map.84 = f32[32,2,64,128]{3,2,1,0:T(8,128)} custom-call(s32[33]{0:T(128)} %pad_add_fusion.1.meta_ref, s32[8192]{0:T(1024)} %reshape.663.win_ref, f32[4096]{0:T(1024)} %get-tuple-element.98.pos_ref, f32[128,512]{1,0:T(8,128)} %get-tuple-element.87.xr_ref, f32[128,512]{1,0:T(8,128)} %get-tuple-element.86.xc_ref), custom_call_target="tpu_custom_call" | custom-call | tf_op jit(solution)/shard_map/pallas_call | solution.py:59
  96.6 2.2 %reduce_sum.28 = f32[32,2,64]{2,1,0:T(2,128)S(1)} reduce(f32[32,2,64,128]{3,2,1,0:T(8,128)} %shard_map.84, f32[]{:T(128)} %constant.178.clone.1), dimensions={3}, to_apply=%region_5.6 | reduce | flops 520192 | bytes 2113540 | tf_op jit(solution)/shard_map/reduce_sum | solution.py:167
  99.0 0.7 broadcast_in_dim.41
  99.7 7.9 %all-to-all-start.1 = ((f32[256,1,128]{2,1,0:T(1,128)}), f32[256,1,128]{2,1,0:T(1,128)S(1)}, u32[]{:S(2)}, u32[]{:S(2)}) async-start(f32[256,1,128]{2,1,0:T(1,128)} %bitcast.181), calls=%async_computation.1 | async-start | bytes 262144 | tf_op jit(solution)/shard_map/all_to_all | solution.py:172
  107.7 3.6 %fusion.104 = f32[128,512]{1,0:T(8,128)} fusion(f32[134,518]{1,0:T(8,128)} %get-tuple-element.92, f32[134,518]{1,0:T(8,128)S(1)} %copy-done.10, f32[134,518]{1,0:T(8,128)} %get-tuple-element.93, f32[134,518]{1,0:T(8,128)} %get-tuple-element.95, f32[134,518]{1,0:T(8,128)} %get-tuple-element.94, f32[134,518]{1,0:T(8,128)S(1)} %copy-done.9, ...), kind=kLoop, calls=%fused_computation.246 | loop fusion | flops 917504 | bytes 3932160 | tf_op jit(solution)/shard_map/sub | solution.py:128
  111.2 9.1 %all-to-all-done.1 = f32[256,1,128]{2,1,0:T(1,128)S(1)} async-done(((f32[256,1,128]{2,1,0:T(1,128)}), f32[256,1,128]{2,1,0:T(1,128)S(1)}, u32[]{:S(2)}, u32[]{:S(2)}) %all-to-all-start.1) | async-done | bytes 131104 | tf_op jit(solution)/shard_map/all_to_all | solution.py:172
  120.7 0.6 copy.36
  (72 shorter events, 5.8 us)
Async XLA Ops:
  0.6 8.8 %copy-start.17 = (f32[64,2]{0,1:T(2,128)S(1)}, f32[64,2]{0,1:T(2,128)}, u32[]{:S(2)}) copy-start(f32[64,2]{0,1:T(2,128)} %param.8) | copy-start | bytes 1540
  0.6 9.1 %copy-start.18 = (s32[1,4]{1,0:T(1,128)S(1)}, s32[1,4]{1,0:T(1,128)}, u32[]{:S(2)}) copy-start(s32[1,4]{1,0:T(1,128)} %param.9) | copy-start | bytes 52
  2.6 31.5 %collective-permute-start = (f32[6,6,512]{2,1,0:T(8,128)S(1)}, f32[6,6,512]{2,1,0:T(8,128)S(1)}, u32[]{:S(2)}, u32[]{:S(2)}) collective-permute-start(f32[6,6,512]{2,1,0:T(8,128)S(1)} %get-tuple-element.84), channel_id=1, source_target_pairs={{0,8},{8,16},{16,24},{24,32},{32,40},{40,48},{48,56},{56,64},{64,7... | collective-permute-start | bytes 221192 | tf_op jit(solution)/shard_map/ppermute | solution.py:78
  7.5 26.6 %collective-permute-start.1 = (f32[6,6,512]{2,1,0:T(8,128)S(1)}, f32[6,6,512]{2,1,0:T(8,128)S(1)}, u32[]{:S(2)}, u32[]{:S(2)}) collective-permute-start(f32[6,6,512]{2,1,0:T(8,128)S(1)} %get-tuple-element.85), channel_id=1, source_target_pairs={{8,0},{16,8},{24,16},{32,24},{40,32},{48,40},{56,48},{64,56},{72,6... | collective-permute-start | bytes 221192 | tf_op jit(solution)/shard_map/ppermute | solution.py:79
  10.4 22.1 %all-to-all-start = ((f32[32,1,132]{2,1,0:T(1,128)}), f32[32,1,132]{2,1,0:T(1,128)S(1)}, u32[]{:S(2)}, u32[]{:S(2)}) async-start(f32[32,1,132]{2,1,0:T(1,128)} %broadcast_in_dim.39), calls=%async_computation | async-start | bytes 65536 | tf_op jit(solution)/shard_map/all_to_all | solution.py:139
  26.0 8.2 %copy-start = (f32[2,128,512]{2,1,0:T(8,128)S(1)}, f32[2,128,512]{2,1,0:T(8,128)}, u32[]{:S(2)}) copy-start(f32[2,128,512]{2,1,0:T(8,128)} %param.6) | copy-start | bytes 1572868
  26.0 8.2 %copy-start.1 = (f32[2,128,512]{2,1,0:T(8,128)S(1)}, f32[2,128,512]{2,1,0:T(8,128)}, u32[]{:S(2)}) copy-start(f32[2,128,512]{2,1,0:T(8,128)} %param.5) | copy-start | bytes 1572868
  34.1 8.3 %copy-start.11 = (f32[6,6,512]{2,1,0:T(8,128)}, f32[6,6,512]{2,1,0:T(8,128)S(1)}, u32[]{:S(2)}) copy-start(f32[6,6,512]{2,1,0:T(8,128)S(1)} %collective-permute-done) | copy-start | bytes 221188
  34.2 8.3 %copy-start.13 = (f32[6,6,512]{2,1,0:T(8,128)}, f32[6,6,512]{2,1,0:T(8,128)S(1)}, u32[]{:S(2)}) copy-start(f32[6,6,512]{2,1,0:T(8,128)S(1)} %collective-permute-done.1) | copy-start | bytes 221188
  34.6 5.8 %collective-permute-start.2 = (f32[5040]{0:T(1024)S(1)}, f32[5040]{0:T(1024)S(1)}, u32[]{:S(2)}, u32[]{:S(2)}) collective-permute-start(f32[5040]{0:T(1024)S(1)} %reshape.656), channel_id=1, source_target_pairs={{0,1},{1,2},{2,3},{3,4},{4,5},{5,6},{6,7},{8,9},{9,10},{10,11},{11... | collective-permute-start | bytes 60488 | tf_op jit(solution)/shard_map/ppermute | solution.py:78
  37.2 5.1 %collective-permute-start.3 = (f32[5040]{0:T(1024)S(1)}, f32[5040]{0:T(1024)S(1)}, u32[]{:S(2)}, u32[]{:S(2)}) collective-permute-start(f32[5040]{0:T(1024)S(1)} %reshape.658), channel_id=1, source_target_pairs={{1,0},{2,1},{3,2},{4,3},{5,4},{6,5},{7,6},{9,8},{10,9},{11,10},{12... | collective-permute-start | bytes 60488 | tf_op jit(solution)/shard_map/ppermute | solution.py:79
  43.6 2.7 %copy-start.12 = (f32[6,6,512]{2,1,0:T(8,128)S(1)}, f32[6,6,512]{2,1,0:T(8,128)}, u32[]{:S(2)}) copy-start(f32[6,6,512]{2,1,0:T(8,128)} %copy-done.11) | copy-start | bytes 221188
  43.7 2.7 %copy-start.14 = (f32[6,6,512]{2,1,0:T(8,128)S(1)}, f32[6,6,512]{2,1,0:T(8,128)}, u32[]{:S(2)}) copy-start(f32[6,6,512]{2,1,0:T(8,128)} %copy-done.13) | copy-start | bytes 221188
  59.2 8.6 %copy-start.4 = (f32[1,134,518]{2,1,0:T(8,128)S(1)}, f32[1,134,518]{2,1,0:T(8,128)}, u32[]{:S(2)}) copy-start(f32[1,134,518]{2,1,0:T(8,128)} %get-tuple-element.63) | copy-start | bytes 832948
  59.2 8.6 %copy-start.15 = (pred[134,518]{1,0:T(8,128)(4,1)S(1)}, pred[134,518]{1,0:T(8,128)(4,1)}, u32[]{:S(2)}) copy-start(pred[134,518]{1,0:T(8,128)(4,1)} %slice_compare_fusion) | copy-start | bytes 208240
  67.8 1.0 copy-start.3
  78.5 4.1 %copy-start.16 = (f32[32,128]{0,1:T(8,128)S(1)}, f32[32,128]{0,1:T(8,128)}, u32[]{:S(2)}) copy-start(f32[32,128]{0,1:T(8,128)} %copy.32) | copy-start | bytes 49156
  79.7 16.9 %copy-start.2 = (f32[2,128,512]{2,1,0:T(8,128)}, f32[2,128,512]{2,1,0:T(8,128)S(1)}, u32[]{:S(2)}) copy-start(f32[2,128,512]{2,1,0:T(8,128)S(1)} %get-tuple-element.30) | copy-start | bytes 1572868
  85.9 21.7 %copy-start.5 = (f32[134,518]{1,0:T(8,128)S(1)}, f32[134,518]{1,0:T(8,128)}, u32[]{:S(2)}) copy-start(f32[134,518]{1,0:T(8,128)} %get-tuple-element.75) | copy-start | bytes 832948
  85.9 21.7 %copy-start.6 = (f32[134,518]{1,0:T(8,128)S(1)}, f32[134,518]{1,0:T(8,128)}, u32[]{:S(2)}) copy-start(f32[134,518]{1,0:T(8,128)} %get-tuple-element.77) | copy-start | bytes 832948
  85.9 21.7 %copy-start.7 = (f32[134,518]{1,0:T(8,128)S(1)}, f32[134,518]{1,0:T(8,128)}, u32[]{:S(2)}) copy-start(f32[134,518]{1,0:T(8,128)} %get-tuple-element.79) | copy-start | bytes 832948
  85.9 21.7 %copy-start.8 = (f32[134,518]{1,0:T(8,128)S(1)}, f32[134,518]{1,0:T(8,128)}, u32[]{:S(2)}) copy-start(f32[134,518]{1,0:T(8,128)} %get-tuple-element.81) | copy-start | bytes 832948
  85.9 21.7 %copy-start.9 = (f32[134,518]{1,0:T(8,128)S(1)}, f32[134,518]{1,0:T(8,128)}, u32[]{:S(2)}) copy-start(f32[134,518]{1,0:T(8,128)} %get-tuple-element.90) | copy-start | bytes 832948
  85.9 21.7 %copy-start.10 = (f32[134,518]{1,0:T(8,128)S(1)}, f32[134,518]{1,0:T(8,128)}, u32[]{:S(2)}) copy-start(f32[134,518]{1,0:T(8,128)} %get-tuple-element.91) | copy-start | bytes 832948
  99.7 20.6 %all-to-all-start.1 = ((f32[256,1,128]{2,1,0:T(1,128)}), f32[256,1,128]{2,1,0:T(1,128)S(1)}, u32[]{:S(2)}, u32[]{:S(2)}) async-start(f32[256,1,128]{2,1,0:T(1,128)} %bitcast.181), calls=%async_computation.1 | async-start | bytes 262144 | tf_op jit(solution)/shard_map/all_to_all | solution.py:172

commit v3 on v2

--- a/solution.py
+++ b/solution.py
@@ -13,9 +13,43 @@
 
 def contact_kernel(meta_ref, win_ref, pos_ref, xr_ref, xc_ref, out_ref):
     out_ref[...] = jnp.zeros_like(out_ref)
-    panels = out_ref.shape[2]
-
-    def per_block(k, carry):
+    blocks, _, panels, _ = out_ref.shape
+    row_tiles = xr_ref.shape[0] // 8
+    col_tiles = xr_ref.shape[1] // 128
+
+    def tile_sums(centre_row, centre_col, row_group, col_group, accs):
+        row = pl.multiple_of(row_group * 8, 8)
+        col = pl.multiple_of(col_group * 128, 128)
+        delta_row = centre_row - xr_ref[pl.ds(row, 8), pl.ds(col, 128)]
+        delta_col = centre_col - xc_ref[pl.ds(row, 8), pl.ds(col, 128)]
+        push = 0.5 * jnp.maximum(4.0 - delta_row * delta_row - delta_col * delta_col, 0.0)
+        return (accs[0] + push * delta_row, accs[1] + push * delta_col)
+
+    def store(block, j, accs):
+        out_ref[block, 0, pl.ds(j, 1), :] = jnp.sum(accs[0], axis=0, keepdims=True)
+        out_ref[block, 1, pl.ds(j, 1), :] = jnp.sum(accs[1], axis=0, keepdims=True)
+
+    zero = jnp.zeros((8, 128), jnp.float32)
+
+    def per_block_narrow(k, carry):
+        block = meta_ref[1 + k]
+
+        def per_panel(j, carry):
+            slot = block * panels + j
+            centre_row = pos_ref[2 * slot]
+            centre_col = pos_ref[2 * slot + 1]
+            first_row = jnp.minimum(win_ref[4 * slot], row_tiles - 2)
+            first_col = jnp.minimum(win_ref[4 * slot + 2], col_tiles - 2)
+            accs = (zero, zero)
+            for r in range(2):
+                for c in range(2):
+                    accs = tile_sums(centre_row, centre_col, first_row + r, first_col + c, accs)
+            store(block, j, accs)
+            return carry
+
+        return lax.fori_loop(0, panels, per_panel, carry, unroll=4)
+
+    def per_block_wide(k, carry):
         block = meta_ref[1 + k]
 
         def per_panel(j, carry):
@@ -28,32 +62,29 @@
             col_groups = win_ref[4 * slot + 3]
 
             def per_row(r, accs):
-                row = pl.multiple_of((first_row + r) * 8, 8)
-
                 def per_col(c, accs):
-                    col = pl.multiple_of((first_col + c) * 128, 128)
-                    delta_row = centre_row - xr_ref[pl.ds(row, 8), pl.ds(col, 128)]
-                    delta_col = centre_col - xc_ref[pl.ds(row, 8), pl.ds(col, 128)]
-                    push = 0.5 * jnp.maximum(
-                        4.0 - delta_row * delta_row - delta_col * delta_col, 0.0
-                    )
-                    return (accs[0] + push * delta_row, accs[1] + push * delta_col)
+                    return tile_sums(centre_row, centre_col, first_row + r, first_col + c, accs)
 
                 return lax.fori_loop(0, col_groups, per_col, accs)
 
-            zero = jnp.zeros((8, 128), jnp.float32)
-            acc_row, acc_col = lax.fori_loop(0, row_groups, per_row, (zero, zero))
-            out_ref[block, 0, pl.ds(j, 1), :] = jnp.sum(acc_row, axis=0, keepdims=True)
-            out_ref[block, 1, pl.ds(j, 1), :] = jnp.sum(acc_col, axis=0, keepdims=True)
+            store(block, j, lax.fori_loop(0, row_groups, per_row, (zero, zero)))
             return carry
 
         return lax.fori_loop(0, panels, per_panel, carry)
 
-    lax.fori_loop(0, meta_ref[0], per_block, 0)
+    narrow = meta_ref[1 + blocks]
+
+    @pl.when(narrow == 1)
+    def _():
+        lax.fori_loop(0, meta_ref[0], per_block_narrow, 0)
+
+    @pl.when(narrow == 0)
+    def _():
+        lax.fori_loop(0, meta_ref[0], per_block_wide, 0)
 
 
 def contact_sums(meta, windows, positions, rows_x, cols_x):
-    blocks = meta.shape[0] - 1
+    blocks = meta.shape[0] - 2
     smem = pl.BlockSpec(memory_space=pltpu.SMEM)
     vmem = pl.BlockSpec(memory_space=pltpu.VMEM)
     return pl.pallas_call(
@@ -149,8 +180,8 @@
     listed_blocks = jnp.sum((prefix[None, :] <= slots[:, None]).astype(jnp.int32), axis=1)
     rows_x = (row_base + jnp.arange(rows, dtype=jnp.int32)).astype(jnp.float32)[:, None] + state_u[0]
     cols_x = (col_base + jnp.arange(cols, dtype=jnp.int32)).astype(jnp.float32)[None, :] + state_u[1]
-    reach_row = 3.0 + jnp.max(jnp.abs(state_u[0]))
-    reach_col = 3.0 + jnp.max(jnp.abs(state_u[1]))
+    reach_row = 2.5 + jnp.max(jnp.abs(state_u[0]))
+    reach_col = 2.5 + jnp.max(jnp.abs(state_u[1]))
     local_row = all_pos[:, :, 0] - row_base.astype(jnp.float32)
     local_col = all_pos[:, :, 1] - col_base.astype(jnp.float32)
     row_lo = jnp.clip(jnp.floor(local_row - reach_row), 0, rows).astype(jnp.int32)
@@ -162,7 +193,8 @@
     first_col = col_lo // 128
     col_groups = jnp.maximum((col_hi + 127) // 128 - first_col, 0)
     windows = jnp.stack([first_row, row_groups, first_col, col_groups], axis=-1).reshape(-1)
-    meta = jnp.concatenate([n_listed[None], listed_blocks])
+    narrow = (jnp.max(row_groups) <= 2) & (jnp.max(col_groups) <= 2)
+    meta = jnp.concatenate([n_listed[None], listed_blocks, narrow.astype(jnp.int32)[None]])
     sums = contact_sums(meta, windows, all_pos.reshape(-1), rows_x, cols_x)
     partials = jnp.transpose(jnp.sum(sums, axis=-1), (0, 2, 1))
     spread = jnp.broadcast_to(

time: 122 us -> 122 us (level)
  Pallas kernels: 10.7 us -> 5.92 us
  starting transfers between devices: 31 us -> 33.1 us
  between operations: 2.41 us -> 3.74 us
    pallas_call x1, Pallas kernels: 10.7 us -> 5.92 us  [contact_sums(): pl.pallas_call(contact_kernel, out_shape=jax.ShapeDtypeStruct((blocks, 2,...]
    all_to_all x1, starting transfers between devices: 7.9 us -> 9.95 us  [body(): arrived = lax.all_to_all(spread, ('along', 'across'), 0, 0, tiled=True)]
    reduce_max x0 -> x2, other arithmetic: none -> 1.36 us  [body(): narrow = (jnp.max(row_groups) <= 2) & (jnp.max(col_groups) <= 2)]
  transfers between devices with their start and end apart: 6 -> 6, of which waited for: 3 -> 3; matrix products, arithmetic and copies ran while one was open for 12% -> 10% of each run, Pallas kernels for 0% -> 0%
where the time goes in v3:
time: 122 us
  other arithmetic  53.9 us (44%)
  starting transfers between devices  33.1 us (27%)
  waiting for transfers between devices  15.2 us (12%)
  local copies, waits for them, and re-layouts  10 us (8%)
  Pallas kernels  5.92 us (5%)
  between operations  3.74 us (3%)
    another operation x4, other arithmetic, forces(): return (jnp.stack([total_row, total_col]), kept_sum, exist_sum)  31 us
    all_to_all x1, starting transfers between devices, body(): lax.all_to_all(jnp.broadcast_to(packed[None], (block_count,) + packed.sha...  12.7 us
    all_to_all x1, starting transfers between devices, body(): arrived = lax.all_to_all(spread, ('along', 'across'), 0, 0, tiled=True)  9.95 us
    all_to_all x1, waiting for transfers between devices, body(): arrived = lax.all_to_all(spread, ('along', 'across'), 0, 0, tiled=True)  9.11 us
    ppermute x2, starting transfers between devices, with_halo(): low = lax.ppermute(low, axis, forward).reshape(strip)  7.24 us
    pallas_call x1, Pallas kernels, contact_sums(): pl.pallas_call(contact_kernel, out_shape=jax.ShapeDtypeStruct((blocks, 2,...  5.92 us
    all_to_all x1, waiting for transfers between devices, body(): lax.all_to_all(jnp.broadcast_to(packed[None], (block_count,) + packed.sha...  3.88 us
    sub x1, other arithmetic, body(): damage = 1.0 - kept_sum[3:-3, 3:-3] / exist_sum[3:-3, 3:-3]  3.56 us
  transfers between devices with their start and end apart: 6, of which 3 were waited for; matrix products, arithmetic and copies ran while one was open for 10% of the time, Pallas kernels for 0%

profile of v3, /device:TPU:1, one launch (start us, length us, event | category | flops | bytes accessed | tf_op | source)
XLA Modules:
  0.0 121.9 jit_solution(5322106204028451628)
XLA Ops:
  0.7 1.1 convert_element_type.425
  1.7 0.8 pad_maximum_fusion.18
  2.6 4.9 %collective-permute-start = (f32[6,6,512]{2,1,0:T(8,128)S(1)}, f32[6,6,512]{2,1,0:T(8,128)S(1)}, u32[]{:S(2)}, u32[]{:S(2)}) collective-permute-start(f32[6,6,512]{2,1,0:T(8,128)S(1)} %get-tuple-element.88), channel_id=1, source_target_pairs={{0,8},{8,16},{16,24},{24,32},{32,40},{40,48},{48,56},{56,64},{64,7... | collective-permute-start | bytes 221192 | tf_op jit(solution)/shard_map/ppermute | solution.py:109
  7.5 1.9 %collective-permute-start.1 = (f32[6,6,512]{2,1,0:T(8,128)S(1)}, f32[6,6,512]{2,1,0:T(8,128)S(1)}, u32[]{:S(2)}, u32[]{:S(2)}) collective-permute-start(f32[6,6,512]{2,1,0:T(8,128)S(1)} %get-tuple-element.89), channel_id=1, source_target_pairs={{8,0},{16,8},{24,16},{32,24},{40,32},{48,40},{56,48},{64,56},{72,6... | collective-permute-start | bytes 221192 | tf_op jit(solution)/shard_map/ppermute | solution.py:110
  10.4 12.7 %all-to-all-start = ((f32[32,1,132]{2,1,0:T(1,128)}), f32[32,1,132]{2,1,0:T(1,128)S(1)}, u32[]{:S(2)}, u32[]{:S(2)}) async-start(f32[32,1,132]{2,1,0:T(1,128)} %broadcast_in_dim.45), calls=%async_computation | async-start | bytes 65536 | tf_op jit(solution)/shard_map/all_to_all | solution.py:170
  23.2 0.8 slice_compare_fusion
  24.0 1.9 %fusion.314 = (f32[134,518]{1,0:T(8,128)}, f32[134,518]{1,0:T(8,128)}, f32[134,518]{1,0:T(8,128)}, f32[134,518]{1,0:T(8,128)}, f32[134,518]{1,0:T(8,128)}, /*index=5*/f32[134,518]{1,0:T(8,128)}) fusion(f32[140,524]{1,0:T(8,128)S(1)} %and_convert_fusion), kind=kLoop, calls=%fused_computation.583 | loop fusion | bytes 3331776 | tf_op jit(solution)/shard_map/slice | solution.py:123
  25.9 2.7 %add_add_fusion = f32[134,518]{1,0:T(8,128)} fusion(f32[140,524]{1,0:T(8,128)S(1)} %and_convert_fusion), kind=kLoop, calls=%fused_computation.210 | loop fusion | flops 1457652 | bytes 6385904 | tf_op jit(solution)/shard_map/add | solution.py:136
  28.6 3.9 %all-to-all-done = f32[32,1,132]{2,1,0:T(1,128)S(1)} async-done(((f32[32,1,132]{2,1,0:T(1,128)}), f32[32,1,132]{2,1,0:T(1,128)S(1)}, u32[]{:S(2)}, u32[]{:S(2)}) %all-to-all-start) | async-done | bytes 16928 | tf_op jit(solution)/shard_map/all_to_all | solution.py:170
  34.0 2.3 %collective-permute-start.2 = (f32[5040]{0:T(1024)S(1)}, f32[5040]{0:T(1024)S(1)}, u32[]{:S(2)}, u32[]{:S(2)}) collective-permute-start(f32[5040]{0:T(1024)S(1)} %reshape.682), channel_id=1, source_target_pairs={{0,1},{1,2},{2,3},{3,4},{4,5},{5,6},{6,7},{8,9},{9,10},{10,11},{11... | collective-permute-start | bytes 60488 | tf_op jit(solution)/shard_map/ppermute | solution.py:109
  36.5 1.3 %collective-permute-start.3 = (f32[5040]{0:T(1024)S(1)}, f32[5040]{0:T(1024)S(1)}, u32[]{:S(2)}, u32[]{:S(2)}) collective-permute-start(f32[5040]{0:T(1024)S(1)} %reshape.684), channel_id=1, source_target_pairs={{1,0},{2,1},{3,2},{4,3},{5,4},{6,5},{7,6},{9,8},{10,9},{11,10},{12... | collective-permute-start | bytes 60488 | tf_op jit(solution)/shard_map/ppermute | solution.py:110
  38.5 0.7 copy.91
  39.4 2.2 %collective-permute-done.3 = f32[5040]{0:T(1024)S(1)} collective-permute-done((f32[5040]{0:T(1024)S(1)}, f32[5040]{0:T(1024)S(1)}, u32[]{:S(2)}, u32[]{:S(2)}) %collective-permute-start.3) | collective-permute-done | bytes 20192 | tf_op jit(solution)/shard_map/ppermute | solution.py:110
  41.8 0.9 pad_maximum_fusion
  43.0 2.7 %add_add_fusion.1 = f32[134,518]{1,0:T(8,128)} fusion(f32[140,524]{1,0:T(8,128)S(1)} %and_convert_fusion, s32[2,134,518]{2,1,0:T(8,128)S(1)} %slice_convert_fusion), kind=kLoop, calls=%fused_computation.211 | loop fusion | flops 7565908 | bytes 6941200 | tf_op jit(solution)/shard_map/add | solution.py:135
  45.7 12.8 %add_bitcast_fusion.1 = (f32[1,134,518]{2,1,0:T(8,128)}, f32[134,518]{1,0:T(8,128)S(1)}, f32[134,518]{1,0:T(8,128)S(1)}, f32[134,518]{1,0:T(8,128)S(1)}, f32[134...) fusion(f32[6,140,524]{2,1,0:T(8,128)S(1)} %pad_maximum_fusion, ...), kind=kLoop, calls=%fused_computation.213 | loop fusion | flops 33248348 | bytes 30358384 | tf_op jit(solution)/shard_map/stack | solution.py:137
  58.5 8.6 %add_bitcast_fusion = f32[1,134,518]{2,1,0:T(8,128)S(1)} fusion(f32[134,518]{1,0:T(8,128)} %get-tuple-element.84, f32[134,518]{1,0:T(8,128)} %get-tuple-element.82, f32[134,518]{1,0:T(8,128)} %get-tuple-element.80, f32[134,518]{1,0:T(8,128)S(1)} %get-tuple-element.78, f32[134,518]{1,0:T(8,128)S(1)} %get-tuple-element.77, ...), kind=kLoop, calls=%fused_computation.212 | loop fusion | flops 23738904 | bytes 22489488 | tf_op jit(solution)/shard_map/stack | solution.py:137
  68.2 7.7 %add_bitcast_fusion.3 = (f32[1,128,512]{2,1,0:T(8,128)S(1)}, f32[128,512]{1,0:T(8,128)S(1)}, f32[128,512]{1,0:T(8,128)S(1)}, f32[128,512]{1,0:T(8,128)S(1)}, f32...) fusion(f32[2,134,518]{2,1,0:T(8,128)S(1)} %get-tuple-element.65, ...), kind=kLoop, calls=%fused_computation.501 | loop fusion | flops 30081024 | bytes 30670848 | tf_op jit(solution)/shard_map/stack | solution.py:137
  75.8 2.0 %add_bitcast_fusion.2 = f32[1,128,512]{2,1,0:T(8,128)S(1)} fusion(f32[128,512]{1,0:T(8,128)S(1)} %get-tuple-element.64, f32[128,512]{1,0:T(8,128)S(1)} %get-tuple-element.63, f32[128,512]{1,0:T(8,128)S(1)} %get-tuple-element.62, f32[128,512]{1,0:T(8,128)S(1)} %get-tuple-element.61, f32[128,512]{1,0:T(8,128)S(1)} %get-tuple-element.60, ...), kind=kLoop, calls=%fused_computation.500 | loop fusion | flops 6881280 | bytes 15204352 | tf_op jit(solution)/shard_map/stack | solution.py:137
  77.9 1.2 slice_add_fusion.3
  79.0 1.6 %fusion.262 = (f32[128,512]{1,0:T(8,128)}, f32[128,512]{1,0:T(8,128)}, f32[]{:T(128)}, f32[]{:T(128)}) fusion(f32[2,128,512]{2,1,0:T(8,128)S(1)} %get-tuple-element.34, f32[512]{0:T(512)S(1)} %add_convert_fusion, f32[128]{0:T(128)S(1)} %add_convert_fusion.1), kind=kLoop, calls=%fused_computation.503 | loop fusion | flops 393214 | bytes 1051144 | tf_op jit(solution)/shard_map/add | solution.py:182
  82.0 0.9 subtract_maximum_fusion
  83.0 1.0 copy.107
  84.0 1.2 %reshape.689.win_ref = s32[8192]{0:T(1024)} reshape(s32[32,64,4]{2,1,0:T(8,128)S(1)} %copy.107) | data formatting | bytes 65536 | tf_op jit(solution)/shard_map/reshape | solution.py:195
  86.6 0.7 fusion.266
  87.9 1.2 pad_add_fusion.1.meta_ref
  89.1 5.9 %shard_map.84 = f32[32,2,64,128]{3,2,1,0:T(8,128)} custom-call(s32[34]{0:T(128)} %pad_add_fusion.1.meta_ref, s32[8192]{0:T(1024)} %reshape.689.win_ref, f32[4096]{0:T(1024)} %get-tuple-element.104.pos_ref, f32[128,512]{1,0:T(8,128)} %get-tuple-element.91.xr_ref, f32[128,512]{1,0:T(8,128)} %get-tuple-element.90.xc_ref), custom_call_target="tpu_custom_call" | custom-call | tf_op jit(solution)/shard_map/pallas_call | solution.py:90
  95.0 2.2 %reduce_sum.28 = f32[32,2,64]{2,1,0:T(2,128)S(1)} reduce(f32[32,2,64,128]{3,2,1,0:T(8,128)} %shard_map.84, f32[]{:T(128)} %constant.180.clone.1), dimensions={3}, to_apply=%region_7.8 | reduce | flops 520192 | bytes 2113540 | tf_op jit(solution)/shard_map/reduce_sum | solution.py:199
  97.4 0.7 broadcast_in_dim.49
  98.1 10.0 %all-to-all-start.1 = ((f32[256,1,128]{2,1,0:T(1,128)}), f32[256,1,128]{2,1,0:T(1,128)S(1)}, u32[]{:S(2)}, u32[]{:S(2)}) async-start(f32[256,1,128]{2,1,0:T(1,128)} %bitcast.186), calls=%async_computation.1 | async-start | bytes 262144 | tf_op jit(solution)/shard_map/all_to_all | solution.py:204
  108.1 3.6 %fusion.104 = f32[128,512]{1,0:T(8,128)} fusion(f32[134,518]{1,0:T(8,128)} %get-tuple-element.96, f32[134,518]{1,0:T(8,128)S(1)} %copy-done.10, f32[134,518]{1,0:T(8,128)} %get-tuple-element.97, f32[134,518]{1,0:T(8,128)} %get-tuple-element.99, f32[134,518]{1,0:T(8,128)} %get-tuple-element.98, f32[134,518]{1,0:T(8,128)S(1)} %copy-done.9, ...), kind=kLoop, calls=%fused_computation.246 | loop fusion | flops 917504 | bytes 3932160 | tf_op jit(solution)/shard_map/sub | solution.py:159
  111.7 9.1 %all-to-all-done.1 = f32[256,1,128]{2,1,0:T(1,128)S(1)} async-done(((f32[256,1,128]{2,1,0:T(1,128)}), f32[256,1,128]{2,1,0:T(1,128)S(1)}, u32[]{:S(2)}, u32[]{:S(2)}) %all-to-all-start.1) | async-done | bytes 131104 | tf_op jit(solution)/shard_map/all_to_all | solution.py:204
  (74 shorter events, 7.1 us)
Async XLA Ops:
  0.6 8.8 %copy-start.17 = (f32[64,2]{0,1:T(2,128)S(1)}, f32[64,2]{0,1:T(2,128)}, u32[]{:S(2)}) copy-start(f32[64,2]{0,1:T(2,128)} %param.8) | copy-start | bytes 1540
  0.6 9.1 %copy-start.18 = (s32[1,4]{1,0:T(1,128)S(1)}, s32[1,4]{1,0:T(1,128)}, u32[]{:S(2)}) copy-start(s32[1,4]{1,0:T(1,128)} %param.9) | copy-start | bytes 52
  2.6 30.9 %collective-permute-start = (f32[6,6,512]{2,1,0:T(8,128)S(1)}, f32[6,6,512]{2,1,0:T(8,128)S(1)}, u32[]{:S(2)}, u32[]{:S(2)}) collective-permute-start(f32[6,6,512]{2,1,0:T(8,128)S(1)} %get-tuple-element.88), channel_id=1, source_target_pairs={{0,8},{8,16},{16,24},{24,32},{32,40},{40,48},{48,56},{56,64},{64,7... | collective-permute-start | bytes 221192 | tf_op jit(solution)/shard_map/ppermute | solution.py:109
  7.5 26.0 %collective-permute-start.1 = (f32[6,6,512]{2,1,0:T(8,128)S(1)}, f32[6,6,512]{2,1,0:T(8,128)S(1)}, u32[]{:S(2)}, u32[]{:S(2)}) collective-permute-start(f32[6,6,512]{2,1,0:T(8,128)S(1)} %get-tuple-element.89), channel_id=1, source_target_pairs={{8,0},{16,8},{24,16},{32,24},{40,32},{48,40},{56,48},{64,56},{72,6... | collective-permute-start | bytes 221192 | tf_op jit(solution)/shard_map/ppermute | solution.py:110
  10.4 22.1 %all-to-all-start = ((f32[32,1,132]{2,1,0:T(1,128)}), f32[32,1,132]{2,1,0:T(1,128)S(1)}, u32[]{:S(2)}, u32[]{:S(2)}) async-start(f32[32,1,132]{2,1,0:T(1,128)} %broadcast_in_dim.45), calls=%async_computation | async-start | bytes 65536 | tf_op jit(solution)/shard_map/all_to_all | solution.py:170
  25.9 7.6 %copy-start = (f32[2,128,512]{2,1,0:T(8,128)S(1)}, f32[2,128,512]{2,1,0:T(8,128)}, u32[]{:S(2)}) copy-start(f32[2,128,512]{2,1,0:T(8,128)} %param.6) | copy-start | bytes 1572868
  25.9 7.6 %copy-start.1 = (f32[2,128,512]{2,1,0:T(8,128)S(1)}, f32[2,128,512]{2,1,0:T(8,128)}, u32[]{:S(2)}) copy-start(f32[2,128,512]{2,1,0:T(8,128)} %param.5) | copy-start | bytes 1572868
  33.5 8.3 %copy-start.11 = (f32[6,6,512]{2,1,0:T(8,128)}, f32[6,6,512]{2,1,0:T(8,128)S(1)}, u32[]{:S(2)}) copy-start(f32[6,6,512]{2,1,0:T(8,128)S(1)} %collective-permute-done) | copy-start | bytes 221188
  33.5 8.3 %copy-start.13 = (f32[6,6,512]{2,1,0:T(8,128)}, f32[6,6,512]{2,1,0:T(8,128)S(1)}, u32[]{:S(2)}) copy-start(f32[6,6,512]{2,1,0:T(8,128)S(1)} %collective-permute-done.1) | copy-start | bytes 221188
  34.0 5.2 %collective-permute-start.2 = (f32[5040]{0:T(1024)S(1)}, f32[5040]{0:T(1024)S(1)}, u32[]{:S(2)}, u32[]{:S(2)}) collective-permute-start(f32[5040]{0:T(1024)S(1)} %reshape.682), channel_id=1, source_target_pairs={{0,1},{1,2},{2,3},{3,4},{4,5},{5,6},{6,7},{8,9},{9,10},{10,11},{11... | collective-permute-start | bytes 60488 | tf_op jit(solution)/shard_map/ppermute | solution.py:109
  36.5 5.1 %collective-permute-start.3 = (f32[5040]{0:T(1024)S(1)}, f32[5040]{0:T(1024)S(1)}, u32[]{:S(2)}, u32[]{:S(2)}) collective-permute-start(f32[5040]{0:T(1024)S(1)} %reshape.684), channel_id=1, source_target_pairs={{1,0},{2,1},{3,2},{4,3},{5,4},{6,5},{7,6},{9,8},{10,9},{11,10},{12... | collective-permute-start | bytes 60488 | tf_op jit(solution)/shard_map/ppermute | solution.py:110
  43.0 2.7 %copy-start.12 = (f32[6,6,512]{2,1,0:T(8,128)S(1)}, f32[6,6,512]{2,1,0:T(8,128)}, u32[]{:S(2)}) copy-start(f32[6,6,512]{2,1,0:T(8,128)} %copy-done.11) | copy-start | bytes 221188
  43.0 2.7 %copy-start.14 = (f32[6,6,512]{2,1,0:T(8,128)S(1)}, f32[6,6,512]{2,1,0:T(8,128)}, u32[]{:S(2)}) copy-start(f32[6,6,512]{2,1,0:T(8,128)} %copy-done.13) | copy-start | bytes 221188
  58.5 8.6 %copy-start.4 = (f32[1,134,518]{2,1,0:T(8,128)S(1)}, f32[1,134,518]{2,1,0:T(8,128)}, u32[]{:S(2)}) copy-start(f32[1,134,518]{2,1,0:T(8,128)} %get-tuple-element.67) | copy-start | bytes 832948
  58.5 8.6 %copy-start.15 = (pred[134,518]{1,0:T(8,128)(4,1)S(1)}, pred[134,518]{1,0:T(8,128)(4,1)}, u32[]{:S(2)}) copy-start(pred[134,518]{1,0:T(8,128)(4,1)} %slice_compare_fusion) | copy-start | bytes 208240
  67.1 1.0 copy-start.3
  77.9 4.1 %copy-start.16 = (f32[32,128]{0,1:T(8,128)S(1)}, f32[32,128]{0,1:T(8,128)}, u32[]{:S(2)}) copy-start(f32[32,128]{0,1:T(8,128)} %copy.91) | copy-start | bytes 49156
  79.0 16.0 %copy-start.2 = (f32[2,128,512]{2,1,0:T(8,128)}, f32[2,128,512]{2,1,0:T(8,128)S(1)}, u32[]{:S(2)}) copy-start(f32[2,128,512]{2,1,0:T(8,128)S(1)} %get-tuple-element.34) | copy-start | bytes 1572868
  89.1 19.0 %copy-start.5 = (f32[134,518]{1,0:T(8,128)S(1)}, f32[134,518]{1,0:T(8,128)}, u32[]{:S(2)}) copy-start(f32[134,518]{1,0:T(8,128)} %get-tuple-element.79) | copy-start | bytes 832948
  89.1 19.0 %copy-start.6 = (f32[134,518]{1,0:T(8,128)S(1)}, f32[134,518]{1,0:T(8,128)}, u32[]{:S(2)}) copy-start(f32[134,518]{1,0:T(8,128)} %get-tuple-element.81) | copy-start | bytes 832948
  89.1 19.0 %copy-start.7 = (f32[134,518]{1,0:T(8,128)S(1)}, f32[134,518]{1,0:T(8,128)}, u32[]{:S(2)}) copy-start(f32[134,518]{1,0:T(8,128)} %get-tuple-element.83) | copy-start | bytes 832948
  89.1 19.0 %copy-start.8 = (f32[134,518]{1,0:T(8,128)S(1)}, f32[134,518]{1,0:T(8,128)}, u32[]{:S(2)}) copy-start(f32[134,518]{1,0:T(8,128)} %get-tuple-element.85) | copy-start | bytes 832948
  89.1 19.0 %copy-start.9 = (f32[134,518]{1,0:T(8,128)S(1)}, f32[134,518]{1,0:T(8,128)}, u32[]{:S(2)}) copy-start(f32[134,518]{1,0:T(8,128)} %get-tuple-element.94) | copy-start | bytes 832948
  89.1 19.0 %copy-start.10 = (f32[134,518]{1,0:T(8,128)S(1)}, f32[134,518]{1,0:T(8,128)}, u32[]{:S(2)}) copy-start(f32[134,518]{1,0:T(8,128)} %get-tuple-element.95) | copy-start | bytes 832948
  98.1 22.7 %all-to-all-start.1 = ((f32[256,1,128]{2,1,0:T(1,128)}), f32[256,1,128]{2,1,0:T(1,128)S(1)}, u32[]{:S(2)}, u32[]{:S(2)}) async-start(f32[256,1,128]{2,1,0:T(1,128)} %bitcast.186), calls=%async_computation.1 | async-start | bytes 262144 | tf_op jit(solution)/shard_map/all_to_all | solution.py:204

commit v4 on v3

--- a/solution.py
+++ b/solution.py
@@ -11,11 +11,21 @@
 offsets = [(rr, cc) for rr in range(-3, 4) for cc in range(-3, 4) if 0 < rr * rr + cc * cc <= 9]
 
 
-def contact_kernel(meta_ref, win_ref, pos_ref, xr_ref, xc_ref, out_ref):
+def contact_kernel(meta_ref, geo_ref, pos_ref, xr_ref, xc_ref, out_ref):
     out_ref[...] = jnp.zeros_like(out_ref)
     blocks, _, panels, _ = out_ref.shape
-    row_tiles = xr_ref.shape[0] // 8
-    col_tiles = xr_ref.shape[1] // 128
+    rows, cols = xr_ref.shape
+    row_tiles = rows // 8
+    col_tiles = cols // 128
+    reach_row, reach_col = geo_ref[0], geo_ref[1]
+    row_base, col_base = geo_ref[2], geo_ref[3]
+
+    def window(centre, base, reach, size, group):
+        local = centre - base
+        low = jnp.clip((local - reach).astype(jnp.int32), 0, size)
+        high = jnp.clip((local + reach).astype(jnp.int32) + 1, 0, size)
+        first = low // group
+        return first, jnp.maximum((high + group - 1) // group - first, 0)
 
     def tile_sums(centre_row, centre_col, row_group, col_group, accs):
         row = pl.multiple_of(row_group * 8, 8)
@@ -38,8 +48,10 @@
             slot = block * panels + j
             centre_row = pos_ref[2 * slot]
             centre_col = pos_ref[2 * slot + 1]
-            first_row = jnp.minimum(win_ref[4 * slot], row_tiles - 2)
-            first_col = jnp.minimum(win_ref[4 * slot + 2], col_tiles - 2)
+            first_row, _ = window(centre_row, row_base, reach_row, rows, 8)
+            first_col, _ = window(centre_col, col_base, reach_col, cols, 128)
+            first_row = jnp.minimum(first_row, row_tiles - 2)
+            first_col = jnp.minimum(first_col, col_tiles - 2)
             accs = (zero, zero)
             for r in range(2):
                 for c in range(2):
@@ -56,10 +68,8 @@
             slot = block * panels + j
             centre_row = pos_ref[2 * slot]
             centre_col = pos_ref[2 * slot + 1]
-            first_row = win_ref[4 * slot]
-            row_groups = win_ref[4 * slot + 1]
-            first_col = win_ref[4 * slot + 2]
-            col_groups = win_ref[4 * slot + 3]
+            first_row, row_groups = window(centre_row, row_base, reach_row, rows, 8)
+            first_col, col_groups = window(centre_col, col_base, reach_col, cols, 128)
 
             def per_row(r, accs):
                 def per_col(c, accs):
@@ -72,19 +82,19 @@
 
         return lax.fori_loop(0, panels, per_panel, carry)
 
-    narrow = meta_ref[1 + blocks]
-
-    @pl.when(narrow == 1)
+    narrow = (reach_row < 4.0) & (reach_col < 4.0)
+
+    @pl.when(narrow)
     def _():
         lax.fori_loop(0, meta_ref[0], per_block_narrow, 0)
 
-    @pl.when(narrow == 0)
+    @pl.when(jnp.logical_not(narrow))
     def _():
         lax.fori_loop(0, meta_ref[0], per_block_wide, 0)
 
 
-def contact_sums(meta, windows, positions, rows_x, cols_x):
-    blocks = meta.shape[0] - 2
+def contact_sums(meta, geometry, positions, rows_x, cols_x):
+    blocks = meta.shape[0] - 1
     smem = pl.BlockSpec(memory_space=pltpu.SMEM)
     vmem = pl.BlockSpec(memory_space=pltpu.VMEM)
     return pl.pallas_call(
@@ -92,7 +102,7 @@
         out_shape=jax.ShapeDtypeStruct((blocks, 2, PAN_DEV, 128), jnp.float32),
         in_specs=[smem, smem, smem, vmem, vmem],
         out_specs=vmem,
-    )(meta, windows, positions, rows_x, cols_x)
+    )(meta, geometry, positions, rows_x, cols_x)
 
 
 def with_halo(block, sides, width):
@@ -182,20 +192,11 @@
     cols_x = (col_base + jnp.arange(cols, dtype=jnp.int32)).astype(jnp.float32)[None, :] + state_u[1]
     reach_row = 2.5 + jnp.max(jnp.abs(state_u[0]))
     reach_col = 2.5 + jnp.max(jnp.abs(state_u[1]))
-    local_row = all_pos[:, :, 0] - row_base.astype(jnp.float32)
-    local_col = all_pos[:, :, 1] - col_base.astype(jnp.float32)
-    row_lo = jnp.clip(jnp.floor(local_row - reach_row), 0, rows).astype(jnp.int32)
-    row_hi = jnp.clip(jnp.floor(local_row + reach_row) + 1, 0, rows).astype(jnp.int32)
-    col_lo = jnp.clip(jnp.floor(local_col - reach_col), 0, cols).astype(jnp.int32)
-    col_hi = jnp.clip(jnp.floor(local_col + reach_col) + 1, 0, cols).astype(jnp.int32)
-    first_row = row_lo // 8
-    row_groups = jnp.maximum((row_hi + 7) // 8 - first_row, 0)
-    first_col = col_lo // 128
-    col_groups = jnp.maximum((col_hi + 127) // 128 - first_col, 0)
-    windows = jnp.stack([first_row, row_groups, first_col, col_groups], axis=-1).reshape(-1)
-    narrow = (jnp.max(row_groups) <= 2) & (jnp.max(col_groups) <= 2)
-    meta = jnp.concatenate([n_listed[None], listed_blocks, narrow.astype(jnp.int32)[None]])
-    sums = contact_sums(meta, windows, all_pos.reshape(-1), rows_x, cols_x)
+    geometry = jnp.stack(
+        [reach_row, reach_col, row_base.astype(jnp.float32), col_base.astype(jnp.float32)]
+    )
+    meta = jnp.concatenate([n_listed[None], listed_blocks])
+    sums = contact_sums(meta, geometry, all_pos.reshape(-1), rows_x, cols_x)
     partials = jnp.transpose(jnp.sum(sums, axis=-1), (0, 2, 1))
     spread = jnp.broadcast_to(
         partials.reshape(block_count, 1, 1, 2 * PAN_DEV),

time: 122 us -> 119 us (0.975); the launches traced: 122 us -> 118 us
  Pallas kernels: 5.92 us -> 12.2 us
  starting transfers between devices: 33.1 us -> 29 us
  local copies, waits for them, and re-layouts: 10 us -> 7.25 us
  other arithmetic: 53.9 us -> 52.1 us
  between operations: 3.74 us -> 2.32 us
    pallas_call x1, Pallas kernels: 5.92 us -> 12.2 us  [contact_sums(): pl.pallas_call(contact_kernel, out_shape=jax.ShapeDtypeStruct((blocks, 2,...]
    all_to_all x1, starting transfers between devices: 9.95 us -> 5.86 us  [body(): arrived = lax.all_to_all(spread, ('along', 'across'), 0, 0, tiled=True)]
    another operation x2 -> x0, local copies, waits for them, and re-layouts: 1.6 us -> none  [the longest x1 0.99 us: body(): jnp.stack([first_row, row_groups, first_col, col_groups], axis=-1)]
    reduce_max x2 -> x0, other arithmetic: 1.36 us -> none  [body(): narrow = (jnp.max(row_groups) <= 2) & (jnp.max(col_groups) <= 2)]
    reshape x1 -> x0, local copies, waits for them, and re-layouts: 1.24 us -> none  [body(): jnp.stack([first_row, row_groups, first_col, col_groups], axis=-1)]
  transfers between devices with their start and end apart: 6 -> 6, of which waited for: 3 -> 3; matrix products, arithmetic and copies ran while one was open for 10% -> 11% of each run, Pallas kernels for 0% -> 0%
where the time goes in v4:
time: 119 us; the launch traced here: 118 us
  other arithmetic  52.1 us (44%)
  starting transfers between devices  29 us (24%)
  waiting for transfers between devices  14.6 us (12%)
  Pallas kernels  12.2 us (10%)
  local copies, waits for them, and re-layouts  7.25 us (6%)
  between operations  2.32 us (2%)
    another operation x4, other arithmetic, forces(): return (jnp.stack([total_row, total_col]), kept_sum, exist_sum)  31 us
    all_to_all x1, starting transfers between devices, body(): lax.all_to_all(jnp.broadcast_to(packed[None], (block_count,) + packed.sha...  12.7 us
    pallas_call x1, Pallas kernels, contact_sums(): pl.pallas_call(contact_kernel, out_shape=jax.ShapeDtypeStruct((blocks, 2,...  12.2 us
    all_to_all x1, waiting for transfers between devices, body(): arrived = lax.all_to_all(spread, ('along', 'across'), 0, 0, tiled=True)  9.11 us
    ppermute x2, starting transfers between devices, with_halo(): low = lax.ppermute(low, axis, forward).reshape(strip)  7.24 us
    all_to_all x1, starting transfers between devices, body(): arrived = lax.all_to_all(spread, ('along', 'across'), 0, 0, tiled=True)  5.86 us
    all_to_all x1, waiting for transfers between devices, body(): lax.all_to_all(jnp.broadcast_to(packed[None], (block_count,) + packed.sha...  3.83 us
    sub x1, other arithmetic, body(): damage = 1.0 - kept_sum[3:-3, 3:-3] / exist_sum[3:-3, 3:-3]  3.56 us
  transfers between devices with their start and end apart: 6, of which 3 were waited for; matrix products, arithmetic and copies ran while one was open for 11% of the time, Pallas kernels for 0%

profile of v4, /device:TPU:1, one launch (start us, length us, event | category | flops | bytes accessed | tf_op | source)
XLA Modules:
  0.0 117.5 jit_solution(16411595644194084259)
XLA Ops:
  0.7 1.1 convert_element_type.388
  1.7 0.8 pad_maximum_fusion.18
  2.6 4.9 %collective-permute-start = (f32[6,6,512]{2,1,0:T(8,128)S(1)}, f32[6,6,512]{2,1,0:T(8,128)S(1)}, u32[]{:S(2)}, u32[]{:S(2)}) collective-permute-start(f32[6,6,512]{2,1,0:T(8,128)S(1)} %get-tuple-element.88), channel_id=1, source_target_pairs={{0,8},{8,16},{16,24},{24,32},{32,40},{40,48},{48,56},{56,64},{64,7... | collective-permute-start | bytes 221192 | tf_op jit(solution)/shard_map/ppermute | solution.py:119
  7.5 1.9 %collective-permute-start.1 = (f32[6,6,512]{2,1,0:T(8,128)S(1)}, f32[6,6,512]{2,1,0:T(8,128)S(1)}, u32[]{:S(2)}, u32[]{:S(2)}) collective-permute-start(f32[6,6,512]{2,1,0:T(8,128)S(1)} %get-tuple-element.89), channel_id=1, source_target_pairs={{8,0},{16,8},{24,16},{32,24},{40,32},{48,40},{56,48},{64,56},{72,6... | collective-permute-start | bytes 221192 | tf_op jit(solution)/shard_map/ppermute | solution.py:120
  9.7 0.6 broadcast_in_dim.39
  10.4 12.7 %all-to-all-start = ((f32[32,1,132]{2,1,0:T(1,128)}), f32[32,1,132]{2,1,0:T(1,128)S(1)}, u32[]{:S(2)}, u32[]{:S(2)}) async-start(f32[32,1,132]{2,1,0:T(1,128)} %broadcast_in_dim.39), calls=%async_computation | async-start | bytes 65536 | tf_op jit(solution)/shard_map/all_to_all | solution.py:180
  23.2 0.8 slice_compare_fusion
  24.0 1.9 %fusion.300 = (f32[134,518]{1,0:T(8,128)}, f32[134,518]{1,0:T(8,128)}, f32[134,518]{1,0:T(8,128)}, f32[134,518]{1,0:T(8,128)}, f32[134,518]{1,0:T(8,128)}, /*index=5*/f32[134,518]{1,0:T(8,128)}) fusion(f32[140,524]{1,0:T(8,128)S(1)} %and_convert_fusion), kind=kLoop, calls=%fused_computation.523 | loop fusion | bytes 3331776 | tf_op jit(solution)/shard_map/slice | solution.py:133
  25.9 2.7 %add_add_fusion = f32[134,518]{1,0:T(8,128)} fusion(f32[140,524]{1,0:T(8,128)S(1)} %and_convert_fusion), kind=kLoop, calls=%fused_computation.210 | loop fusion | flops 1457652 | bytes 6385904 | tf_op jit(solution)/shard_map/add | solution.py:146
  28.6 3.8 %all-to-all-done = f32[32,1,132]{2,1,0:T(1,128)S(1)} async-done(((f32[32,1,132]{2,1,0:T(1,128)}), f32[32,1,132]{2,1,0:T(1,128)S(1)}, u32[]{:S(2)}, u32[]{:S(2)}) %all-to-all-start) | async-done | bytes 16928 | tf_op jit(solution)/shard_map/all_to_all | solution.py:180
  32.9 0.5 slice.1365
  34.0 2.3 %collective-permute-start.2 = (f32[5040]{0:T(1024)S(1)}, f32[5040]{0:T(1024)S(1)}, u32[]{:S(2)}, u32[]{:S(2)}) collective-permute-start(f32[5040]{0:T(1024)S(1)} %reshape.650), channel_id=1, source_target_pairs={{0,1},{1,2},{2,3},{3,4},{4,5},{5,6},{6,7},{8,9},{9,10},{10,11},{11... | collective-permute-start | bytes 60488 | tf_op jit(solution)/shard_map/ppermute | solution.py:119
  36.6 1.3 %collective-permute-start.3 = (f32[5040]{0:T(1024)S(1)}, f32[5040]{0:T(1024)S(1)}, u32[]{:S(2)}, u32[]{:S(2)}) collective-permute-start(f32[5040]{0:T(1024)S(1)} %reshape.652), channel_id=1, source_target_pairs={{1,0},{2,1},{3,2},{4,3},{5,4},{6,5},{7,6},{9,8},{10,9},{11,10},{12... | collective-permute-start | bytes 60488 | tf_op jit(solution)/shard_map/ppermute | solution.py:120
  37.9 1.2 %pad_add_fusion.meta_ref = s32[33]{0:T(128)} fusion(s32[32]{0:T(128)S(1)} %convert_reduce_fusion, s32[1]{0:T(128)} %bitcast.175), kind=kLoop, calls=%fused_computation.519 | loop fusion | flops 33 | bytes 264 | tf_op jit(solution)/shard_map/concatenate | solution.py:198
  39.1 0.7 copy.43
  40.0 1.7 %collective-permute-done.3 = f32[5040]{0:T(1024)S(1)} collective-permute-done((f32[5040]{0:T(1024)S(1)}, f32[5040]{0:T(1024)S(1)}, u32[]{:S(2)}, u32[]{:S(2)}) %collective-permute-start.3) | collective-permute-done | bytes 20192 | tf_op jit(solution)/shard_map/ppermute | solution.py:120
  41.9 0.9 pad_maximum_fusion
  43.1 2.7 %add_add_fusion.1 = f32[134,518]{1,0:T(8,128)} fusion(f32[140,524]{1,0:T(8,128)S(1)} %and_convert_fusion, s32[2,134,518]{2,1,0:T(8,128)S(1)} %slice_convert_fusion), kind=kLoop, calls=%fused_computation.211 | loop fusion | flops 7565908 | bytes 6941200 | tf_op jit(solution)/shard_map/add | solution.py:145
  45.8 12.8 %add_bitcast_fusion.1 = (f32[1,134,518]{2,1,0:T(8,128)}, f32[134,518]{1,0:T(8,128)S(1)}, f32[134,518]{1,0:T(8,128)S(1)}, f32[134,518]{1,0:T(8,128)S(1)}, f32[134...) fusion(f32[6,140,524]{2,1,0:T(8,128)S(1)} %pad_maximum_fusion, ...), kind=kLoop, calls=%fused_computation.213 | loop fusion | flops 33248348 | bytes 30358384 | tf_op jit(solution)/shard_map/stack | solution.py:147
  58.5 8.6 %add_bitcast_fusion = f32[1,134,518]{2,1,0:T(8,128)S(1)} fusion(f32[134,518]{1,0:T(8,128)} %get-tuple-element.84, f32[134,518]{1,0:T(8,128)} %get-tuple-element.82, f32[134,518]{1,0:T(8,128)} %get-tuple-element.80, f32[134,518]{1,0:T(8,128)S(1)} %get-tuple-element.78, f32[134,518]{1,0:T(8,128)S(1)} %get-tuple-element.77, ...), kind=kLoop, calls=%fused_computation.212 | loop fusion | flops 23738904 | bytes 22489488 | tf_op jit(solution)/shard_map/stack | solution.py:147
  68.2 7.7 %add_bitcast_fusion.3 = (f32[1,128,512]{2,1,0:T(8,128)S(1)}, f32[128,512]{1,0:T(8,128)S(1)}, f32[128,512]{1,0:T(8,128)S(1)}, f32[128,512]{1,0:T(8,128)S(1)}, f32...) fusion(f32[2,134,518]{2,1,0:T(8,128)S(1)} %get-tuple-element.65, ...), kind=kLoop, calls=%fused_computation.501 | loop fusion | flops 30081024 | bytes 30670848 | tf_op jit(solution)/shard_map/stack | solution.py:147
  75.8 2.0 %add_bitcast_fusion.2 = f32[1,128,512]{2,1,0:T(8,128)S(1)} fusion(f32[128,512]{1,0:T(8,128)S(1)} %get-tuple-element.64, f32[128,512]{1,0:T(8,128)S(1)} %get-tuple-element.63, f32[128,512]{1,0:T(8,128)S(1)} %get-tuple-element.62, f32[128,512]{1,0:T(8,128)S(1)} %get-tuple-element.61, f32[128,512]{1,0:T(8,128)S(1)} %get-tuple-element.60, ...), kind=kLoop, calls=%fused_computation.500 | loop fusion | flops 6881280 | bytes 15204352 | tf_op jit(solution)/shard_map/stack | solution.py:147
  77.9 1.2 slice_add_fusion.3
  79.1 1.6 %fusion.262 = (f32[128,512]{1,0:T(8,128)}, f32[128,512]{1,0:T(8,128)}, f32[]{:T(128)}, f32[]{:T(128)}) fusion(f32[2,128,512]{2,1,0:T(8,128)S(1)} %get-tuple-element.34, f32[512]{0:T(512)S(1)} %add_convert_fusion, f32[128]{0:T(128)S(1)} %add_convert_fusion.1), kind=kLoop, calls=%fused_computation.503 | loop fusion | flops 393214 | bytes 1051144 | tf_op jit(solution)/shard_map/add | solution.py:192
  81.9 0.6 pad_maximum_fusion.20.geo_ref
  82.5 12.2 %shard_map.84 = f32[32,2,64,128]{3,2,1,0:T(8,128)} custom-call(s32[33]{0:T(128)} %pad_add_fusion.meta_ref, f32[4]{0:T(128)} %pad_maximum_fusion.20.geo_ref, f32[4096]{0:T(1024)} %bitcast.1103, f32[128,512]{1,0:T(8,128)} %get-tuple-element.91.xr_ref, f32[128,512]{1,0:T(8,128)} %get-tuple-element.90.xc_ref), custom_call_target="tpu_custom_call" | custom-call | tf_op jit(solution)/shard_map/pallas_call | solution.py:100
  94.8 2.2 %reduce_sum.28 = f32[32,2,64]{2,1,0:T(2,128)S(1)} reduce(f32[32,2,64,128]{3,2,1,0:T(8,128)} %shard_map.84, f32[]{:T(128)} %constant.139.clone.1), dimensions={3}, to_apply=%region_5.6 | reduce | flops 520192 | bytes 2113540 | tf_op jit(solution)/shard_map/reduce_sum | solution.py:200
  97.2 0.7 broadcast_in_dim.41
  97.8 5.9 %all-to-all-start.1 = ((f32[256,1,128]{2,1,0:T(1,128)}), f32[256,1,128]{2,1,0:T(1,128)S(1)}, u32[]{:S(2)}, u32[]{:S(2)}) async-start(f32[256,1,128]{2,1,0:T(1,128)} %bitcast.185), calls=%async_computation.1 | async-start | bytes 262144 | tf_op jit(solution)/shard_map/all_to_all | solution.py:205
  103.8 3.6 %fusion.104 = f32[128,512]{1,0:T(8,128)} fusion(f32[134,518]{1,0:T(8,128)} %get-tuple-element.96, f32[134,518]{1,0:T(8,128)S(1)} %copy-done.10, f32[134,518]{1,0:T(8,128)} %get-tuple-element.97, f32[134,518]{1,0:T(8,128)} %get-tuple-element.99, f32[134,518]{1,0:T(8,128)} %get-tuple-element.98, f32[134,518]{1,0:T(8,128)S(1)} %copy-done.9, ...), kind=kLoop, calls=%fused_computation.246 | loop fusion | flops 917504 | bytes 3932160 | tf_op jit(solution)/shard_map/sub | solution.py:169
  107.3 9.1 %all-to-all-done.1 = f32[256,1,128]{2,1,0:T(1,128)S(1)} async-done(((f32[256,1,128]{2,1,0:T(1,128)}), f32[256,1,128]{2,1,0:T(1,128)S(1)}, u32[]{:S(2)}, u32[]{:S(2)}) %all-to-all-start.1) | async-done | bytes 131104 | tf_op jit(solution)/shard_map/all_to_all | solution.py:205
  116.9 0.6 copy.46
  (67 shorter events, 3.9 us)
Async XLA Ops:
  0.6 8.8 %copy-start.16 = (f32[64,2]{0,1:T(2,128)S(1)}, f32[64,2]{0,1:T(2,128)}, u32[]{:S(2)}) copy-start(f32[64,2]{0,1:T(2,128)} %param.8) | copy-start | bytes 1540
  0.6 9.1 %copy-start.17 = (s32[1,4]{1,0:T(1,128)S(1)}, s32[1,4]{1,0:T(1,128)}, u32[]{:S(2)}) copy-start(s32[1,4]{1,0:T(1,128)} %param.9) | copy-start | bytes 52
  2.6 30.9 %collective-permute-start = (f32[6,6,512]{2,1,0:T(8,128)S(1)}, f32[6,6,512]{2,1,0:T(8,128)S(1)}, u32[]{:S(2)}, u32[]{:S(2)}) collective-permute-start(f32[6,6,512]{2,1,0:T(8,128)S(1)} %get-tuple-element.88), channel_id=1, source_target_pairs={{0,8},{8,16},{16,24},{24,32},{32,40},{40,48},{48,56},{56,64},{64,7... | collective-permute-start | bytes 221192 | tf_op jit(solution)/shard_map/ppermute | solution.py:119
  7.5 26.0 %collective-permute-start.1 = (f32[6,6,512]{2,1,0:T(8,128)S(1)}, f32[6,6,512]{2,1,0:T(8,128)S(1)}, u32[]{:S(2)}, u32[]{:S(2)}) collective-permute-start(f32[6,6,512]{2,1,0:T(8,128)S(1)} %get-tuple-element.89), channel_id=1, source_target_pairs={{8,0},{16,8},{24,16},{32,24},{40,32},{48,40},{56,48},{64,56},{72,6... | collective-permute-start | bytes 221192 | tf_op jit(solution)/shard_map/ppermute | solution.py:120
  10.4 22.1 %all-to-all-start = ((f32[32,1,132]{2,1,0:T(1,128)}), f32[32,1,132]{2,1,0:T(1,128)S(1)}, u32[]{:S(2)}, u32[]{:S(2)}) async-start(f32[32,1,132]{2,1,0:T(1,128)} %broadcast_in_dim.39), calls=%async_computation | async-start | bytes 65536 | tf_op jit(solution)/shard_map/all_to_all | solution.py:180
  25.9 7.6 %copy-start = (f32[2,128,512]{2,1,0:T(8,128)S(1)}, f32[2,128,512]{2,1,0:T(8,128)}, u32[]{:S(2)}) copy-start(f32[2,128,512]{2,1,0:T(8,128)} %param.6) | copy-start | bytes 1572868
  25.9 7.6 %copy-start.1 = (f32[2,128,512]{2,1,0:T(8,128)S(1)}, f32[2,128,512]{2,1,0:T(8,128)}, u32[]{:S(2)}) copy-start(f32[2,128,512]{2,1,0:T(8,128)} %param.5) | copy-start | bytes 1572868
  33.5 8.3 %copy-start.11 = (f32[6,6,512]{2,1,0:T(8,128)}, f32[6,6,512]{2,1,0:T(8,128)S(1)}, u32[]{:S(2)}) copy-start(f32[6,6,512]{2,1,0:T(8,128)S(1)} %collective-permute-done) | copy-start | bytes 221188
  33.6 8.3 %copy-start.13 = (f32[6,6,512]{2,1,0:T(8,128)}, f32[6,6,512]{2,1,0:T(8,128)S(1)}, u32[]{:S(2)}) copy-start(f32[6,6,512]{2,1,0:T(8,128)S(1)} %collective-permute-done.1) | copy-start | bytes 221188
  34.0 5.8 %collective-permute-start.2 = (f32[5040]{0:T(1024)S(1)}, f32[5040]{0:T(1024)S(1)}, u32[]{:S(2)}, u32[]{:S(2)}) collective-permute-start(f32[5040]{0:T(1024)S(1)} %reshape.650), channel_id=1, source_target_pairs={{0,1},{1,2},{2,3},{3,4},{4,5},{5,6},{6,7},{8,9},{9,10},{10,11},{11... | collective-permute-start | bytes 60488 | tf_op jit(solution)/shard_map/ppermute | solution.py:119
  36.6 5.1 %collective-permute-start.3 = (f32[5040]{0:T(1024)S(1)}, f32[5040]{0:T(1024)S(1)}, u32[]{:S(2)}, u32[]{:S(2)}) collective-permute-start(f32[5040]{0:T(1024)S(1)} %reshape.652), channel_id=1, source_target_pairs={{1,0},{2,1},{3,2},{4,3},{5,4},{6,5},{7,6},{9,8},{10,9},{11,10},{12... | collective-permute-start | bytes 60488 | tf_op jit(solution)/shard_map/ppermute | solution.py:120
  43.0 2.7 %copy-start.12 = (f32[6,6,512]{2,1,0:T(8,128)S(1)}, f32[6,6,512]{2,1,0:T(8,128)}, u32[]{:S(2)}) copy-start(f32[6,6,512]{2,1,0:T(8,128)} %copy-done.11) | copy-start | bytes 221188
  43.1 2.7 %copy-start.14 = (f32[6,6,512]{2,1,0:T(8,128)S(1)}, f32[6,6,512]{2,1,0:T(8,128)}, u32[]{:S(2)}) copy-start(f32[6,6,512]{2,1,0:T(8,128)} %copy-done.13) | copy-start | bytes 221188
  58.5 8.6 %copy-start.4 = (f32[1,134,518]{2,1,0:T(8,128)S(1)}, f32[1,134,518]{2,1,0:T(8,128)}, u32[]{:S(2)}) copy-start(f32[1,134,518]{2,1,0:T(8,128)} %get-tuple-element.67) | copy-start | bytes 832948
  58.5 8.6 %copy-start.15 = (pred[134,518]{1,0:T(8,128)(4,1)S(1)}, pred[134,518]{1,0:T(8,128)(4,1)}, u32[]{:S(2)}) copy-start(pred[134,518]{1,0:T(8,128)(4,1)} %slice_compare_fusion) | copy-start | bytes 208240
  67.1 1.0 copy-start.3
  79.1 17.9 %copy-start.2 = (f32[2,128,512]{2,1,0:T(8,128)}, f32[2,128,512]{2,1,0:T(8,128)S(1)}, u32[]{:S(2)}) copy-start(f32[2,128,512]{2,1,0:T(8,128)S(1)} %get-tuple-element.34) | copy-start | bytes 1572868
  82.5 21.2 %copy-start.5 = (f32[134,518]{1,0:T(8,128)S(1)}, f32[134,518]{1,0:T(8,128)}, u32[]{:S(2)}) copy-start(f32[134,518]{1,0:T(8,128)} %get-tuple-element.79) | copy-start | bytes 832948
  82.5 21.2 %copy-start.6 = (f32[134,518]{1,0:T(8,128)S(1)}, f32[134,518]{1,0:T(8,128)}, u32[]{:S(2)}) copy-start(f32[134,518]{1,0:T(8,128)} %get-tuple-element.81) | copy-start | bytes 832948
  82.5 21.2 %copy-start.7 = (f32[134,518]{1,0:T(8,128)S(1)}, f32[134,518]{1,0:T(8,128)}, u32[]{:S(2)}) copy-start(f32[134,518]{1,0:T(8,128)} %get-tuple-element.83) | copy-start | bytes 832948
  82.5 21.2 %copy-start.8 = (f32[134,518]{1,0:T(8,128)S(1)}, f32[134,518]{1,0:T(8,128)}, u32[]{:S(2)}) copy-start(f32[134,518]{1,0:T(8,128)} %get-tuple-element.85) | copy-start | bytes 832948
  82.5 21.2 %copy-start.9 = (f32[134,518]{1,0:T(8,128)S(1)}, f32[134,518]{1,0:T(8,128)}, u32[]{:S(2)}) copy-start(f32[134,518]{1,0:T(8,128)} %get-tuple-element.94) | copy-start | bytes 832948
  82.5 21.2 %copy-start.10 = (f32[134,518]{1,0:T(8,128)S(1)}, f32[134,518]{1,0:T(8,128)}, u32[]{:S(2)}) copy-start(f32[134,518]{1,0:T(8,128)} %get-tuple-element.95) | copy-start | bytes 832948
  97.8 18.6 %all-to-all-start.1 = ((f32[256,1,128]{2,1,0:T(1,128)}), f32[256,1,128]{2,1,0:T(1,128)S(1)}, u32[]{:S(2)}, u32[]{:S(2)}) async-start(f32[256,1,128]{2,1,0:T(1,128)} %bitcast.185), calls=%async_computation.1 | async-start | bytes 262144 | tf_op jit(solution)/shard_map/all_to_all | solution.py:205

commit v5 on v4

--- a/solution.py
+++ b/solution.py
@@ -120,6 +120,19 @@
         high = lax.ppermute(high, axis, backward).reshape(strip)
         block = jnp.concatenate([low, block, high], axis=dim)
     return block
+
+
+def bond_counts(bits, present_pad, rows, cols):
+    kept_sum = jnp.zeros((rows, cols), jnp.float32)
+    exist_sum = jnp.zeros((rows, cols), jnp.float32)
+    for index, (row_off, col_off) in enumerate(offsets):
+        present = present_pad[3 + row_off : 3 + row_off + rows, 3 + col_off : 3 + col_off + cols]
+        flag = jnp.bitwise_and(jnp.right_shift(bits[index // 14], index % 14), 1).astype(
+            jnp.float32
+        )
+        kept_sum = kept_sum + flag * present
+        exist_sum = exist_sum + present
+    return kept_sum, exist_sum
 
 
 def forces(padded, bits, present_pad, rows, cols):
@@ -163,10 +176,11 @@
     inside_col = (grid_col >= 0) & (grid_col < total_cols)
     present_wide = (inside_row[:, None] & inside_col[None, :]).astype(jnp.float32)
     present_ring = present_wide[3:-3, 3:-3]
-    force, kept_sum, exist_sum = forces(
+    force, _, _ = forces(
         ext[0:2], ext[4:6, 3:-3, 3:-3].astype(jnp.int32), present_wide, rows + 6, cols + 6
     )
-    damage = 1.0 - kept_sum[3:-3, 3:-3] / exist_sum[3:-3, 3:-3]
+    kept_sum, exist_sum = bond_counts(bond_bits, present_ring, rows, cols)
+    damage = 1.0 - kept_sum / exist_sum
     ring_v = ext[2:4, 3:-3, 3:-3] + 10.0 * force
     ring_u = ext[0:2, 3:-3, 3:-3] + 0.05 * ring_v
     ring_u = jnp.where(present_ring[None] > 0.0, ring_u, 0.0)

time: 119 us -> 123 us (1.034); the launches traced: 118 us -> 123 us
  waiting for transfers between devices: 14.6 us -> 20.3 us
  other arithmetic: 52.1 us -> 48.8 us
  starting transfers between devices: 29 us -> 32.1 us
  local copies, waits for them, and re-layouts: 7.25 us -> 5.32 us
  Pallas kernels: 12.2 us -> 14 us
    add x2 -> x0, other arithmetic: 5.41 us -> none  [the longest x1 2.72 us: forces(): exist_sum = exist_sum + present]
    all_to_all x1, waiting for transfers between devices: 3.83 us -> 8.48 us  [body(): lax.all_to_all(jnp.broadcast_to(packed[None], (block_count,) + packed.sha...]
    all_to_all x1, starting transfers between devices: 5.86 us -> 8.99 us  [body(): arrived = lax.all_to_all(spread, ('along', 'across'), 0, 0, tiled=True)]
    another operation x4, other arithmetic: 31 us -> 33 us  [forces(): return (jnp.stack([total_row, total_col]), kept_sum, exist_sum)]
    slice x1 -> x0, local copies, waits for them, and re-layouts: 1.92 us -> none  [forces(): present_pad[3 + row_off:3 + row_off + rows, 3 + col_off:3 + col_off + cols]]
    pallas_call x1, Pallas kernels: 12.2 us -> 14 us  [contact_sums(): pl.pallas_call(contact_kernel, out_shape=jax.ShapeDtypeStruct((blocks, 2,...]
  transfers between devices with their start and end apart: 6 -> 6, of which waited for: 3 -> 3; matrix products, arithmetic and copies ran while one was open for 11% -> 6% of each run, Pallas kernels for 0% -> 0%
where the time goes in v5:
time: 123 us
  other arithmetic  48.8 us (40%)
  starting transfers between devices  32.1 us (26%)
  waiting for transfers between devices  20.3 us (17%)
  Pallas kernels  14 us (11%)
  local copies, waits for them, and re-layouts  5.32 us (4%)
  between operations  2.25 us (2%)
    another operation x4, other arithmetic, forces(): return (jnp.stack([total_row, total_col]), kept_sum, exist_sum)  33 us
    pallas_call x1, Pallas kernels, contact_sums(): pl.pallas_call(contact_kernel, out_shape=jax.ShapeDtypeStruct((blocks, 2,...  14 us
    all_to_all x1, starting transfers between devices, body(): lax.all_to_all(jnp.broadcast_to(packed[None], (block_count,) + packed.sha...  12.7 us
    all_to_all x1, waiting for transfers between devices, body(): arrived = lax.all_to_all(spread, ('along', 'across'), 0, 0, tiled=True)  10.2 us
    all_to_all x1, starting transfers between devices, body(): arrived = lax.all_to_all(spread, ('along', 'across'), 0, 0, tiled=True)  8.99 us
    all_to_all x1, waiting for transfers between devices, body(): lax.all_to_all(jnp.broadcast_to(packed[None], (block_count,) + packed.sha...  8.48 us
    ppermute x2, starting transfers between devices, with_halo(): low = lax.ppermute(low, axis, forward).reshape(strip)  7.24 us
    ppermute x2, starting transfers between devices, with_halo(): high = lax.ppermute(high, axis, backward).reshape(strip)  3.21 us
  transfers between devices with their start and end apart: 6, of which 3 were waited for; matrix products, arithmetic and copies ran while one was open for 6% of the time, Pallas kernels for 0%

profile of v5, /device:TPU:1, one launch (start us, length us, event | category | flops | bytes accessed | tf_op | source)
XLA Modules:
  0.0 122.9 jit_solution(4205605596076211793)
XLA Ops:
  0.7 1.2 convert_element_type.416
  1.8 0.8 pad_maximum_fusion.18
  2.7 4.9 %collective-permute-start = (f32[6,6,512]{2,1,0:T(8,128)S(1)}, f32[6,6,512]{2,1,0:T(8,128)S(1)}, u32[]{:S(2)}, u32[]{:S(2)}) collective-permute-start(f32[6,6,512]{2,1,0:T(8,128)S(1)} %get-tuple-element.82), channel_id=1, source_target_pairs={{0,8},{8,16},{16,24},{24,32},{32,40},{40,48},{48,56},{56,64},{64,7... | collective-permute-start | bytes 221192 | tf_op jit(solution)/shard_map/ppermute | solution.py:119
  7.6 1.9 %collective-permute-start.1 = (f32[6,6,512]{2,1,0:T(8,128)S(1)}, f32[6,6,512]{2,1,0:T(8,128)S(1)}, u32[]{:S(2)}, u32[]{:S(2)}) collective-permute-start(f32[6,6,512]{2,1,0:T(8,128)S(1)} %get-tuple-element.83), channel_id=1, source_target_pairs={{8,0},{16,8},{24,16},{32,24},{40,32},{48,40},{56,48},{64,56},{72,6... | collective-permute-start | bytes 221192 | tf_op jit(solution)/shard_map/ppermute | solution.py:120
  9.8 0.6 broadcast_in_dim.39
  10.5 12.7 %all-to-all-start = ((f32[32,1,132]{2,1,0:T(1,128)}), f32[32,1,132]{2,1,0:T(1,128)S(1)}, u32[]{:S(2)}, u32[]{:S(2)}) async-start(f32[32,1,132]{2,1,0:T(1,128)} %broadcast_in_dim.39), calls=%async_computation | async-start | bytes 65536 | tf_op jit(solution)/shard_map/all_to_all | solution.py:194
  23.3 0.8 slice_compare_fusion
  24.1 8.5 %all-to-all-done = f32[32,1,132]{2,1,0:T(1,128)S(1)} async-done(((f32[32,1,132]{2,1,0:T(1,128)}), f32[32,1,132]{2,1,0:T(1,128)S(1)}, u32[]{:S(2)}, u32[]{:S(2)}) %all-to-all-start) | async-done | bytes 16928 | tf_op jit(solution)/shard_map/all_to_all | solution.py:194
  33.0 0.5 slice.1399
  34.1 2.3 %collective-permute-start.2 = (f32[5040]{0:T(1024)S(1)}, f32[5040]{0:T(1024)S(1)}, u32[]{:S(2)}, u32[]{:S(2)}) collective-permute-start(f32[5040]{0:T(1024)S(1)} %reshape.650), channel_id=1, source_target_pairs={{0,1},{1,2},{2,3},{3,4},{4,5},{5,6},{6,7},{8,9},{9,10},{10,11},{11... | collective-permute-start | bytes 60488 | tf_op jit(solution)/shard_map/ppermute | solution.py:119
  36.7 1.3 %collective-permute-start.3 = (f32[5040]{0:T(1024)S(1)}, f32[5040]{0:T(1024)S(1)}, u32[]{:S(2)}, u32[]{:S(2)}) collective-permute-start(f32[5040]{0:T(1024)S(1)} %reshape.652), channel_id=1, source_target_pairs={{1,0},{2,1},{3,2},{4,3},{5,4},{6,5},{7,6},{9,8},{10,9},{11,10},{12... | collective-permute-start | bytes 60488 | tf_op jit(solution)/shard_map/ppermute | solution.py:120
  38.0 1.2 %pad_add_fusion.meta_ref = s32[33]{0:T(128)} fusion(s32[32]{0:T(128)S(1)} %convert_reduce_fusion, s32[1]{0:T(128)} %bitcast.175), kind=kLoop, calls=%fused_computation.504 | loop fusion | flops 33 | bytes 264 | tf_op jit(solution)/shard_map/concatenate | solution.py:212
  39.2 0.7 copy.43
  40.1 1.6 %collective-permute-done.3 = f32[5040]{0:T(1024)S(1)} collective-permute-done((f32[5040]{0:T(1024)S(1)}, f32[5040]{0:T(1024)S(1)}, u32[]{:S(2)}, u32[]{:S(2)}) %collective-permute-start.3) | collective-permute-done | bytes 20192 | tf_op jit(solution)/shard_map/ppermute | solution.py:120
  42.0 1.9 %pad_maximum_fusion = f32[6,140,524]{2,1,0:T(8,128)S(1)} fusion(f32[6,140,6]{2,1,0:T(8,128)S(1)} %reshape.653, f32[6,6,512]{2,1,0:T(8,128)} %copy-done.6, f32[2,128,512]{2,1,0:T(8,128)S(1)} %convert_element_type.416, f32[2,128,512]{2,1,0:T(8,128)S(1)} %copy-done, f32[2,128,512]{2,1,0:T(8,128)S(1)} %copy-done.1, f32[6,6,512]{2,1,0:T(8,128)} %copy-done.4, ...), kind=kLoop, calls=%fused_computation | loop fusion | flops 2640960 | bytes 3521280 | tf_op jit(solution)/shard_map/concatenate | solution.py:121
  44.1 13.7 %add_bitcast_fusion.1 = (f32[1,134,518]{2,1,0:T(8,128)S(1)}, f32[134,518]{1,0:T(8,128)S(1)}, f32[134,518]{1,0:T(8,128)}, f32[134,518]{1,0:T(8,128)}, f32[134,518...) fusion(f32[6,140,524]{2,1,0:T(8,128)S(1)} %pad_maximum_fusion, ...), kind=kLoop, calls=%fused_computation.267 | loop fusion | flops 33248348 | bytes 33690160 | tf_op jit(solution)/shard_map/stack | solution.py:160
  57.8 6.5 %add_bitcast_fusion = f32[1,134,518]{2,1,0:T(8,128)S(1)} fusion(f32[134,518]{1,0:T(8,128)} %get-tuple-element.79, f32[134,518]{1,0:T(8,128)} %get-tuple-element.78, f32[134,518]{1,0:T(8,128)} %get-tuple-element.77, f32[134,518]{1,0:T(8,128)} %get-tuple-element.76, f32[134,518]{1,0:T(8,128)} %get-tuple-element.75, f32[134,518]{1,0:T(8,128)} %get-tuple-element.74, ...), kind=kLoop, calls=%fused_computation.266 | loop fusion | flops 8537676 | bytes 17214176 | tf_op jit(solution)/shard_map/stack | solution.py:160
  64.4 0.5 fusion
  64.9 0.5 copy-done.2
  65.4 7.4 %add_bitcast_fusion.3 = (f32[1,128,512]{2,1,0:T(8,128)S(1)}, f32[128,512]{1,0:T(8,128)S(1)}, f32[128,512]{1,0:T(8,128)S(1)}, f32[128,512]{1,0:T(8,128)S(1)}, f32...) fusion(f32[2,134,518]{2,1,0:T(8,128)S(1)} %get-tuple-element.47, ...), kind=kLoop, calls=%fused_computation.458 | loop fusion | flops 30081024 | bytes 25952256 | tf_op jit(solution)/shard_map/stack | solution.py:160
  72.8 5.4 %add_bitcast_fusion.2 = f32[1,128,512]{2,1,0:T(8,128)S(1)} fusion(f32[128,512]{1,0:T(8,128)S(1)} %get-tuple-element.46, f32[128,512]{1,0:T(8,128)S(1)} %get-tuple-element.45, f32[128,512]{1,0:T(8,128)S(1)} %get-tuple-element.44, f32[128,512]{1,0:T(8,128)S(1)} %get-tuple-element.43, f32[128,512]{1,0:T(8,128)S(1)} %get-tuple-element.42, ...), kind=kLoop, calls=%fused_computation.457 | loop fusion | flops 21692416 | bytes 20709376 | tf_op jit(solution)/shard_map/stack | solution.py:160
  78.3 1.2 slice_add_fusion.3
  79.4 1.6 %fusion.260 = (f32[128,512]{1,0:T(8,128)}, f32[128,512]{1,0:T(8,128)}, f32[]{:T(128)}, f32[]{:T(128)}) fusion(f32[2,128,512]{2,1,0:T(8,128)S(1)} %get-tuple-element.34, f32[512]{0:T(512)S(1)} %add_convert_fusion, f32[128]{0:T(128)S(1)} %add_convert_fusion.1), kind=kLoop, calls=%fused_computation.488 | loop fusion | flops 393214 | bytes 1051144 | tf_op jit(solution)/shard_map/add | solution.py:206
  82.3 0.6 pad_maximum_fusion.20.geo_ref
  82.8 14.0 %shard_map.84 = f32[32,2,64,128]{3,2,1,0:T(8,128)} custom-call(s32[33]{0:T(128)} %pad_add_fusion.meta_ref, f32[4]{0:T(128)} %pad_maximum_fusion.20.geo_ref, f32[4096]{0:T(1024)} %bitcast.1129, f32[128,512]{1,0:T(8,128)} %get-tuple-element.85.xr_ref, f32[128,512]{1,0:T(8,128)} %get-tuple-element.84.xc_ref), custom_call_target="tpu_custom_call" | custom-call | tf_op jit(solution)/shard_map/pallas_call | solution.py:100
  96.8 2.2 %reduce_sum.28 = f32[32,2,64]{2,1,0:T(2,128)S(1)} reduce(f32[32,2,64,128]{3,2,1,0:T(8,128)} %shard_map.84, f32[]{:T(128)} %constant.139.clone.1), dimensions={3}, to_apply=%region_5.6 | reduce | flops 520192 | bytes 2113540 | tf_op jit(solution)/shard_map/reduce_sum | solution.py:214
  99.2 0.7 broadcast_in_dim.41
  99.9 9.0 %all-to-all-start.1 = ((f32[256,1,128]{2,1,0:T(1,128)}), f32[256,1,128]{2,1,0:T(1,128)S(1)}, u32[]{:S(2)}, u32[]{:S(2)}) async-start(f32[256,1,128]{2,1,0:T(1,128)} %bitcast.185), calls=%async_computation.1 | async-start | bytes 262144 | tf_op jit(solution)/shard_map/all_to_all | solution.py:219
  108.9 2.7 %divide_subtract_fusion = f32[128,512]{1,0:T(8,128)} fusion(f32[140,524]{1,0:T(8,128)S(1)} %and_convert_fusion, s32[2,128,512]{2,1,0:T(8,128)S(1)} %copy-done.2), kind=kLoop, calls=%fused_computation.456 | loop fusion | flops 11010048 | bytes 8126464 | tf_op jit(solution)/shard_map/sub | solution.py:183
  111.6 10.2 %all-to-all-done.1 = f32[256,1,128]{2,1,0:T(1,128)S(1)} async-done(((f32[256,1,128]{2,1,0:T(1,128)}), f32[256,1,128]{2,1,0:T(1,128)S(1)}, u32[]{:S(2)}, u32[]{:S(2)}) %all-to-all-start.1) | async-done | bytes 131104 | tf_op jit(solution)/shard_map/all_to_all | solution.py:219
  121.8 0.3 reduce_sum.29
  122.2 0.6 copy.46
  (50 shorter events, 2.6 us)
Async XLA Ops:
  0.6 33.0 %copy-start.1 = (f32[2,128,512]{2,1,0:T(8,128)S(1)}, f32[2,128,512]{2,1,0:T(8,128)}, u32[]{:S(2)}) copy-start(f32[2,128,512]{2,1,0:T(8,128)} %param.5) | copy-start | bytes 1572868
  0.6 33.0 %copy-start = (f32[2,128,512]{2,1,0:T(8,128)S(1)}, f32[2,128,512]{2,1,0:T(8,128)}, u32[]{:S(2)}) copy-start(f32[2,128,512]{2,1,0:T(8,128)} %param.6) | copy-start | bytes 1572868
  0.7 8.9 %copy-start.9 = (f32[64,2]{0,1:T(2,128)S(1)}, f32[64,2]{0,1:T(2,128)}, u32[]{:S(2)}) copy-start(f32[64,2]{0,1:T(2,128)} %param.8) | copy-start | bytes 1540
  0.7 9.1 %copy-start.10 = (s32[1,4]{1,0:T(1,128)S(1)}, s32[1,4]{1,0:T(1,128)}, u32[]{:S(2)}) copy-start(s32[1,4]{1,0:T(1,128)} %param.9) | copy-start | bytes 52
  2.7 30.9 %collective-permute-start = (f32[6,6,512]{2,1,0:T(8,128)S(1)}, f32[6,6,512]{2,1,0:T(8,128)S(1)}, u32[]{:S(2)}, u32[]{:S(2)}) collective-permute-start(f32[6,6,512]{2,1,0:T(8,128)S(1)} %get-tuple-element.82), channel_id=1, source_target_pairs={{0,8},{8,16},{16,24},{24,32},{32,40},{40,48},{48,56},{56,64},{64,7... | collective-permute-start | bytes 221192 | tf_op jit(solution)/shard_map/ppermute | solution.py:119
  7.6 26.0 %collective-permute-start.1 = (f32[6,6,512]{2,1,0:T(8,128)S(1)}, f32[6,6,512]{2,1,0:T(8,128)S(1)}, u32[]{:S(2)}, u32[]{:S(2)}) collective-permute-start(f32[6,6,512]{2,1,0:T(8,128)S(1)} %get-tuple-element.83), channel_id=1, source_target_pairs={{8,0},{16,8},{24,16},{32,24},{40,32},{48,40},{56,48},{64,56},{72,6... | collective-permute-start | bytes 221192 | tf_op jit(solution)/shard_map/ppermute | solution.py:120
  10.5 22.1 %all-to-all-start = ((f32[32,1,132]{2,1,0:T(1,128)}), f32[32,1,132]{2,1,0:T(1,128)S(1)}, u32[]{:S(2)}, u32[]{:S(2)}) async-start(f32[32,1,132]{2,1,0:T(1,128)} %broadcast_in_dim.39), calls=%async_computation | async-start | bytes 65536 | tf_op jit(solution)/shard_map/all_to_all | solution.py:194
  33.6 6.3 %copy-start.4 = (f32[6,6,512]{2,1,0:T(8,128)}, f32[6,6,512]{2,1,0:T(8,128)S(1)}, u32[]{:S(2)}) copy-start(f32[6,6,512]{2,1,0:T(8,128)S(1)} %collective-permute-done) | copy-start | bytes 221188
  33.6 6.2 %copy-start.6 = (f32[6,6,512]{2,1,0:T(8,128)}, f32[6,6,512]{2,1,0:T(8,128)S(1)}, u32[]{:S(2)}) copy-start(f32[6,6,512]{2,1,0:T(8,128)S(1)} %collective-permute-done.1) | copy-start | bytes 221188
  34.1 5.8 %collective-permute-start.2 = (f32[5040]{0:T(1024)S(1)}, f32[5040]{0:T(1024)S(1)}, u32[]{:S(2)}, u32[]{:S(2)}) collective-permute-start(f32[5040]{0:T(1024)S(1)} %reshape.650), channel_id=1, source_target_pairs={{0,1},{1,2},{2,3},{3,4},{4,5},{5,6},{6,7},{8,9},{9,10},{10,11},{11... | collective-permute-start | bytes 60488 | tf_op jit(solution)/shard_map/ppermute | solution.py:119
  36.7 5.1 %collective-permute-start.3 = (f32[5040]{0:T(1024)S(1)}, f32[5040]{0:T(1024)S(1)}, u32[]{:S(2)}, u32[]{:S(2)}) collective-permute-start(f32[5040]{0:T(1024)S(1)} %reshape.652), channel_id=1, source_target_pairs={{1,0},{2,1},{3,2},{4,3},{5,4},{6,5},{7,6},{9,8},{10,9},{11,10},{12... | collective-permute-start | bytes 60488 | tf_op jit(solution)/shard_map/ppermute | solution.py:120
  41.9 2.2 %copy-start.5 = (f32[6,6,512]{2,1,0:T(8,128)S(1)}, f32[6,6,512]{2,1,0:T(8,128)}, u32[]{:S(2)}) copy-start(f32[6,6,512]{2,1,0:T(8,128)} %copy-done.4) | copy-start | bytes 221188
  42.0 2.2 %copy-start.7 = (f32[6,6,512]{2,1,0:T(8,128)S(1)}, f32[6,6,512]{2,1,0:T(8,128)}, u32[]{:S(2)}) copy-start(f32[6,6,512]{2,1,0:T(8,128)} %copy-done.6) | copy-start | bytes 221188
  57.8 6.6 %copy-start.8 = (pred[134,518]{1,0:T(8,128)(4,1)S(1)}, pred[134,518]{1,0:T(8,128)(4,1)}, u32[]{:S(2)}) copy-start(pred[134,518]{1,0:T(8,128)(4,1)} %slice_compare_fusion) | copy-start | bytes 208240
  64.4 1.0 copy-start.2
  79.4 19.6 %copy-start.3 = (f32[2,128,512]{2,1,0:T(8,128)}, f32[2,128,512]{2,1,0:T(8,128)S(1)}, u32[]{:S(2)}) copy-start(f32[2,128,512]{2,1,0:T(8,128)S(1)} %get-tuple-element.34) | copy-start | bytes 1572868
  99.9 21.9 %all-to-all-start.1 = ((f32[256,1,128]{2,1,0:T(1,128)}), f32[256,1,128]{2,1,0:T(1,128)S(1)}, u32[]{:S(2)}, u32[]{:S(2)}) async-start(f32[256,1,128]{2,1,0:T(1,128)} %bitcast.185), calls=%async_computation.1 | async-start | bytes 262144 | tf_op jit(solution)/shard_map/all_to_all | solution.py:219

commit v6 on v5

--- a/solution.py
+++ b/solution.py
@@ -194,6 +194,7 @@
     gathered = lax.all_to_all(
         jnp.broadcast_to(packed[None], (block_count,) + packed.shape), "along", 0, 0, tiled=True
     ).reshape(block_count, -1)
+    gathered, state_u = lax.optimization_barrier((gathered, state_u))
     all_pos = gathered[:, : 2 * PAN_DEV].reshape(block_count, PAN_DEV, 2)
     all_lists = gathered[:, 2 * PAN_DEV :].astype(jnp.int32)
     my_tile = lax.axis_index("along") * across_count + lax.axis_index("across")

time: 123 us -> 116 us (0.943)
  waiting for transfers between devices: 20.3 us -> 14.3 us
  starting transfers between devices: 32.1 us -> 29 us
  Pallas kernels: 14 us -> 15.9 us
    all_to_all x1, waiting for transfers between devices: 8.48 us -> 4.11 us  [body(): lax.all_to_all(jnp.broadcast_to(packed[None], (block_count,) + packed.sha...]
    all_to_all x1, starting transfers between devices: 8.99 us -> 5.89 us  [body(): arrived = lax.all_to_all(spread, ('along', 'across'), 0, 0, tiled=True)]
    pallas_call x1, Pallas kernels: 14 us -> 15.9 us  [contact_sums(): pl.pallas_call(contact_kernel, out_shape=jax.ShapeDtypeStruct((blocks, 2,...]
    ppermute x2, waiting for transfers between devices: 1.64 us -> 0.01 us  [with_halo(): high = lax.ppermute(high, axis, backward).reshape(strip)]
  transfers between devices with their start and end apart: 6 -> 6, of which waited for: 3 -> 2; matrix products, arithmetic and copies ran while one was open for 6% -> 5% of each run, Pallas kernels for 0% -> 0%
where the time goes in v6:
time: 116 us
  other arithmetic  48.7 us (42%)
  starting transfers between devices  29 us (25%)
  Pallas kernels  15.9 us (14%)
  waiting for transfers between devices  14.3 us (12%)
  local copies, waits for them, and re-layouts  5.95 us (5%)
  between operations  2.19 us (2%)
    another operation x4, other arithmetic, forces(): return (jnp.stack([total_row, total_col]), kept_sum, exist_sum)  33 us
    pallas_call x1, Pallas kernels, contact_sums(): pl.pallas_call(contact_kernel, out_shape=jax.ShapeDtypeStruct((blocks, 2,...  15.9 us
    all_to_all x1, starting transfers between devices, body(): lax.all_to_all(jnp.broadcast_to(packed[None], (block_count,) + packed.sha...  12.7 us
    all_to_all x1, waiting for transfers between devices, body(): arrived = lax.all_to_all(spread, ('along', 'across'), 0, 0, tiled=True)  10.2 us
    ppermute x2, starting transfers between devices, with_halo(): low = lax.ppermute(low, axis, forward).reshape(strip)  7.24 us
    all_to_all x1, starting transfers between devices, body(): arrived = lax.all_to_all(spread, ('along', 'across'), 0, 0, tiled=True)  5.89 us
    all_to_all x1, waiting for transfers between devices, body(): lax.all_to_all(jnp.broadcast_to(packed[None], (block_count,) + packed.sha...  4.11 us
    ppermute x2, starting transfers between devices, with_halo(): high = lax.ppermute(high, axis, backward).reshape(strip)  3.21 us
  transfers between devices with their start and end apart: 6, of which 2 were waited for; matrix products, arithmetic and copies ran while one was open for 5% of the time, Pallas kernels for 0%

profile of v6, /device:TPU:1, one launch (start us, length us, event | category | flops | bytes accessed | tf_op | source)
XLA Modules:
  0.0 116.1 jit_solution(12842211177956617539)
XLA Ops:
  0.7 1.2 %convert_element_type.417 = f32[2,128,512]{2,1,0:T(8,128)S(1)} convert(s32[2,128,512]{2,1,0:T(8,128)} %param.7) | non-fusion elementwise | flops 131072 | bytes 1048576 | tf_op jit(solution)/shard_map/convert_element_type | solution.py:171
  1.8 0.8 pad_maximum_fusion.18
  2.7 4.9 %collective-permute-start = (f32[6,6,512]{2,1,0:T(8,128)S(1)}, f32[6,6,512]{2,1,0:T(8,128)S(1)}, u32[]{:S(2)}, u32[]{:S(2)}) collective-permute-start(f32[6,6,512]{2,1,0:T(8,128)S(1)} %get-tuple-element.86), channel_id=1, source_target_pairs={{0,8},{8,16},{16,24},{24,32},{32,40},{40,48},{48,56},{56,64},{64,7... | collective-permute-start | bytes 221192 | tf_op jit(solution)/shard_map/ppermute | solution.py:119
  7.6 1.9 %collective-permute-start.1 = (f32[6,6,512]{2,1,0:T(8,128)S(1)}, f32[6,6,512]{2,1,0:T(8,128)S(1)}, u32[]{:S(2)}, u32[]{:S(2)}) collective-permute-start(f32[6,6,512]{2,1,0:T(8,128)S(1)} %get-tuple-element.87), channel_id=1, source_target_pairs={{8,0},{16,8},{24,16},{32,24},{40,32},{48,40},{56,48},{64,56},{72,6... | collective-permute-start | bytes 221192 | tf_op jit(solution)/shard_map/ppermute | solution.py:120
  9.8 0.6 broadcast_in_dim.37
  10.5 12.7 %all-to-all-start = ((f32[32,1,132]{2,1,0:T(1,128)}), f32[32,1,132]{2,1,0:T(1,128)S(1)}, u32[]{:S(2)}, u32[]{:S(2)}) async-start(f32[32,1,132]{2,1,0:T(1,128)} %broadcast_in_dim.37), calls=%async_computation | async-start | bytes 65536 | tf_op jit(solution)/shard_map/all_to_all | solution.py:194
  23.3 0.8 slice_compare_fusion
  24.6 2.3 %collective-permute-start.2 = (f32[5040]{0:T(1024)S(1)}, f32[5040]{0:T(1024)S(1)}, u32[]{:S(2)}, u32[]{:S(2)}) collective-permute-start(f32[5040]{0:T(1024)S(1)} %reshape.652), channel_id=1, source_target_pairs={{0,1},{1,2},{2,3},{3,4},{4,5},{5,6},{6,7},{8,9},{9,10},{10,11},{11... | collective-permute-start | bytes 60488 | tf_op jit(solution)/shard_map/ppermute | solution.py:119
  27.1 1.3 %collective-permute-start.3 = (f32[5040]{0:T(1024)S(1)}, f32[5040]{0:T(1024)S(1)}, u32[]{:S(2)}, u32[]{:S(2)}) collective-permute-start(f32[5040]{0:T(1024)S(1)} %reshape.654), channel_id=1, source_target_pairs={{1,0},{2,1},{3,2},{4,3},{5,4},{6,5},{7,6},{9,8},{10,9},{11,10},{12... | collective-permute-start | bytes 60488 | tf_op jit(solution)/shard_map/ppermute | solution.py:120
  28.5 4.1 %all-to-all-done = f32[32,1,132]{2,1,0:T(1,128)S(1)} async-done(((f32[32,1,132]{2,1,0:T(1,128)}), f32[32,1,132]{2,1,0:T(1,128)S(1)}, u32[]{:S(2)}, u32[]{:S(2)}) %all-to-all-start) | async-done | bytes 16928 | tf_op jit(solution)/shard_map/all_to_all | solution.py:194
  32.6 0.7 copy.41
  33.8 1.9 %pad_maximum_fusion = f32[6,140,524]{2,1,0:T(8,128)S(1)} fusion(f32[6,140,6]{2,1,0:T(8,128)S(1)} %reshape.655, f32[6,6,512]{2,1,0:T(8,128)} %copy-done.6, f32[2,128,512]{2,1,0:T(8,128)S(1)} %convert_element_type.417, f32[2,128,512]{2,1,0:T(8,128)S(1)} %copy-done, f32[2,128,512]{2,1,0:T(8,128)S(1)} %copy-done.1, f32[6,6,512]{2,1,0:T(8,128)} %copy-done.4, ...), kind=kLoop, calls=%fused_computation | loop fusion | flops 2640960 | bytes 3521280 | tf_op jit(solution)/shard_map/concatenate | solution.py:121
  35.9 13.7 %add_bitcast_fusion.1 = (f32[1,134,518]{2,1,0:T(8,128)S(1)}, f32[134,518]{1,0:T(8,128)S(1)}, f32[134,518]{1,0:T(8,128)}, f32[134,518]{1,0:T(8,128)}, f32[134,518...) fusion(f32[6,140,524]{2,1,0:T(8,128)S(1)} %pad_maximum_fusion, ...), kind=kLoop, calls=%fused_computation.267 | loop fusion | flops 33248348 | bytes 33690160 | tf_op jit(solution)/shard_map/stack | solution.py:160
  49.6 6.5 %add_bitcast_fusion = f32[1,134,518]{2,1,0:T(8,128)S(1)} fusion(f32[134,518]{1,0:T(8,128)} %get-tuple-element.83, f32[134,518]{1,0:T(8,128)} %get-tuple-element.82, f32[134,518]{1,0:T(8,128)} %get-tuple-element.81, f32[134,518]{1,0:T(8,128)} %get-tuple-element.80, f32[134,518]{1,0:T(8,128)} %get-tuple-element.79, f32[134,518]{1,0:T(8,128)} %get-tuple-element.78, ...), kind=kLoop, calls=%fused_computation.266 | loop fusion | flops 8537676 | bytes 17214176 | tf_op jit(solution)/shard_map/stack | solution.py:160
  56.2 0.5 fusion
  56.7 0.5 copy-done.2
  57.2 7.4 %add_bitcast_fusion.3 = (f32[1,128,512]{2,1,0:T(8,128)S(1)}, f32[128,512]{1,0:T(8,128)S(1)}, f32[128,512]{1,0:T(8,128)S(1)}, f32[128,512]{1,0:T(8,128)S(1)}, f32...) fusion(f32[2,134,518]{2,1,0:T(8,128)S(1)} %get-tuple-element.51, ...), kind=kLoop, calls=%fused_computation.460 | loop fusion | flops 30081024 | bytes 25952256 | tf_op jit(solution)/shard_map/stack | solution.py:160
  64.6 5.4 %add_bitcast_fusion.2 = f32[1,128,512]{2,1,0:T(8,128)S(1)} fusion(f32[128,512]{1,0:T(8,128)S(1)} %get-tuple-element.50, f32[128,512]{1,0:T(8,128)S(1)} %get-tuple-element.49, f32[128,512]{1,0:T(8,128)S(1)} %get-tuple-element.48, f32[128,512]{1,0:T(8,128)S(1)} %get-tuple-element.47, f32[128,512]{1,0:T(8,128)S(1)} %get-tuple-element.46, ...), kind=kLoop, calls=%fused_computation.459 | loop fusion | flops 21692416 | bytes 20709376 | tf_op jit(solution)/shard_map/stack | solution.py:160
  70.1 1.2 slice_add_fusion.3
  71.5 0.5 slice.1398
  72.0 1.5 %bitcast_add_fusion = (f32[128,512]{1,0:T(8,128)}, f32[128,512]{1,0:T(8,128)}, f32[]{:T(128)}, f32[]{:T(128)}) fusion(f32[2,128,512]{2,1,0:T(8,128)S(1)} %get-tuple-element.32, f32[512]{0:T(512)S(1)} %add_convert_fusion, f32[128]{0:T(128)S(1)} %add_convert_fusion.1), kind=kLoop, calls=%fused_computation.424 | loop fusion | flops 393214 | bytes 1051144 | tf_op jit(solution)/shard_map/add | solution.py:207
  74.8 0.7 copy.43
  75.5 1.2 %pad_add_fusion.meta_ref = s32[33]{0:T(128)} fusion(s32[32]{0:T(128)S(1)} %convert_reduce_fusion, s32[1]{0:T(128)} %bitcast.175), kind=kLoop, calls=%fused_computation.503 | loop fusion | flops 33 | bytes 264 | tf_op jit(solution)/shard_map/concatenate | solution.py:213
  76.7 0.6 pad_maximum_fusion.20.geo_ref
  77.3 15.9 %shard_map.84 = f32[32,2,64,128]{3,2,1,0:T(8,128)} custom-call(s32[33]{0:T(128)} %pad_add_fusion.meta_ref, f32[4]{0:T(128)} %pad_maximum_fusion.20.geo_ref, f32[4096]{0:T(1024)} %bitcast.1127, f32[128,512]{1,0:T(8,128)} %get-tuple-element.89.xr_ref, f32[128,512]{1,0:T(8,128)} %get-tuple-element.88.xc_ref), custom_call_target="tpu_custom_call" | custom-call | tf_op jit(solution)/shard_map/pallas_call | solution.py:100
  93.2 2.2 %reduce_sum.28 = f32[32,2,64]{2,1,0:T(2,128)S(1)} reduce(f32[32,2,64,128]{3,2,1,0:T(8,128)} %shard_map.84, f32[]{:T(128)} %constant.139.clone.1), dimensions={3}, to_apply=%region_5.6 | reduce | flops 520192 | bytes 2113540 | tf_op jit(solution)/shard_map/reduce_sum | solution.py:215
  95.6 0.7 broadcast_in_dim.41
  96.3 5.9 %all-to-all-start.1 = ((f32[256,1,128]{2,1,0:T(1,128)}), f32[256,1,128]{2,1,0:T(1,128)S(1)}, u32[]{:S(2)}, u32[]{:S(2)}) async-start(f32[256,1,128]{2,1,0:T(1,128)} %bitcast.185), calls=%async_computation.1 | async-start | bytes 262144 | tf_op jit(solution)/shard_map/all_to_all | solution.py:220
  102.2 2.7 %divide_subtract_fusion = f32[128,512]{1,0:T(8,128)} fusion(f32[140,524]{1,0:T(8,128)S(1)} %and_convert_fusion, s32[2,128,512]{2,1,0:T(8,128)S(1)} %copy-done.2), kind=kLoop, calls=%fused_computation.458 | loop fusion | flops 11010048 | bytes 8126464 | tf_op jit(solution)/shard_map/sub | solution.py:183
  104.8 10.2 %all-to-all-done.1 = f32[256,1,128]{2,1,0:T(1,128)S(1)} async-done(((f32[256,1,128]{2,1,0:T(1,128)}), f32[256,1,128]{2,1,0:T(1,128)S(1)}, u32[]{:S(2)}, u32[]{:S(2)}) %all-to-all-start.1) | async-done | bytes 131104 | tf_op jit(solution)/shard_map/all_to_all | solution.py:220
  115.0 0.3 reduce_sum.29
  115.4 0.6 copy.46
  (52 shorter events, 2.5 us)
Async XLA Ops:
  0.6 23.5 %copy-start.1 = (f32[2,128,512]{2,1,0:T(8,128)S(1)}, f32[2,128,512]{2,1,0:T(8,128)}, u32[]{:S(2)}) copy-start(f32[2,128,512]{2,1,0:T(8,128)} %param.5) | copy-start | bytes 1572868
  0.6 23.5 %copy-start = (f32[2,128,512]{2,1,0:T(8,128)S(1)}, f32[2,128,512]{2,1,0:T(8,128)}, u32[]{:S(2)}) copy-start(f32[2,128,512]{2,1,0:T(8,128)} %param.6) | copy-start | bytes 1572868
  0.7 8.9 %copy-start.10 = (f32[64,2]{0,1:T(2,128)S(1)}, f32[64,2]{0,1:T(2,128)}, u32[]{:S(2)}) copy-start(f32[64,2]{0,1:T(2,128)} %param.8) | copy-start | bytes 1540
  0.7 9.1 %copy-start.11 = (s32[1,4]{1,0:T(1,128)S(1)}, s32[1,4]{1,0:T(1,128)}, u32[]{:S(2)}) copy-start(s32[1,4]{1,0:T(1,128)} %param.9) | copy-start | bytes 52
  2.7 21.4 %collective-permute-start = (f32[6,6,512]{2,1,0:T(8,128)S(1)}, f32[6,6,512]{2,1,0:T(8,128)S(1)}, u32[]{:S(2)}, u32[]{:S(2)}) collective-permute-start(f32[6,6,512]{2,1,0:T(8,128)S(1)} %get-tuple-element.86), channel_id=1, source_target_pairs={{0,8},{8,16},{16,24},{24,32},{32,40},{40,48},{48,56},{56,64},{64,7... | collective-permute-start | bytes 221192 | tf_op jit(solution)/shard_map/ppermute | solution.py:119
  7.6 16.5 %collective-permute-start.1 = (f32[6,6,512]{2,1,0:T(8,128)S(1)}, f32[6,6,512]{2,1,0:T(8,128)S(1)}, u32[]{:S(2)}, u32[]{:S(2)}) collective-permute-start(f32[6,6,512]{2,1,0:T(8,128)S(1)} %get-tuple-element.87), channel_id=1, source_target_pairs={{8,0},{16,8},{24,16},{32,24},{40,32},{48,40},{56,48},{64,56},{72,6... | collective-permute-start | bytes 221192 | tf_op jit(solution)/shard_map/ppermute | solution.py:120
  10.5 22.1 %all-to-all-start = ((f32[32,1,132]{2,1,0:T(1,128)}), f32[32,1,132]{2,1,0:T(1,128)S(1)}, u32[]{:S(2)}, u32[]{:S(2)}) async-start(f32[32,1,132]{2,1,0:T(1,128)} %broadcast_in_dim.37), calls=%async_computation | async-start | bytes 65536 | tf_op jit(solution)/shard_map/all_to_all | solution.py:194
  24.1 9.2 %copy-start.4 = (f32[6,6,512]{2,1,0:T(8,128)}, f32[6,6,512]{2,1,0:T(8,128)S(1)}, u32[]{:S(2)}) copy-start(f32[6,6,512]{2,1,0:T(8,128)S(1)} %collective-permute-done) | copy-start | bytes 221188
  24.1 9.2 %copy-start.6 = (f32[6,6,512]{2,1,0:T(8,128)}, f32[6,6,512]{2,1,0:T(8,128)S(1)}, u32[]{:S(2)}) copy-start(f32[6,6,512]{2,1,0:T(8,128)S(1)} %collective-permute-done.1) | copy-start | bytes 221188
  24.6 8.7 %collective-permute-start.2 = (f32[5040]{0:T(1024)S(1)}, f32[5040]{0:T(1024)S(1)}, u32[]{:S(2)}, u32[]{:S(2)}) collective-permute-start(f32[5040]{0:T(1024)S(1)} %reshape.652), channel_id=1, source_target_pairs={{0,1},{1,2},{2,3},{3,4},{4,5},{5,6},{6,7},{8,9},{9,10},{10,11},{11... | collective-permute-start | bytes 60488 | tf_op jit(solution)/shard_map/ppermute | solution.py:119
  27.1 6.4 %collective-permute-start.3 = (f32[5040]{0:T(1024)S(1)}, f32[5040]{0:T(1024)S(1)}, u32[]{:S(2)}, u32[]{:S(2)}) collective-permute-start(f32[5040]{0:T(1024)S(1)} %reshape.654), channel_id=1, source_target_pairs={{1,0},{2,1},{3,2},{4,3},{5,4},{6,5},{7,6},{9,8},{10,9},{11,10},{12... | collective-permute-start | bytes 60488 | tf_op jit(solution)/shard_map/ppermute | solution.py:120
  33.7 2.2 %copy-start.5 = (f32[6,6,512]{2,1,0:T(8,128)S(1)}, f32[6,6,512]{2,1,0:T(8,128)}, u32[]{:S(2)}) copy-start(f32[6,6,512]{2,1,0:T(8,128)} %copy-done.4) | copy-start | bytes 221188
  33.7 2.2 %copy-start.7 = (f32[6,6,512]{2,1,0:T(8,128)S(1)}, f32[6,6,512]{2,1,0:T(8,128)}, u32[]{:S(2)}) copy-start(f32[6,6,512]{2,1,0:T(8,128)} %copy-done.6) | copy-start | bytes 221188
  49.6 6.6 %copy-start.8 = (pred[134,518]{1,0:T(8,128)(4,1)S(1)}, pred[134,518]{1,0:T(8,128)(4,1)}, u32[]{:S(2)}) copy-start(pred[134,518]{1,0:T(8,128)(4,1)} %slice_compare_fusion) | copy-start | bytes 208240
  56.1 1.0 copy-start.2
  70.0 1.2 %copy-start.9 = (f32[32,1,132]{0,2,1:T(8,128)S(1)}, f32[32,1,132]{0,2,1:T(8,128)}, u32[]{:S(2)}) copy-start(f32[32,1,132]{0,2,1:T(8,128)} %copy.41) | copy-start | bytes 50692
  71.2 24.2 %copy-start.3 = (f32[2,128,512]{2,1,0:T(8,128)}, f32[2,128,512]{2,1,0:T(8,128)S(1)}, u32[]{:S(2)}) copy-start(f32[2,128,512]{2,1,0:T(8,128)S(1)} %get-tuple-element.32) | copy-start | bytes 1572868
  96.3 18.8 %all-to-all-start.1 = ((f32[256,1,128]{2,1,0:T(1,128)}), f32[256,1,128]{2,1,0:T(1,128)S(1)}, u32[]{:S(2)}, u32[]{:S(2)}) async-start(f32[256,1,128]{2,1,0:T(1,128)} %bitcast.185), calls=%async_computation.1 | async-start | bytes 262144 | tf_op jit(solution)/shard_map/all_to_all | solution.py:220

commit v7 on v6

--- a/solution.py
+++ b/solution.py
@@ -11,14 +11,16 @@
 offsets = [(rr, cc) for rr in range(-3, 4) for cc in range(-3, 4) if 0 < rr * rr + cc * cc <= 9]
 
 
-def contact_kernel(meta_ref, geo_ref, pos_ref, xr_ref, xc_ref, out_ref):
+def contact_kernel(geo_ref, pos_ref, xr_ref, xc_ref, out_ref):
     out_ref[...] = jnp.zeros_like(out_ref)
     blocks, _, panels, _ = out_ref.shape
     rows, cols = xr_ref.shape
     row_tiles = rows // 8
     col_tiles = cols // 128
     reach_row, reach_col = geo_ref[0], geo_ref[1]
-    row_base, col_base = geo_ref[2], geo_ref[3]
+    row_base, col_base, my_tile = geo_ref[2], geo_ref[3], geo_ref[4]
+    stride = pos_ref.shape[0] // blocks
+    listing = stride - 2 * panels
 
     def window(centre, base, reach, size, group):
         local = centre - base
@@ -41,13 +43,10 @@
 
     zero = jnp.zeros((8, 128), jnp.float32)
 
-    def per_block_narrow(k, carry):
-        block = meta_ref[1 + k]
-
+    def per_block_narrow(block):
         def per_panel(j, carry):
-            slot = block * panels + j
-            centre_row = pos_ref[2 * slot]
-            centre_col = pos_ref[2 * slot + 1]
+            centre_row = pos_ref[block * stride + 2 * j]
+            centre_col = pos_ref[block * stride + 2 * j + 1]
             first_row, _ = window(centre_row, row_base, reach_row, rows, 8)
             first_col, _ = window(centre_col, col_base, reach_col, cols, 128)
             first_row = jnp.minimum(first_row, row_tiles - 2)
@@ -59,15 +58,12 @@
             store(block, j, accs)
             return carry
 
-        return lax.fori_loop(0, panels, per_panel, carry, unroll=4)
-
-    def per_block_wide(k, carry):
-        block = meta_ref[1 + k]
-
+        lax.fori_loop(0, panels, per_panel, 0, unroll=8)
+
+    def per_block_wide(block):
         def per_panel(j, carry):
-            slot = block * panels + j
-            centre_row = pos_ref[2 * slot]
-            centre_col = pos_ref[2 * slot + 1]
+            centre_row = pos_ref[block * stride + 2 * j]
+            centre_col = pos_ref[block * stride + 2 * j + 1]
             first_row, row_groups = window(centre_row, row_base, reach_row, rows, 8)
             first_col, col_groups = window(centre_col, col_base, reach_col, cols, 128)
 
@@ -80,29 +76,38 @@
             store(block, j, lax.fori_loop(0, row_groups, per_row, (zero, zero)))
             return carry
 
-        return lax.fori_loop(0, panels, per_panel, carry)
+        lax.fori_loop(0, panels, per_panel, 0)
 
     narrow = (reach_row < 4.0) & (reach_col < 4.0)
 
-    @pl.when(narrow)
-    def _():
-        lax.fori_loop(0, meta_ref[0], per_block_narrow, 0)
-
-    @pl.when(jnp.logical_not(narrow))
-    def _():
-        lax.fori_loop(0, meta_ref[0], per_block_wide, 0)
-
-
-def contact_sums(meta, geometry, positions, rows_x, cols_x):
-    blocks = meta.shape[0] - 1
+    def per_block(block, carry):
+        listed = pos_ref[block * stride + 2 * panels] == my_tile
+        for slot in range(1, listing):
+            listed = listed | (pos_ref[block * stride + 2 * panels + slot] == my_tile)
+
+        @pl.when(listed & narrow)
+        def _():
+            per_block_narrow(block)
+
+        @pl.when(listed & jnp.logical_not(narrow))
+        def _():
+            per_block_wide(block)
+
+        return carry
+
+    lax.fori_loop(0, blocks, per_block, 0)
+
+
+def contact_sums(geometry, gathered, rows_x, cols_x):
+    blocks = gathered.shape[0]
     smem = pl.BlockSpec(memory_space=pltpu.SMEM)
     vmem = pl.BlockSpec(memory_space=pltpu.VMEM)
     return pl.pallas_call(
         contact_kernel,
         out_shape=jax.ShapeDtypeStruct((blocks, 2, PAN_DEV, 128), jnp.float32),
-        in_specs=[smem, smem, smem, vmem, vmem],
+        in_specs=[smem, smem, vmem, vmem],
         out_specs=vmem,
-    )(meta, geometry, positions, rows_x, cols_x)
+    )(geometry, gathered.reshape(-1), rows_x, cols_x)
 
 
 def with_halo(block, sides, width):
@@ -195,23 +200,21 @@
         jnp.broadcast_to(packed[None], (block_count,) + packed.shape), "along", 0, 0, tiled=True
     ).reshape(block_count, -1)
     gathered, state_u = lax.optimization_barrier((gathered, state_u))
-    all_pos = gathered[:, : 2 * PAN_DEV].reshape(block_count, PAN_DEV, 2)
-    all_lists = gathered[:, 2 * PAN_DEV :].astype(jnp.int32)
     my_tile = lax.axis_index("along") * across_count + lax.axis_index("across")
-    listed = jnp.any(all_lists == my_tile, axis=1).astype(jnp.int32)
-    prefix = jnp.cumsum(listed)
-    n_listed = prefix[-1]
-    slots = jnp.arange(block_count, dtype=jnp.int32)
-    listed_blocks = jnp.sum((prefix[None, :] <= slots[:, None]).astype(jnp.int32), axis=1)
     rows_x = (row_base + jnp.arange(rows, dtype=jnp.int32)).astype(jnp.float32)[:, None] + state_u[0]
     cols_x = (col_base + jnp.arange(cols, dtype=jnp.int32)).astype(jnp.float32)[None, :] + state_u[1]
     reach_row = 2.5 + jnp.max(jnp.abs(state_u[0]))
     reach_col = 2.5 + jnp.max(jnp.abs(state_u[1]))
     geometry = jnp.stack(
-        [reach_row, reach_col, row_base.astype(jnp.float32), col_base.astype(jnp.float32)]
-    )
-    meta = jnp.concatenate([n_listed[None], listed_blocks])
-    sums = contact_sums(meta, geometry, all_pos.reshape(-1), rows_x, cols_x)
+        [
+            reach_row,
+            reach_col,
+            row_base.astype(jnp.float32),
+            col_base.astype(jnp.float32),
+            my_tile.astype(jnp.float32),
+        ]
+    )
+    sums = contact_sums(geometry, gathered, rows_x, cols_x)
     partials = jnp.transpose(jnp.sum(sums, axis=-1), (0, 2, 1))
     spread = jnp.broadcast_to(
         partials.reshape(block_count, 1, 1, 2 * PAN_DEV),

time: 116 us -> 113 us (0.974); the launches traced: 116 us -> 111 us
  Pallas kernels: 15.9 us -> 5.1 us
  starting transfers between devices: 29 us -> 37 us
    pallas_call x1, Pallas kernels: 15.9 us -> 5.1 us  [contact_sums(): pl.pallas_call(contact_kernel, out_shape=jax.ShapeDtypeStruct((blocks, 2,...]
    all_to_all x1, starting transfers between devices: 5.89 us -> 13.9 us  [body(): arrived = lax.all_to_all(spread, ('along', 'across'), 0, 0, tiled=True)]
    reduce_max x0 -> x1, other arithmetic: none -> 1.53 us  [body(): reach_col = 2.5 + jnp.max(jnp.abs(state_u[1]))]
    add x1 -> x0, other arithmetic: 1.46 us -> none  [body(): (col_base + jnp.arange(cols, dtype=jnp.int32)).astype(jnp.float32)[None, :]]
    concatenate x1 -> x0, other arithmetic: 1.22 us -> none  [body(): meta = jnp.concatenate([n_listed[None], listed_blocks])]
    slice x3 -> x0, local copies, waits for them, and re-layouts: 1.2 us -> none  [the longest x2 0.69 us: body(): all_pos = gathered[:, :2 * PAN_DEV].reshape(block_count, PAN_DEV, 2)]
  transfers between devices with their start and end apart: 6 -> 6, of which waited for: 2 -> 3; matrix products, arithmetic and copies ran while one was open for 5% -> 6% of each run, Pallas kernels for 0% -> 0%
where the time goes in v7:
time: 113 us; the launch traced here: 111 us
  other arithmetic  47.7 us (42%)
  starting transfers between devices  37 us (33%)
  waiting for transfers between devices  13.4 us (12%)
  local copies, waits for them, and re-layouts  5.34 us (5%)
  Pallas kernels  5.1 us (5%)
  between operations  2.19 us (2%)
    another operation x4, other arithmetic, forces(): return (jnp.stack([total_row, total_col]), kept_sum, exist_sum)  33 us
    all_to_all x1, starting transfers between devices, body(): arrived = lax.all_to_all(spread, ('along', 'across'), 0, 0, tiled=True)  13.9 us
    all_to_all x1, starting transfers between devices, body(): lax.all_to_all(jnp.broadcast_to(packed[None], (block_count,) + packed.sha...  12.7 us
    all_to_all x1, waiting for transfers between devices, body(): arrived = lax.all_to_all(spread, ('along', 'across'), 0, 0, tiled=True)  10.1 us
    ppermute x2, starting transfers between devices, with_halo(): low = lax.ppermute(low, axis, forward).reshape(strip)  7.24 us
    pallas_call x1, Pallas kernels, contact_sums(): pl.pallas_call(contact_kernel, out_shape=jax.ShapeDtypeStruct((blocks, 2,...  5.1 us
    ppermute x2, starting transfers between devices, with_halo(): high = lax.ppermute(high, axis, backward).reshape(strip)  3.21 us
    all_to_all x1, waiting for transfers between devices, body(): lax.all_to_all(jnp.broadcast_to(packed[None], (block_count,) + packed.sha...  3.04 us
  transfers between devices with their start and end apart: 6, of which 3 were waited for; matrix products, arithmetic and copies ran while one was open for 6% of the time, Pallas kernels for 0%

profile of v7, /device:TPU:1, one launch (start us, length us, event | category | flops | bytes accessed | tf_op | source)
XLA Modules:
  0.0 110.8 jit_solution(17510114506857493336)
XLA Ops:
  0.7 1.2 %convert_element_type.401 = f32[2,128,512]{2,1,0:T(8,128)S(1)} convert(s32[2,128,512]{2,1,0:T(8,128)} %param.7) | non-fusion elementwise | flops 131072 | bytes 1048576 | tf_op jit(solution)/shard_map/convert_element_type | solution.py:176
  1.8 0.8 pad_maximum_fusion.18
  2.7 4.9 %collective-permute-start = (f32[6,6,512]{2,1,0:T(8,128)S(1)}, f32[6,6,512]{2,1,0:T(8,128)S(1)}, u32[]{:S(2)}, u32[]{:S(2)}) collective-permute-start(f32[6,6,512]{2,1,0:T(8,128)S(1)} %get-tuple-element.70), channel_id=1, source_target_pairs={{0,8},{8,16},{16,24},{24,32},{32,40},{40,48},{48,56},{56,64},{64,7... | collective-permute-start | bytes 221192 | tf_op jit(solution)/shard_map/ppermute | solution.py:124
  7.6 1.9 %collective-permute-start.1 = (f32[6,6,512]{2,1,0:T(8,128)S(1)}, f32[6,6,512]{2,1,0:T(8,128)S(1)}, u32[]{:S(2)}, u32[]{:S(2)}) collective-permute-start(f32[6,6,512]{2,1,0:T(8,128)S(1)} %get-tuple-element.71), channel_id=1, source_target_pairs={{8,0},{16,8},{24,16},{32,24},{40,32},{48,40},{56,48},{64,56},{72,6... | collective-permute-start | bytes 221192 | tf_op jit(solution)/shard_map/ppermute | solution.py:125
  9.8 0.6 broadcast_in_dim.35
  10.5 12.7 %all-to-all-start = ((f32[32,1,132]{2,1,0:T(1,128)}), f32[32,1,132]{2,1,0:T(1,128)S(1)}, u32[]{:S(2)}, u32[]{:S(2)}) async-start(f32[32,1,132]{2,1,0:T(1,128)} %broadcast_in_dim.35), calls=%async_computation | async-start | bytes 65536 | tf_op jit(solution)/shard_map/all_to_all | solution.py:199
  23.3 0.8 slice_compare_fusion
  24.1 0.6 add_convert_fusion
  25.2 2.3 %collective-permute-start.2 = (f32[5040]{0:T(1024)S(1)}, f32[5040]{0:T(1024)S(1)}, u32[]{:S(2)}, u32[]{:S(2)}) collective-permute-start(f32[5040]{0:T(1024)S(1)} %reshape.641), channel_id=1, source_target_pairs={{0,1},{1,2},{2,3},{3,4},{4,5},{5,6},{6,7},{8,9},{9,10},{10,11},{11... | collective-permute-start | bytes 60488 | tf_op jit(solution)/shard_map/ppermute | solution.py:124
  27.7 1.3 %collective-permute-start.3 = (f32[5040]{0:T(1024)S(1)}, f32[5040]{0:T(1024)S(1)}, u32[]{:S(2)}, u32[]{:S(2)}) collective-permute-start(f32[5040]{0:T(1024)S(1)} %reshape.643), channel_id=1, source_target_pairs={{1,0},{2,1},{3,2},{4,3},{5,4},{6,5},{7,6},{9,8},{10,9},{11,10},{12... | collective-permute-start | bytes 60488 | tf_op jit(solution)/shard_map/ppermute | solution.py:125
  29.0 0.5 add_convert_fusion.1
  29.5 3.0 %all-to-all-done = f32[32,1,132]{2,1,0:T(1,128)S(1)} async-done(((f32[32,1,132]{2,1,0:T(1,128)}), f32[32,1,132]{2,1,0:T(1,128)S(1)}, u32[]{:S(2)}, u32[]{:S(2)}) %all-to-all-start) | async-done | bytes 16928 | tf_op jit(solution)/shard_map/all_to_all | solution.py:199
  32.8 0.3 collective-permute-done.3
  33.3 1.9 %pad_maximum_fusion = f32[6,140,524]{2,1,0:T(8,128)S(1)} fusion(f32[6,140,6]{2,1,0:T(8,128)S(1)} %reshape.644, f32[6,6,512]{2,1,0:T(8,128)} %copy-done.6, f32[2,128,512]{2,1,0:T(8,128)S(1)} %convert_element_type.401, f32[2,128,512]{2,1,0:T(8,128)S(1)} %copy-done, f32[2,128,512]{2,1,0:T(8,128)S(1)} %copy-done.1, f32[6,6,512]{2,1,0:T(8,128)} %copy-done.4, ...), kind=kLoop, calls=%fused_computation | loop fusion | flops 2640960 | bytes 3521280 | tf_op jit(solution)/shard_map/concatenate | solution.py:126
  35.5 13.7 %add_bitcast_fusion.1 = (f32[1,134,518]{2,1,0:T(8,128)S(1)}, f32[134,518]{1,0:T(8,128)S(1)}, f32[134,518]{1,0:T(8,128)}, f32[134,518]{1,0:T(8,128)}, f32[134,518...) fusion(f32[6,140,524]{2,1,0:T(8,128)S(1)} %pad_maximum_fusion, ...), kind=kLoop, calls=%fused_computation.267 | loop fusion | flops 33248348 | bytes 33690160 | tf_op jit(solution)/shard_map/stack | solution.py:165
  49.2 6.5 %add_bitcast_fusion = f32[1,134,518]{2,1,0:T(8,128)S(1)} fusion(f32[134,518]{1,0:T(8,128)} %get-tuple-element.67, f32[134,518]{1,0:T(8,128)} %get-tuple-element.66, f32[134,518]{1,0:T(8,128)} %get-tuple-element.65, f32[134,518]{1,0:T(8,128)} %get-tuple-element.64, f32[134,518]{1,0:T(8,128)} %get-tuple-element.63, f32[134,518]{1,0:T(8,128)} %get-tuple-element.62, ...), kind=kLoop, calls=%fused_computation.266 | loop fusion | flops 8537676 | bytes 17214176 | tf_op jit(solution)/shard_map/stack | solution.py:165
  55.7 0.5 fusion
  56.2 0.5 copy-done.2
  56.7 7.4 %add_bitcast_fusion.3 = (f32[1,128,512]{2,1,0:T(8,128)S(1)}, f32[128,512]{1,0:T(8,128)S(1)}, f32[128,512]{1,0:T(8,128)S(1)}, f32[128,512]{1,0:T(8,128)S(1)}, f32...) fusion(f32[2,134,518]{2,1,0:T(8,128)S(1)} %get-tuple-element.35, ...), kind=kLoop, calls=%fused_computation.460 | loop fusion | flops 30081024 | bytes 25952256 | tf_op jit(solution)/shard_map/stack | solution.py:165
  64.1 5.4 %add_bitcast_fusion.2 = f32[1,128,512]{2,1,0:T(8,128)S(1)} fusion(f32[128,512]{1,0:T(8,128)S(1)} %get-tuple-element.34, f32[128,512]{1,0:T(8,128)S(1)} %get-tuple-element.33, f32[128,512]{1,0:T(8,128)S(1)} %get-tuple-element.32, f32[128,512]{1,0:T(8,128)S(1)} %get-tuple-element.31, f32[128,512]{1,0:T(8,128)S(1)} %get-tuple-element.30, ...), kind=kLoop, calls=%fused_computation.459 | loop fusion | flops 21692416 | bytes 20709376 | tf_op jit(solution)/shard_map/stack | solution.py:165
  69.6 1.2 %slice_add_fusion.3 = (f32[2,128,512]{2,1,0:T(8,128)S(1)}, f32[2,128,512]{2,1,0:T(8,128)}) fusion(f32[2,134,518]{2,1,0:T(8,128)S(1)} %get-tuple-element.35, f32[1,128,512]{2,1,0:T(8,128)S(1)} %add_bitcast_fusion.2, f32[1,128,512]{2,1,0:T(8,128)S(1)} %get-tuple-element.24, f32[2,134,518]{2,1,0:T(8,128)S(1)} %get-tuple-element.36), kind=kLoop, calls=%fused_computation.7 | loop fusion | flops 655360 | bytes 2621440 | tf_op jit(solution)/shard_map/add | solution.py:194
  70.8 1.5 %fusion.259 = (f32[]{:T(128)}, f32[]{:T(128)}, f32[128,512]{1,0:T(8,128)}, f32[128,512]{1,0:T(8,128)}) fusion(f32[2,128,512]{2,1,0:T(8,128)S(1)} %get-tuple-element.16, f32[512]{0:T(512)S(1)} %copy-done.9, f32[128]{0:T(128)S(1)} %copy-done.11), kind=kLoop, calls=%fused_computation.426 | loop fusion | flops 393214 | bytes 1051144 | tf_op jit(solution)/shard_map/reduce_max | solution.py:207
  73.5 0.7 reshape.645.pos_ref
  74.2 0.7 stack.47.geo_ref
  74.9 5.1 %shard_map.84 = f32[32,2,64,128]{3,2,1,0:T(8,128)} custom-call(f32[5]{0:T(128)} %stack.47.geo_ref, f32[4224]{0:T(1024)} %reshape.645.pos_ref, f32[128,512]{1,0:T(8,128)} %get-tuple-element.73.xr_ref, f32[128,512]{1,0:T(8,128)} %get-tuple-element.72.xc_ref), custom_call_target="tpu_custom_call" | custom-call | tf_op jit(solution)/shard_map/pallas_call | solution.py:105
  80.0 2.2 %reduce_sum.18 = f32[32,2,64]{2,1,0:T(2,128)S(1)} reduce(f32[32,2,64,128]{3,2,1,0:T(8,128)} %shard_map.84, f32[]{:T(128)} %constant.134.clone.1), dimensions={3}, to_apply=%region_2.3 | reduce | flops 520192 | bytes 2113540 | tf_op jit(solution)/shard_map/reduce_sum | solution.py:218
  82.4 0.7 broadcast_in_dim.39
  83.1 13.9 %all-to-all-start.1 = ((f32[256,1,128]{2,1,0:T(1,128)}), f32[256,1,128]{2,1,0:T(1,128)S(1)}, u32[]{:S(2)}, u32[]{:S(2)}) async-start(f32[256,1,128]{2,1,0:T(1,128)} %bitcast.182), calls=%async_computation.1 | async-start | bytes 262144 | tf_op jit(solution)/shard_map/all_to_all | solution.py:223
  97.0 2.7 %divide_subtract_fusion = f32[128,512]{1,0:T(8,128)} fusion(f32[140,524]{1,0:T(8,128)S(1)} %and_convert_fusion, s32[2,128,512]{2,1,0:T(8,128)S(1)} %copy-done.2), kind=kLoop, calls=%fused_computation.458 | loop fusion | flops 11010048 | bytes 8126464 | tf_op jit(solution)/shard_map/sub | solution.py:188
  99.6 10.1 %all-to-all-done.1 = f32[256,1,128]{2,1,0:T(1,128)S(1)} async-done(((f32[256,1,128]{2,1,0:T(1,128)}), f32[256,1,128]{2,1,0:T(1,128)S(1)}, u32[]{:S(2)}, u32[]{:S(2)}) %all-to-all-start.1) | async-done | bytes 131104 | tf_op jit(solution)/shard_map/all_to_all | solution.py:223
  109.7 0.3 reduce_sum.19
  110.1 0.6 copy.17
  (45 shorter events, 2.1 us)
Async XLA Ops:
  0.6 24.0 %copy-start.1 = (f32[2,128,512]{2,1,0:T(8,128)S(1)}, f32[2,128,512]{2,1,0:T(8,128)}, u32[]{:S(2)}) copy-start(f32[2,128,512]{2,1,0:T(8,128)} %param.5) | copy-start | bytes 1572868
  0.6 24.0 %copy-start = (f32[2,128,512]{2,1,0:T(8,128)S(1)}, f32[2,128,512]{2,1,0:T(8,128)}, u32[]{:S(2)}) copy-start(f32[2,128,512]{2,1,0:T(8,128)} %param.6) | copy-start | bytes 1572868
  0.7 8.9 %copy-start.10 = (f32[64,2]{0,1:T(2,128)S(1)}, f32[64,2]{0,1:T(2,128)}, u32[]{:S(2)}) copy-start(f32[64,2]{0,1:T(2,128)} %param.8) | copy-start | bytes 1540
  0.7 9.1 %copy-start.12 = (s32[1,4]{1,0:T(1,128)S(1)}, s32[1,4]{1,0:T(1,128)}, u32[]{:S(2)}) copy-start(s32[1,4]{1,0:T(1,128)} %param.9) | copy-start | bytes 52
  2.7 22.0 %collective-permute-start = (f32[6,6,512]{2,1,0:T(8,128)S(1)}, f32[6,6,512]{2,1,0:T(8,128)S(1)}, u32[]{:S(2)}, u32[]{:S(2)}) collective-permute-start(f32[6,6,512]{2,1,0:T(8,128)S(1)} %get-tuple-element.70), channel_id=1, source_target_pairs={{0,8},{8,16},{16,24},{24,32},{32,40},{40,48},{48,56},{56,64},{64,7... | collective-permute-start | bytes 221192 | tf_op jit(solution)/shard_map/ppermute | solution.py:124
  7.6 17.1 %collective-permute-start.1 = (f32[6,6,512]{2,1,0:T(8,128)S(1)}, f32[6,6,512]{2,1,0:T(8,128)S(1)}, u32[]{:S(2)}, u32[]{:S(2)}) collective-permute-start(f32[6,6,512]{2,1,0:T(8,128)S(1)} %get-tuple-element.71), channel_id=1, source_target_pairs={{8,0},{16,8},{24,16},{32,24},{40,32},{48,40},{56,48},{64,56},{72,6... | collective-permute-start | bytes 221192 | tf_op jit(solution)/shard_map/ppermute | solution.py:125
  10.5 22.1 %all-to-all-start = ((f32[32,1,132]{2,1,0:T(1,128)}), f32[32,1,132]{2,1,0:T(1,128)S(1)}, u32[]{:S(2)}, u32[]{:S(2)}) async-start(f32[32,1,132]{2,1,0:T(1,128)} %broadcast_in_dim.35), calls=%async_computation | async-start | bytes 65536 | tf_op jit(solution)/shard_map/all_to_all | solution.py:199
  24.7 7.9 %copy-start.4 = (f32[6,6,512]{2,1,0:T(8,128)}, f32[6,6,512]{2,1,0:T(8,128)S(1)}, u32[]{:S(2)}) copy-start(f32[6,6,512]{2,1,0:T(8,128)S(1)} %collective-permute-done) | copy-start | bytes 221188
  24.7 7.9 %copy-start.6 = (f32[6,6,512]{2,1,0:T(8,128)}, f32[6,6,512]{2,1,0:T(8,128)S(1)}, u32[]{:S(2)}) copy-start(f32[6,6,512]{2,1,0:T(8,128)S(1)} %collective-permute-done.1) | copy-start | bytes 221188
  25.2 7.4 %collective-permute-start.2 = (f32[5040]{0:T(1024)S(1)}, f32[5040]{0:T(1024)S(1)}, u32[]{:S(2)}, u32[]{:S(2)}) collective-permute-start(f32[5040]{0:T(1024)S(1)} %reshape.641), channel_id=1, source_target_pairs={{0,1},{1,2},{2,3},{3,4},{4,5},{5,6},{6,7},{8,9},{9,10},{10,11},{11... | collective-permute-start | bytes 60488 | tf_op jit(solution)/shard_map/ppermute | solution.py:124
  27.7 5.4 %collective-permute-start.3 = (f32[5040]{0:T(1024)S(1)}, f32[5040]{0:T(1024)S(1)}, u32[]{:S(2)}, u32[]{:S(2)}) collective-permute-start(f32[5040]{0:T(1024)S(1)} %reshape.643), channel_id=1, source_target_pairs={{1,0},{2,1},{3,2},{4,3},{5,4},{6,5},{7,6},{9,8},{10,9},{11,10},{12... | collective-permute-start | bytes 60488 | tf_op jit(solution)/shard_map/ppermute | solution.py:125
  33.3 2.2 %copy-start.5 = (f32[6,6,512]{2,1,0:T(8,128)S(1)}, f32[6,6,512]{2,1,0:T(8,128)}, u32[]{:S(2)}) copy-start(f32[6,6,512]{2,1,0:T(8,128)} %copy-done.4) | copy-start | bytes 221188
  33.3 2.2 %copy-start.7 = (f32[6,6,512]{2,1,0:T(8,128)S(1)}, f32[6,6,512]{2,1,0:T(8,128)}, u32[]{:S(2)}) copy-start(f32[6,6,512]{2,1,0:T(8,128)} %copy-done.6) | copy-start | bytes 221188
  49.2 6.6 %copy-start.8 = (pred[134,518]{1,0:T(8,128)(4,1)S(1)}, pred[134,518]{1,0:T(8,128)(4,1)}, u32[]{:S(2)}) copy-start(pred[134,518]{1,0:T(8,128)(4,1)} %slice_compare_fusion) | copy-start | bytes 208240
  55.7 1.0 copy-start.2
  69.6 1.2 %copy-start.9 = (f32[512]{0:T(512)S(1)}, f32[512]{0:T(512)}, u32[]{:S(2)}) copy-start(f32[512]{0:T(512)} %add_convert_fusion) | copy-start | bytes 6148
  69.6 1.2 %copy-start.11 = (f32[128]{0:T(128)S(1)}, f32[128]{0:T(128)}, u32[]{:S(2)}) copy-start(f32[128]{0:T(128)} %add_convert_fusion.1) | copy-start | bytes 1540
  70.8 11.5 %copy-start.3 = (f32[2,128,512]{2,1,0:T(8,128)}, f32[2,128,512]{2,1,0:T(8,128)S(1)}, u32[]{:S(2)}) copy-start(f32[2,128,512]{2,1,0:T(8,128)S(1)} %get-tuple-element.16) | copy-start | bytes 1572868
  83.1 26.6 %all-to-all-start.1 = ((f32[256,1,128]{2,1,0:T(1,128)}), f32[256,1,128]{2,1,0:T(1,128)S(1)}, u32[]{:S(2)}, u32[]{:S(2)}) async-start(f32[256,1,128]{2,1,0:T(1,128)} %bitcast.182), calls=%async_computation.1 | async-start | bytes 262144 | tf_op jit(solution)/shard_map/all_to_all | solution.py:223

commit v8 on v7

--- a/solution.py
+++ b/solution.py
@@ -155,9 +155,9 @@
         keep = flag * present
         row_part = row_off + (other[0] - centre[0])
         col_part = col_off + (other[1] - centre[1])
-        length = jnp.sqrt(row_part * row_part + col_part * col_part)
-        rest = float((row_off * row_off + col_off * col_off) ** 0.5)
-        coeff = keep * (length - rest) / (rest * length)
+        inv_length = lax.rsqrt(row_part * row_part + col_part * col_part)
+        inv_rest = 1.0 / float((row_off * row_off + col_off * col_off) ** 0.5)
+        coeff = keep * (inv_rest - inv_length)
         total_row = total_row + coeff * row_part
         total_col = total_col + coeff * col_part
         kept_sum = kept_sum + keep

time: 113 us -> 105 us (0.929); the launches traced: 111 us -> 104 us
  starting transfers between devices: 37 us -> 30.3 us
  other arithmetic: 47.7 us -> 41.4 us
  Pallas kernels: 5.1 us -> 10.3 us
  waiting for transfers between devices: 13.4 us -> 14.8 us
    all_to_all x1, starting transfers between devices: 13.9 us -> 7.17 us  [body(): arrived = lax.all_to_all(spread, ('along', 'across'), 0, 0, tiled=True)]
    pallas_call x1, Pallas kernels: 5.1 us -> 10.3 us  [contact_sums(): pl.pallas_call(contact_kernel, out_shape=jax.ShapeDtypeStruct((blocks, 2,...]
    another operation x4, other arithmetic: 33 us -> 29.3 us  [forces(): return (jnp.stack([total_row, total_col]), kept_sum, exist_sum)]
    all_to_all x1, waiting for transfers between devices: 3.04 us -> 4.74 us  [body(): lax.all_to_all(jnp.broadcast_to(packed[None], (block_count,) + packed.sha...]
  transfers between devices with their start and end apart: 6 -> 6, of which waited for: 3 -> 2; matrix products, arithmetic and copies ran while one was open for 6% -> 5% of each run, Pallas kernels for 0% -> 0%
where the time goes in v8:
time: 105 us; the launch traced here: 104 us
  other arithmetic  41.4 us (39%)
  starting transfers between devices  30.3 us (29%)
  waiting for transfers between devices  14.8 us (14%)
  Pallas kernels  10.3 us (10%)
  local copies, waits for them, and re-layouts  5.26 us (5%)
  between operations  2.25 us (2%)
    another operation x4, other arithmetic, forces(): return (jnp.stack([total_row, total_col]), kept_sum, exist_sum)  29.3 us
    all_to_all x1, starting transfers between devices, body(): lax.all_to_all(jnp.broadcast_to(packed[None], (block_count,) + packed.sha...  12.7 us
    pallas_call x1, Pallas kernels, contact_sums(): pl.pallas_call(contact_kernel, out_shape=jax.ShapeDtypeStruct((blocks, 2,...  10.3 us
    all_to_all x1, waiting for transfers between devices, body(): arrived = lax.all_to_all(spread, ('along', 'across'), 0, 0, tiled=True)  10.1 us
    ppermute x2, starting transfers between devices, with_halo(): low = lax.ppermute(low, axis, forward).reshape(strip)  7.24 us
    all_to_all x1, starting transfers between devices, body(): arrived = lax.all_to_all(spread, ('along', 'across'), 0, 0, tiled=True)  7.17 us
    all_to_all x1, waiting for transfers between devices, body(): lax.all_to_all(jnp.broadcast_to(packed[None], (block_count,) + packed.sha...  4.74 us
    ppermute x2, starting transfers between devices, with_halo(): high = lax.ppermute(high, axis, backward).reshape(strip)  3.21 us
  transfers between devices with their start and end apart: 6, of which 2 were waited for; matrix products, arithmetic and copies ran while one was open for 5% of the time, Pallas kernels for 0%

profile of v8, /device:TPU:1, one launch (start us, length us, event | category | flops | bytes accessed | tf_op | source)
XLA Modules:
  0.0 104.3 jit_solution(10297788973439727203)
XLA Ops:
  0.7 1.2 %convert_element_type.401 = f32[2,128,512]{2,1,0:T(8,128)S(1)} convert(s32[2,128,512]{2,1,0:T(8,128)} %param.7) | non-fusion elementwise | flops 131072 | bytes 1048576 | tf_op jit(solution)/shard_map/convert_element_type | solution.py:176
  1.8 0.8 pad_maximum_fusion.18
  2.7 4.9 %collective-permute-start = (f32[6,6,512]{2,1,0:T(8,128)S(1)}, f32[6,6,512]{2,1,0:T(8,128)S(1)}, u32[]{:S(2)}, u32[]{:S(2)}) collective-permute-start(f32[6,6,512]{2,1,0:T(8,128)S(1)} %get-tuple-element.33), channel_id=1, source_target_pairs={{0,8},{8,16},{16,24},{24,32},{32,40},{40,48},{48,56},{56,64},{64,7... | collective-permute-start | bytes 221192 | tf_op jit(solution)/shard_map/ppermute | solution.py:124
  7.6 1.9 %collective-permute-start.1 = (f32[6,6,512]{2,1,0:T(8,128)S(1)}, f32[6,6,512]{2,1,0:T(8,128)S(1)}, u32[]{:S(2)}, u32[]{:S(2)}) collective-permute-start(f32[6,6,512]{2,1,0:T(8,128)S(1)} %get-tuple-element.34), channel_id=1, source_target_pairs={{8,0},{16,8},{24,16},{32,24},{40,32},{48,40},{56,48},{64,56},{72,6... | collective-permute-start | bytes 221192 | tf_op jit(solution)/shard_map/ppermute | solution.py:125
  9.8 0.6 broadcast_in_dim.35
  10.5 12.7 %all-to-all-start = ((f32[32,1,132]{2,1,0:T(1,128)}), f32[32,1,132]{2,1,0:T(1,128)S(1)}, u32[]{:S(2)}, u32[]{:S(2)}) async-start(f32[32,1,132]{2,1,0:T(1,128)} %broadcast_in_dim.35), calls=%async_computation | async-start | bytes 65536 | tf_op jit(solution)/shard_map/all_to_all | solution.py:199
  23.5 0.2 pad_maximum_fusion.5
  23.7 0.2 reshape.641
  24.0 2.3 %collective-permute-start.2 = (f32[5040]{0:T(1024)S(1)}, f32[5040]{0:T(1024)S(1)}, u32[]{:S(2)}, u32[]{:S(2)}) collective-permute-start(f32[5040]{0:T(1024)S(1)} %reshape.641), channel_id=1, source_target_pairs={{0,1},{1,2},{2,3},{3,4},{4,5},{5,6},{6,7},{8,9},{9,10},{10,11},{11... | collective-permute-start | bytes 60488 | tf_op jit(solution)/shard_map/ppermute | solution.py:124
  26.3 0.2 reshape.643
  26.5 1.3 %collective-permute-start.3 = (f32[5040]{0:T(1024)S(1)}, f32[5040]{0:T(1024)S(1)}, u32[]{:S(2)}, u32[]{:S(2)}) collective-permute-start(f32[5040]{0:T(1024)S(1)} %reshape.643), channel_id=1, source_target_pairs={{1,0},{2,1},{3,2},{4,3},{5,4},{6,5},{7,6},{9,8},{10,9},{11,10},{12... | collective-permute-start | bytes 60488 | tf_op jit(solution)/shard_map/ppermute | solution.py:125
  27.8 4.7 %all-to-all-done = f32[32,1,132]{2,1,0:T(1,128)S(1)} async-done(((f32[32,1,132]{2,1,0:T(1,128)}), f32[32,1,132]{2,1,0:T(1,128)S(1)}, u32[]{:S(2)}, u32[]{:S(2)}) %all-to-all-start) | async-done | bytes 16928 | tf_op jit(solution)/shard_map/all_to_all | solution.py:199
  33.0 0.9 pad_maximum_fusion
  33.9 0.3 slice_convert_fusion
  34.2 9.2 %add_bitcast_fusion.1 = (f32[1,134,518]{2,1,0:T(8,128)S(1)}, f32[134,518]{1,0:T(8,128)S(1)}, f32[134,518]{1,0:T(8,128)S(1)}, f32[134,518]{1,0:T(8,128)S(1)}, f32[134,518]{1,0:T(8,128)S(1)}) fusion(f32[140,524]{1,0:T(8,128)S(1)} %and_convert_fusion, s32[2,134,518]{2,1,0:T(8,128)S(1)} %slice_convert_fusion, f32[6,140,524]{2,1,0:T(8,128)S(1)} %pad_maximum_fusion, ...), kind=kLoop, calls=%fused_computation.239 | loop fusion | flops 29638924 | bytes 26471312 | tf_op jit(solution)/shard_map/stack | solution.py:165
  43.4 8.1 %add_bitcast_fusion = f32[1,134,518]{2,1,0:T(8,128)S(1)} fusion(f32[134,518]{1,0:T(8,128)S(1)} %get-tuple-element.30, f32[134,518]{1,0:T(8,128)S(1)} %get-tuple-element.29, f32[140,524]{1,0:T(8,128)S(1)} %and_convert_fusion, f32[134,518]{1,0:T(8,128)S(1)} %get-tuple-element.28, f32[134,518]{1,0:T(8,128)S(1)} %get-tuple-element.27, ...), kind=kLoop, calls=%fused_computation.238 | loop fusion | flops 27834212 | bytes 24710672 | tf_op jit(solution)/shard_map/stack | solution.py:165
  51.5 0.5 fusion
  52.0 0.5 copy-done.2
  52.5 5.9 %add_bitcast_fusion.3 = f32[1,128,512]{2,1,0:T(8,128)S(1)} fusion(f32[2,134,518]{2,1,0:T(8,128)S(1)} %get-tuple-element.24, f32[140,524]{1,0:T(8,128)S(1)} %and_convert_fusion, s32[2,128,512]{2,1,0:T(8,128)S(1)} %copy-done.2), kind=kLoop, calls=%fused_computation.460 | loop fusion | flops 26673152 | bytes 23330816 | tf_op jit(solution)/shard_map/stack | solution.py:165
  58.5 6.1 %add_bitcast_fusion.2 = f32[1,128,512]{2,1,0:T(8,128)S(1)} fusion(f32[2,134,518]{2,1,0:T(8,128)S(1)} %get-tuple-element.24, f32[140,524]{1,0:T(8,128)S(1)} %and_convert_fusion, s32[2,128,512]{2,1,0:T(8,128)S(1)} %copy-done.2), kind=kLoop, calls=%fused_computation.459 | loop fusion | flops 26673152 | bytes 23330816 | tf_op jit(solution)/shard_map/stack | solution.py:165
  64.6 1.2 %slice_add_fusion.3 = (f32[2,128,512]{2,1,0:T(8,128)S(1)}, f32[2,128,512]{2,1,0:T(8,128)}) fusion(f32[2,134,518]{2,1,0:T(8,128)S(1)} %get-tuple-element.24, f32[1,128,512]{2,1,0:T(8,128)S(1)} %add_bitcast_fusion.2, f32[1,128,512]{2,1,0:T(8,128)S(1)} %add_bitcast_fusion.3, f32[2,134,518]{2,1,0:T(8,128)S(1)} %get-tuple-element.25), kind=kLoop, calls=%fused_computation.7 | loop fusion | flops 655360 | bytes 2621440 | tf_op jit(solution)/shard_map/add | solution.py:194
  65.7 1.5 %fusion.231 = (f32[]{:T(128)}, f32[]{:T(128)}, f32[128,512]{1,0:T(8,128)}, f32[128,512]{1,0:T(8,128)}) fusion(f32[2,128,512]{2,1,0:T(8,128)S(1)} %get-tuple-element.16, f32[512]{0:T(512)S(1)} %add_convert_fusion, f32[128]{0:T(128)S(1)} %add_convert_fusion.1), kind=kLoop, calls=%fused_computation.426 | loop fusion | flops 393214 | bytes 1051144 | tf_op jit(solution)/shard_map/reduce_max | solution.py:207
  68.6 0.7 reshape.645.pos_ref
  69.3 0.6 stack.47.geo_ref
  69.9 10.3 %shard_map.84 = f32[32,2,64,128]{3,2,1,0:T(8,128)} custom-call(f32[5]{0:T(128)} %stack.47.geo_ref, f32[4224]{0:T(1024)} %reshape.645.pos_ref, f32[128,512]{1,0:T(8,128)} %get-tuple-element.36.xr_ref, f32[128,512]{1,0:T(8,128)} %get-tuple-element.35.xc_ref), custom_call_target="tpu_custom_call" | custom-call | tf_op jit(solution)/shard_map/pallas_call | solution.py:105
  80.2 2.2 %reduce_sum.18 = f32[32,2,64]{2,1,0:T(2,128)S(1)} reduce(f32[32,2,64,128]{3,2,1,0:T(8,128)} %shard_map.84, f32[]{:T(128)} %constant.45.clone.1), dimensions={3}, to_apply=%region_2.3 | reduce | flops 520192 | bytes 2113540 | tf_op jit(solution)/shard_map/reduce_sum | solution.py:218
  82.6 0.7 broadcast_in_dim.39
  83.3 7.2 %all-to-all-start.1 = ((f32[256,1,128]{2,1,0:T(1,128)}), f32[256,1,128]{2,1,0:T(1,128)S(1)}, u32[]{:S(2)}, u32[]{:S(2)}) async-start(f32[256,1,128]{2,1,0:T(1,128)} %bitcast.182), calls=%async_computation.1 | async-start | bytes 262144 | tf_op jit(solution)/shard_map/all_to_all | solution.py:223
  90.4 2.7 %divide_subtract_fusion = f32[128,512]{1,0:T(8,128)} fusion(f32[140,524]{1,0:T(8,128)S(1)} %and_convert_fusion, s32[2,128,512]{2,1,0:T(8,128)S(1)} %copy-done.2), kind=kLoop, calls=%fused_computation.458 | loop fusion | flops 11010048 | bytes 8126464 | tf_op jit(solution)/shard_map/sub | solution.py:188
  93.1 10.1 %all-to-all-done.1 = f32[256,1,128]{2,1,0:T(1,128)S(1)} async-done(((f32[256,1,128]{2,1,0:T(1,128)}), f32[256,1,128]{2,1,0:T(1,128)S(1)}, u32[]{:S(2)}, u32[]{:S(2)}) %all-to-all-start.1) | async-done | bytes 131104 | tf_op jit(solution)/shard_map/all_to_all | solution.py:223
  103.2 0.3 reduce_sum.19
  103.6 0.6 copy.17
  (31 shorter events, 1.2 us)
Async XLA Ops:
  0.6 22.9 %copy-start.1 = (f32[2,128,512]{2,1,0:T(8,128)S(1)}, f32[2,128,512]{2,1,0:T(8,128)}, u32[]{:S(2)}) copy-start(f32[2,128,512]{2,1,0:T(8,128)} %param.5) | copy-start | bytes 1572868
  0.6 22.9 %copy-start = (f32[2,128,512]{2,1,0:T(8,128)S(1)}, f32[2,128,512]{2,1,0:T(8,128)}, u32[]{:S(2)}) copy-start(f32[2,128,512]{2,1,0:T(8,128)} %param.6) | copy-start | bytes 1572868
  0.7 8.9 %copy-start.4 = (f32[64,2]{0,1:T(2,128)S(1)}, f32[64,2]{0,1:T(2,128)}, u32[]{:S(2)}) copy-start(f32[64,2]{0,1:T(2,128)} %param.8) | copy-start | bytes 1540
  0.7 9.1 %copy-start.5 = (s32[1,4]{1,0:T(1,128)S(1)}, s32[1,4]{1,0:T(1,128)}, u32[]{:S(2)}) copy-start(s32[1,4]{1,0:T(1,128)} %param.9) | copy-start | bytes 52
  2.7 20.8 %collective-permute-start = (f32[6,6,512]{2,1,0:T(8,128)S(1)}, f32[6,6,512]{2,1,0:T(8,128)S(1)}, u32[]{:S(2)}, u32[]{:S(2)}) collective-permute-start(f32[6,6,512]{2,1,0:T(8,128)S(1)} %get-tuple-element.33), channel_id=1, source_target_pairs={{0,8},{8,16},{16,24},{24,32},{32,40},{40,48},{48,56},{56,64},{64,7... | collective-permute-start | bytes 221192 | tf_op jit(solution)/shard_map/ppermute | solution.py:124
  7.6 15.9 %collective-permute-start.1 = (f32[6,6,512]{2,1,0:T(8,128)S(1)}, f32[6,6,512]{2,1,0:T(8,128)S(1)}, u32[]{:S(2)}, u32[]{:S(2)}) collective-permute-start(f32[6,6,512]{2,1,0:T(8,128)S(1)} %get-tuple-element.34), channel_id=1, source_target_pairs={{8,0},{16,8},{24,16},{32,24},{40,32},{48,40},{56,48},{64,56},{72,6... | collective-permute-start | bytes 221192 | tf_op jit(solution)/shard_map/ppermute | solution.py:125
  10.5 22.1 %all-to-all-start = ((f32[32,1,132]{2,1,0:T(1,128)}), f32[32,1,132]{2,1,0:T(1,128)S(1)}, u32[]{:S(2)}, u32[]{:S(2)}) async-start(f32[32,1,132]{2,1,0:T(1,128)} %broadcast_in_dim.35), calls=%async_computation | async-start | bytes 65536 | tf_op jit(solution)/shard_map/all_to_all | solution.py:199
  24.0 8.6 %collective-permute-start.2 = (f32[5040]{0:T(1024)S(1)}, f32[5040]{0:T(1024)S(1)}, u32[]{:S(2)}, u32[]{:S(2)}) collective-permute-start(f32[5040]{0:T(1024)S(1)} %reshape.641), channel_id=1, source_target_pairs={{0,1},{1,2},{2,3},{3,4},{4,5},{5,6},{6,7},{8,9},{9,10},{10,11},{11... | collective-permute-start | bytes 60488 | tf_op jit(solution)/shard_map/ppermute | solution.py:124
  26.5 6.3 %collective-permute-start.3 = (f32[5040]{0:T(1024)S(1)}, f32[5040]{0:T(1024)S(1)}, u32[]{:S(2)}, u32[]{:S(2)}) collective-permute-start(f32[5040]{0:T(1024)S(1)} %reshape.643), channel_id=1, source_target_pairs={{1,0},{2,1},{3,2},{4,3},{5,4},{6,5},{7,6},{9,8},{10,9},{11,10},{12... | collective-permute-start | bytes 60488 | tf_op jit(solution)/shard_map/ppermute | solution.py:125
  51.5 1.0 %copy-start.2 = (s32[2,128,512]{2,1,0:T(8,128)S(1)}, s32[2,128,512]{2,1,0:T(8,128)}, u32[]{:S(2)}) copy-start(s32[2,128,512]{2,1,0:T(8,128)} %param.7) | copy-start | bytes 1572868
  65.7 16.7 %copy-start.3 = (f32[2,128,512]{2,1,0:T(8,128)}, f32[2,128,512]{2,1,0:T(8,128)S(1)}, u32[]{:S(2)}) copy-start(f32[2,128,512]{2,1,0:T(8,128)S(1)} %get-tuple-element.16) | copy-start | bytes 1572868
  83.3 19.9 %all-to-all-start.1 = ((f32[256,1,128]{2,1,0:T(1,128)}), f32[256,1,128]{2,1,0:T(1,128)S(1)}, u32[]{:S(2)}, u32[]{:S(2)}) async-start(f32[256,1,128]{2,1,0:T(1,128)} %bitcast.182), calls=%async_computation.1 | async-start | bytes 262144 | tf_op jit(solution)/shard_map/all_to_all | solution.py:223

commit v9 on v8

--- a/solution.py
+++ b/solution.py
@@ -13,7 +13,8 @@
 
 def contact_kernel(geo_ref, pos_ref, xr_ref, xc_ref, out_ref):
     out_ref[...] = jnp.zeros_like(out_ref)
-    blocks, _, panels, _ = out_ref.shape
+    blocks = out_ref.shape[0]
+    panels = PAN_DEV
     rows, cols = xr_ref.shape
     row_tiles = rows // 8
     col_tiles = cols // 128
@@ -21,6 +22,7 @@
     row_base, col_base, my_tile = geo_ref[2], geo_ref[3], geo_ref[4]
     stride = pos_ref.shape[0] // blocks
     listing = stride - 2 * panels
+    empty = jnp.zeros((1, 128), jnp.float32)
 
     def window(centre, base, reach, size, group):
         local = centre - base
@@ -37,14 +39,22 @@
         push = 0.5 * jnp.maximum(4.0 - delta_row * delta_row - delta_col * delta_col, 0.0)
         return (accs[0] + push * delta_row, accs[1] + push * delta_col)
 
-    def store(block, j, accs):
-        out_ref[block, 0, pl.ds(j, 1), :] = jnp.sum(accs[0], axis=0, keepdims=True)
-        out_ref[block, 1, pl.ds(j, 1), :] = jnp.sum(accs[1], axis=0, keepdims=True)
+    lane = lax.broadcasted_iota(jnp.int32, (1, 128), 1)
+
+    def place(j, accs, sums):
+        return (
+            jnp.where(lane == j, jnp.sum(accs[0]), sums[0]),
+            jnp.where(lane == j, jnp.sum(accs[1]), sums[1]),
+        )
+
+    def store(block, sums):
+        out_ref[block, pl.ds(0, 1), :] = sums[0]
+        out_ref[block, pl.ds(1, 1), :] = sums[1]
 
     zero = jnp.zeros((8, 128), jnp.float32)
 
     def per_block_narrow(block):
-        def per_panel(j, carry):
+        def per_panel(j, sums):
             centre_row = pos_ref[block * stride + 2 * j]
             centre_col = pos_ref[block * stride + 2 * j + 1]
             first_row, _ = window(centre_row, row_base, reach_row, rows, 8)
@@ -55,13 +65,12 @@
             for r in range(2):
                 for c in range(2):
                     accs = tile_sums(centre_row, centre_col, first_row + r, first_col + c, accs)
-            store(block, j, accs)
-            return carry
-
-        lax.fori_loop(0, panels, per_panel, 0, unroll=8)
+            return place(j, accs, sums)
+
+        store(block, lax.fori_loop(0, panels, per_panel, (empty, empty), unroll=8))
 
     def per_block_wide(block):
-        def per_panel(j, carry):
+        def per_panel(j, sums):
             centre_row = pos_ref[block * stride + 2 * j]
             centre_col = pos_ref[block * stride + 2 * j + 1]
             first_row, row_groups = window(centre_row, row_base, reach_row, rows, 8)
@@ -73,10 +82,9 @@
 
                 return lax.fori_loop(0, col_groups, per_col, accs)
 
-            store(block, j, lax.fori_loop(0, row_groups, per_row, (zero, zero)))
-            return carry
-
-        lax.fori_loop(0, panels, per_panel, 0)
+            return place(j, lax.fori_loop(0, row_groups, per_row, (zero, zero)), sums)
+
+        store(block, lax.fori_loop(0, panels, per_panel, (empty, empty)))
 
     narrow = (reach_row < 4.0) & (reach_col < 4.0)
 
@@ -104,7 +112,7 @@
     vmem = pl.BlockSpec(memory_space=pltpu.VMEM)
     return pl.pallas_call(
         contact_kernel,
-        out_shape=jax.ShapeDtypeStruct((blocks, 2, PAN_DEV, 128), jnp.float32),
+        out_shape=jax.ShapeDtypeStruct((blocks, 2, 128), jnp.float32),
         in_specs=[smem, smem, vmem, vmem],
         out_specs=vmem,
     )(geometry, gathered.reshape(-1), rows_x, cols_x)
@@ -215,7 +223,7 @@
         ]
     )
     sums = contact_sums(geometry, gathered, rows_x, cols_x)
-    partials = jnp.transpose(jnp.sum(sums, axis=-1), (0, 2, 1))
+    partials = jnp.transpose(sums[:, :, :PAN_DEV], (0, 2, 1))
     spread = jnp.broadcast_to(
         partials.reshape(block_count, 1, 1, 2 * PAN_DEV),
         (block_count, across_count, 1, 2 * PAN_DEV),

time: 105 us -> 109 us (1.038); the launches traced: 104 us -> 109 us
  Pallas kernels: 10.3 us -> 15.6 us
  other arithmetic: 41.4 us -> 39.1 us
  starting transfers between devices: 30.3 us -> 31.7 us
    pallas_call x1, Pallas kernels: 10.3 us -> 15.6 us  [contact_sums(): pl.pallas_call(contact_kernel, out_shape=jax.ShapeDtypeStruct((blocks, 2,...]
    reduce_sum x1 -> x0, other arithmetic: 2.22 us -> none  [body(): partials = jnp.transpose(jnp.sum(sums, axis=-1), (0, 2, 1))]
    all_to_all x1, starting transfers between devices: 7.17 us -> 8.53 us  [body(): arrived = lax.all_to_all(spread, ('along', 'across'), 0, 0, tiled=True)]
  transfers between devices with their start and end apart: 6 -> 6, of which waited for: 2 -> 2; matrix products, arithmetic and copies ran while one was open for 5% -> 4% of each run, Pallas kernels for 0% -> 0%
where the time goes in v9:
time: 109 us
  other arithmetic  39.1 us (36%)
  starting transfers between devices  31.7 us (29%)
  Pallas kernels  15.6 us (14%)
  waiting for transfers between devices  14.9 us (14%)
  local copies, waits for them, and re-layouts  5.98 us (5%)
  between operations  2.17 us (2%)
    another operation x4, other arithmetic, forces(): return (jnp.stack([total_row, total_col]), kept_sum, exist_sum)  29.3 us
    pallas_call x1, Pallas kernels, contact_sums(): pl.pallas_call(contact_kernel, out_shape=jax.ShapeDtypeStruct((blocks, 2,...  15.6 us
    all_to_all x1, starting transfers between devices, body(): lax.all_to_all(jnp.broadcast_to(packed[None], (block_count,) + packed.sha...  12.7 us
    all_to_all x1, waiting for transfers between devices, body(): arrived = lax.all_to_all(spread, ('along', 'across'), 0, 0, tiled=True)  10.2 us
    all_to_all x1, starting transfers between devices, body(): arrived = lax.all_to_all(spread, ('along', 'across'), 0, 0, tiled=True)  8.53 us
    ppermute x2, starting transfers between devices, with_halo(): low = lax.ppermute(low, axis, forward).reshape(strip)  7.24 us
    all_to_all x1, waiting for transfers between devices, body(): lax.all_to_all(jnp.broadcast_to(packed[None], (block_count,) + packed.sha...  4.74 us
    ppermute x2, starting transfers between devices, with_halo(): high = lax.ppermute(high, axis, backward).reshape(strip)  3.21 us
  transfers between devices with their start and end apart: 6, of which 2 were waited for; matrix products, arithmetic and copies ran while one was open for 4% of the time, Pallas kernels for 0%

profile of v9, /device:TPU:1, one launch (start us, length us, event | category | flops | bytes accessed | tf_op | source)
XLA Modules:
  0.0 109.5 jit_solution(6527663921999991066)
XLA Ops:
  0.7 1.2 %convert_element_type.401 = f32[2,128,512]{2,1,0:T(8,128)S(1)} convert(s32[2,128,512]{2,1,0:T(8,128)} %param.7) | non-fusion elementwise | flops 131072 | bytes 1048576 | tf_op jit(solution)/shard_map/convert_element_type | solution.py:184
  1.8 0.8 pad_maximum_fusion.18
  2.7 4.9 %collective-permute-start = (f32[6,6,512]{2,1,0:T(8,128)S(1)}, f32[6,6,512]{2,1,0:T(8,128)S(1)}, u32[]{:S(2)}, u32[]{:S(2)}) collective-permute-start(f32[6,6,512]{2,1,0:T(8,128)S(1)} %get-tuple-element.33), channel_id=1, source_target_pairs={{0,8},{8,16},{16,24},{24,32},{32,40},{40,48},{48,56},{56,64},{64,7... | collective-permute-start | bytes 221192 | tf_op jit(solution)/shard_map/ppermute | solution.py:132
  7.6 1.9 %collective-permute-start.1 = (f32[6,6,512]{2,1,0:T(8,128)S(1)}, f32[6,6,512]{2,1,0:T(8,128)S(1)}, u32[]{:S(2)}, u32[]{:S(2)}) collective-permute-start(f32[6,6,512]{2,1,0:T(8,128)S(1)} %get-tuple-element.34), channel_id=1, source_target_pairs={{8,0},{16,8},{24,16},{32,24},{40,32},{48,40},{56,48},{64,56},{72,6... | collective-permute-start | bytes 221192 | tf_op jit(solution)/shard_map/ppermute | solution.py:133
  9.8 0.6 broadcast_in_dim.35
  10.5 12.7 %all-to-all-start = ((f32[32,1,132]{2,1,0:T(1,128)}), f32[32,1,132]{2,1,0:T(1,128)S(1)}, u32[]{:S(2)}, u32[]{:S(2)}) async-start(f32[32,1,132]{2,1,0:T(1,128)} %broadcast_in_dim.35), calls=%async_computation | async-start | bytes 65536 | tf_op jit(solution)/shard_map/all_to_all | solution.py:207
  23.5 0.2 pad_maximum_fusion.5
  23.7 0.2 reshape.641
  24.0 2.3 %collective-permute-start.2 = (f32[5040]{0:T(1024)S(1)}, f32[5040]{0:T(1024)S(1)}, u32[]{:S(2)}, u32[]{:S(2)}) collective-permute-start(f32[5040]{0:T(1024)S(1)} %reshape.641), channel_id=1, source_target_pairs={{0,1},{1,2},{2,3},{3,4},{4,5},{5,6},{6,7},{8,9},{9,10},{10,11},{11... | collective-permute-start | bytes 60488 | tf_op jit(solution)/shard_map/ppermute | solution.py:132
  26.3 0.2 reshape.643
  26.5 1.3 %collective-permute-start.3 = (f32[5040]{0:T(1024)S(1)}, f32[5040]{0:T(1024)S(1)}, u32[]{:S(2)}, u32[]{:S(2)}) collective-permute-start(f32[5040]{0:T(1024)S(1)} %reshape.643), channel_id=1, source_target_pairs={{1,0},{2,1},{3,2},{4,3},{5,4},{6,5},{7,6},{9,8},{10,9},{11,10},{12... | collective-permute-start | bytes 60488 | tf_op jit(solution)/shard_map/ppermute | solution.py:133
  27.8 4.7 %all-to-all-done = f32[32,1,132]{2,1,0:T(1,128)S(1)} async-done(((f32[32,1,132]{2,1,0:T(1,128)}), f32[32,1,132]{2,1,0:T(1,128)S(1)}, u32[]{:S(2)}, u32[]{:S(2)}) %all-to-all-start) | async-done | bytes 16928 | tf_op jit(solution)/shard_map/all_to_all | solution.py:207
  33.0 0.9 pad_maximum_fusion
  33.9 0.3 slice_convert_fusion
  34.2 9.2 %add_bitcast_fusion.1 = (f32[1,134,518]{2,1,0:T(8,128)S(1)}, f32[134,518]{1,0:T(8,128)S(1)}, f32[134,518]{1,0:T(8,128)S(1)}, f32[134,518]{1,0:T(8,128)S(1)}, f32[134,518]{1,0:T(8,128)S(1)}) fusion(f32[140,524]{1,0:T(8,128)S(1)} %and_convert_fusion, s32[2,134,518]{2,1,0:T(8,128)S(1)} %slice_convert_fusion, f32[6,140,524]{2,1,0:T(8,128)S(1)} %pad_maximum_fusion, ...), kind=kLoop, calls=%fused_computation.239 | loop fusion | flops 29638924 | bytes 26471312 | tf_op jit(solution)/shard_map/stack | solution.py:173
  43.4 8.1 %add_bitcast_fusion = f32[1,134,518]{2,1,0:T(8,128)S(1)} fusion(f32[134,518]{1,0:T(8,128)S(1)} %get-tuple-element.30, f32[134,518]{1,0:T(8,128)S(1)} %get-tuple-element.29, f32[140,524]{1,0:T(8,128)S(1)} %and_convert_fusion, f32[134,518]{1,0:T(8,128)S(1)} %get-tuple-element.28, f32[134,518]{1,0:T(8,128)S(1)} %get-tuple-element.27, ...), kind=kLoop, calls=%fused_computation.238 | loop fusion | flops 27834212 | bytes 24710672 | tf_op jit(solution)/shard_map/stack | solution.py:173
  51.5 0.5 fusion
  52.0 0.5 copy-done.2
  52.5 5.9 %add_bitcast_fusion.3 = f32[1,128,512]{2,1,0:T(8,128)S(1)} fusion(f32[2,134,518]{2,1,0:T(8,128)S(1)} %get-tuple-element.24, f32[140,524]{1,0:T(8,128)S(1)} %and_convert_fusion, s32[2,128,512]{2,1,0:T(8,128)S(1)} %copy-done.2), kind=kLoop, calls=%fused_computation.460 | loop fusion | flops 26673152 | bytes 23330816 | tf_op jit(solution)/shard_map/stack | solution.py:173
  58.5 6.1 %add_bitcast_fusion.2 = f32[1,128,512]{2,1,0:T(8,128)S(1)} fusion(f32[2,134,518]{2,1,0:T(8,128)S(1)} %get-tuple-element.24, f32[140,524]{1,0:T(8,128)S(1)} %and_convert_fusion, s32[2,128,512]{2,1,0:T(8,128)S(1)} %copy-done.2), kind=kLoop, calls=%fused_computation.459 | loop fusion | flops 26673152 | bytes 23330816 | tf_op jit(solution)/shard_map/stack | solution.py:173
  64.6 1.2 %slice_add_fusion.3 = (f32[2,128,512]{2,1,0:T(8,128)S(1)}, f32[2,128,512]{2,1,0:T(8,128)}) fusion(f32[2,134,518]{2,1,0:T(8,128)S(1)} %get-tuple-element.24, f32[1,128,512]{2,1,0:T(8,128)S(1)} %add_bitcast_fusion.2, f32[1,128,512]{2,1,0:T(8,128)S(1)} %add_bitcast_fusion.3, f32[2,134,518]{2,1,0:T(8,128)S(1)} %get-tuple-element.25), kind=kLoop, calls=%fused_computation.7 | loop fusion | flops 655360 | bytes 2621440 | tf_op jit(solution)/shard_map/add | solution.py:202
  65.8 1.5 %fusion.231 = (f32[]{:T(128)}, f32[]{:T(128)}, f32[128,512]{1,0:T(8,128)}, f32[128,512]{1,0:T(8,128)}) fusion(f32[2,128,512]{2,1,0:T(8,128)S(1)} %get-tuple-element.16, f32[512]{0:T(512)S(1)} %add_convert_fusion, f32[128]{0:T(128)S(1)} %add_convert_fusion.1), kind=kLoop, calls=%fused_computation.426 | loop fusion | flops 393214 | bytes 1051144 | tf_op jit(solution)/shard_map/reduce_max | solution.py:215
  68.5 0.7 reshape.645.pos_ref
  69.2 0.6 stack.47.geo_ref
  69.8 15.6 %shard_map.84 = f32[32,2,128]{2,1,0:T(2,128)} custom-call(f32[5]{0:T(128)} %stack.47.geo_ref, f32[4224]{0:T(1024)} %reshape.645.pos_ref, f32[128,512]{1,0:T(8,128)} %get-tuple-element.36.xr_ref, f32[128,512]{1,0:T(8,128)} %get-tuple-element.35.xc_ref), custom_call_target="tpu_custom_call" | custom-call | tf_op jit(solution)/shard_map/pallas_call | solution.py:113
  85.4 0.8 slice_bitcast_fusion
  86.3 0.7 broadcast_in_dim.39
  87.0 8.5 %all-to-all-start.1 = ((f32[256,1,128]{2,1,0:T(1,128)}), f32[256,1,128]{2,1,0:T(1,128)S(1)}, u32[]{:S(2)}, u32[]{:S(2)}) async-start(f32[256,1,128]{2,1,0:T(1,128)} %bitcast.182), calls=%async_computation.1 | async-start | bytes 262144 | tf_op jit(solution)/shard_map/all_to_all | solution.py:231
  95.5 2.7 %divide_subtract_fusion = f32[128,512]{1,0:T(8,128)} fusion(f32[140,524]{1,0:T(8,128)S(1)} %and_convert_fusion, s32[2,128,512]{2,1,0:T(8,128)S(1)} %copy-done.2), kind=kLoop, calls=%fused_computation.458 | loop fusion | flops 11010048 | bytes 8126464 | tf_op jit(solution)/shard_map/sub | solution.py:196
  98.2 10.2 %all-to-all-done.1 = f32[256,1,128]{2,1,0:T(1,128)S(1)} async-done(((f32[256,1,128]{2,1,0:T(1,128)}), f32[256,1,128]{2,1,0:T(1,128)S(1)}, u32[]{:S(2)}, u32[]{:S(2)}) %all-to-all-start.1) | async-done | bytes 131104 | tf_op jit(solution)/shard_map/all_to_all | solution.py:231
  108.4 0.3 reduce_sum.9
  108.8 0.6 copy.18
  (31 shorter events, 1.2 us)
Async XLA Ops:
  0.6 22.9 %copy-start.1 = (f32[2,128,512]{2,1,0:T(8,128)S(1)}, f32[2,128,512]{2,1,0:T(8,128)}, u32[]{:S(2)}) copy-start(f32[2,128,512]{2,1,0:T(8,128)} %param.5) | copy-start | bytes 1572868
  0.6 22.9 %copy-start = (f32[2,128,512]{2,1,0:T(8,128)S(1)}, f32[2,128,512]{2,1,0:T(8,128)}, u32[]{:S(2)}) copy-start(f32[2,128,512]{2,1,0:T(8,128)} %param.6) | copy-start | bytes 1572868
  0.7 8.9 %copy-start.4 = (f32[64,2]{0,1:T(2,128)S(1)}, f32[64,2]{0,1:T(2,128)}, u32[]{:S(2)}) copy-start(f32[64,2]{0,1:T(2,128)} %param.8) | copy-start | bytes 1540
  0.7 9.1 %copy-start.5 = (s32[1,4]{1,0:T(1,128)S(1)}, s32[1,4]{1,0:T(1,128)}, u32[]{:S(2)}) copy-start(s32[1,4]{1,0:T(1,128)} %param.9) | copy-start | bytes 52
  2.7 20.8 %collective-permute-start = (f32[6,6,512]{2,1,0:T(8,128)S(1)}, f32[6,6,512]{2,1,0:T(8,128)S(1)}, u32[]{:S(2)}, u32[]{:S(2)}) collective-permute-start(f32[6,6,512]{2,1,0:T(8,128)S(1)} %get-tuple-element.33), channel_id=1, source_target_pairs={{0,8},{8,16},{16,24},{24,32},{32,40},{40,48},{48,56},{56,64},{64,7... | collective-permute-start | bytes 221192 | tf_op jit(solution)/shard_map/ppermute | solution.py:132
  7.6 15.9 %collective-permute-start.1 = (f32[6,6,512]{2,1,0:T(8,128)S(1)}, f32[6,6,512]{2,1,0:T(8,128)S(1)}, u32[]{:S(2)}, u32[]{:S(2)}) collective-permute-start(f32[6,6,512]{2,1,0:T(8,128)S(1)} %get-tuple-element.34), channel_id=1, source_target_pairs={{8,0},{16,8},{24,16},{32,24},{40,32},{48,40},{56,48},{64,56},{72,6... | collective-permute-start | bytes 221192 | tf_op jit(solution)/shard_map/ppermute | solution.py:133
  10.5 22.1 %all-to-all-start = ((f32[32,1,132]{2,1,0:T(1,128)}), f32[32,1,132]{2,1,0:T(1,128)S(1)}, u32[]{:S(2)}, u32[]{:S(2)}) async-start(f32[32,1,132]{2,1,0:T(1,128)} %broadcast_in_dim.35), calls=%async_computation | async-start | bytes 65536 | tf_op jit(solution)/shard_map/all_to_all | solution.py:207
  24.0 8.6 %collective-permute-start.2 = (f32[5040]{0:T(1024)S(1)}, f32[5040]{0:T(1024)S(1)}, u32[]{:S(2)}, u32[]{:S(2)}) collective-permute-start(f32[5040]{0:T(1024)S(1)} %reshape.641), channel_id=1, source_target_pairs={{0,1},{1,2},{2,3},{3,4},{4,5},{5,6},{6,7},{8,9},{9,10},{10,11},{11... | collective-permute-start | bytes 60488 | tf_op jit(solution)/shard_map/ppermute | solution.py:132
  26.5 6.3 %collective-permute-start.3 = (f32[5040]{0:T(1024)S(1)}, f32[5040]{0:T(1024)S(1)}, u32[]{:S(2)}, u32[]{:S(2)}) collective-permute-start(f32[5040]{0:T(1024)S(1)} %reshape.643), channel_id=1, source_target_pairs={{1,0},{2,1},{3,2},{4,3},{5,4},{6,5},{7,6},{9,8},{10,9},{11,10},{12... | collective-permute-start | bytes 60488 | tf_op jit(solution)/shard_map/ppermute | solution.py:133
  51.5 1.0 copy-start.2
  65.8 32.4 %copy-start.3 = (f32[2,128,512]{2,1,0:T(8,128)}, f32[2,128,512]{2,1,0:T(8,128)S(1)}, u32[]{:S(2)}) copy-start(f32[2,128,512]{2,1,0:T(8,128)S(1)} %get-tuple-element.16) | copy-start | bytes 1572868
  87.0 21.4 %all-to-all-start.1 = ((f32[256,1,128]{2,1,0:T(1,128)}), f32[256,1,128]{2,1,0:T(1,128)S(1)}, u32[]{:S(2)}, u32[]{:S(2)}) async-start(f32[256,1,128]{2,1,0:T(1,128)} %bitcast.182), calls=%async_computation.1 | async-start | bytes 262144 | tf_op jit(solution)/shard_map/all_to_all | solution.py:231

commit v10 on v8

--- a/solution.py
+++ b/solution.py
@@ -140,19 +140,15 @@
     return kept_sum, exist_sum
 
 
-def forces(padded, bits, present_pad, rows, cols):
+def forces(padded, bits, rows, cols):
     centre = padded[:, 3 : 3 + rows, 3 : 3 + cols]
     total_row = jnp.zeros((rows, cols), jnp.float32)
     total_col = jnp.zeros((rows, cols), jnp.float32)
-    kept_sum = jnp.zeros((rows, cols), jnp.float32)
-    exist_sum = jnp.zeros((rows, cols), jnp.float32)
     for index, (row_off, col_off) in enumerate(offsets):
         other = padded[:, 3 + row_off : 3 + row_off + rows, 3 + col_off : 3 + col_off + cols]
-        present = present_pad[3 + row_off : 3 + row_off + rows, 3 + col_off : 3 + col_off + cols]
-        flag = jnp.bitwise_and(jnp.right_shift(bits[index // 14], index % 14), 1).astype(
+        keep = jnp.bitwise_and(jnp.right_shift(bits[index // 14], index % 14), 1).astype(
             jnp.float32
         )
-        keep = flag * present
         row_part = row_off + (other[0] - centre[0])
         col_part = col_off + (other[1] - centre[1])
         inv_length = lax.rsqrt(row_part * row_part + col_part * col_part)
@@ -160,9 +156,7 @@
         coeff = keep * (inv_rest - inv_length)
         total_row = total_row + coeff * row_part
         total_col = total_col + coeff * col_part
-        kept_sum = kept_sum + keep
-        exist_sum = exist_sum + present
-    return (jnp.stack([total_row, total_col]), kept_sum, exist_sum)
+    return jnp.stack([total_row, total_col])
 
 
 def body(disp, velocity, bond_bits, panel_pos, contact_list):
@@ -181,15 +175,21 @@
     inside_col = (grid_col >= 0) & (grid_col < total_cols)
     present_wide = (inside_row[:, None] & inside_col[None, :]).astype(jnp.float32)
     present_ring = present_wide[3:-3, 3:-3]
-    force, _, _ = forces(
-        ext[0:2], ext[4:6, 3:-3, 3:-3].astype(jnp.int32), present_wide, rows + 6, cols + 6
-    )
+    ring_bits = ext[4:6, 3:-3, 3:-3].astype(jnp.int32)
+    words = [jnp.zeros((rows + 6, cols + 6), jnp.int32) for _ in range(2)]
+    for index, (row_off, col_off) in enumerate(offsets):
+        inside = present_wide[3 + row_off : 3 + row_off + rows + 6, 3 + col_off : 3 + col_off + cols + 6]
+        words[index // 14] = words[index // 14] | jnp.left_shift(
+            inside.astype(jnp.int32), index % 14
+        )
+    ring_bits = jnp.bitwise_and(ring_bits, jnp.stack(words))
+    force = forces(ext[0:2], ring_bits, rows + 6, cols + 6)
     kept_sum, exist_sum = bond_counts(bond_bits, present_ring, rows, cols)
     damage = 1.0 - kept_sum / exist_sum
     ring_v = ext[2:4, 3:-3, 3:-3] + 10.0 * force
     ring_u = ext[0:2, 3:-3, 3:-3] + 0.05 * ring_v
     ring_u = jnp.where(present_ring[None] > 0.0, ring_u, 0.0)
-    force, _, _ = forces(ring_u, bond_bits, present_ring, rows, cols)
+    force = forces(ring_u, ring_bits[:, 3:-3, 3:-3], rows, cols)
     state_v = ring_v[:, 3:-3, 3:-3] + 10.0 * force
     state_u = ring_u[:, 3:-3, 3:-3] + 0.05 * state_v
     block_count = lax.axis_size("along")

time: 105 us -> 109 us (1.038); the launches traced: 104 us -> 110 us
  starting transfers between devices: 30.3 us -> 39 us
  Pallas kernels: 10.3 us -> 6.89 us
  waiting for transfers between devices: 14.8 us -> 12.6 us
  local copies, waits for them, and re-layouts: 5.26 us -> 7.39 us
    another operation x4 -> x2, other arithmetic: 29.3 us -> 2.56 us  [body(): ring_bits = jnp.bitwise_and(ring_bits, jnp.stack(words))]
    add x0 -> x4, other arithmetic: none -> 23.9 us  [the longest x2 13.2 us: forces(): total_row = total_row + coeff * row_part]
    all_to_all x1, starting transfers between devices: 7.17 us -> 15.9 us  [body(): arrived = lax.all_to_all(spread, ('along', 'across'), 0, 0, tiled=True)]
    all_to_all x1, waiting for transfers between devices: 4.74 us -> 0.01 us  [body(): lax.all_to_all(jnp.broadcast_to(packed[None], (block_count,) + packed.sha...]
    pallas_call x1, Pallas kernels: 10.3 us -> 6.89 us  [contact_sums(): pl.pallas_call(contact_kernel, out_shape=jax.ShapeDtypeStruct((blocks, 2,...]
    ppermute x2, waiting for transfers between devices: 0.01 us -> 2.54 us  [with_halo(): high = lax.ppermute(high, axis, backward).reshape(strip)]
  transfers between devices with their start and end apart: 6 -> 6, of which waited for: 2 -> 2; matrix products, arithmetic and copies ran while one was open for 5% -> 10% of each run, Pallas kernels for 0% -> 0%
where the time goes in v10:
time: 109 us; the launch traced here: 110 us
  other arithmetic  42 us (39%)
  starting transfers between devices  39 us (36%)
  waiting for transfers between devices  12.6 us (12%)
  local copies, waits for them, and re-layouts  7.39 us (7%)
  Pallas kernels  6.89 us (6%)
  between operations  2.24 us (2%)
    all_to_all x1, starting transfers between devices, body(): arrived = lax.all_to_all(spread, ('along', 'across'), 0, 0, tiled=True)  15.9 us
    add x2, other arithmetic, forces(): total_row = total_row + coeff * row_part  13.2 us
    all_to_all x1, starting transfers between devices, body(): lax.all_to_all(jnp.broadcast_to(packed[None], (block_count,) + packed.sha...  12.7 us
    add x2, other arithmetic, forces(): total_col = total_col + coeff * col_part  10.6 us
    all_to_all x1, waiting for transfers between devices, body(): arrived = lax.all_to_all(spread, ('along', 'across'), 0, 0, tiled=True)  10.1 us
    ppermute x2, starting transfers between devices, with_halo(): low = lax.ppermute(low, axis, forward).reshape(strip)  7.22 us
    pallas_call x1, Pallas kernels, contact_sums(): pl.pallas_call(contact_kernel, out_shape=jax.ShapeDtypeStruct((blocks, 2,...  6.89 us
    ppermute x2, starting transfers between devices, with_halo(): high = lax.ppermute(high, axis, backward).reshape(strip)  3.21 us
  transfers between devices with their start and end apart: 6, of which 2 were waited for; matrix products, arithmetic and copies ran while one was open for 10% of the time, Pallas kernels for 0%

profile of v10, /device:TPU:1, one launch (start us, length us, event | category | flops | bytes accessed | tf_op | source)
XLA Modules:
  0.0 110.1 jit_solution(15846689744655718601)
XLA Ops:
  0.7 1.1 convert_element_type.569
  1.7 0.8 pad_maximum_fusion.18
  2.6 4.9 %collective-permute-start = (f32[6,6,512]{2,1,0:T(8,128)S(1)}, f32[6,6,512]{2,1,0:T(8,128)S(1)}, u32[]{:S(2)}, u32[]{:S(2)}) collective-permute-start(f32[6,6,512]{2,1,0:T(8,128)S(1)} %get-tuple-element.33), channel_id=1, source_target_pairs={{0,8},{8,16},{16,24},{24,32},{32,40},{40,48},{48,56},{56,64},{64,7... | collective-permute-start | bytes 221192 | tf_op jit(solution)/shard_map/ppermute | solution.py:124
  7.5 1.9 %collective-permute-start.1 = (f32[6,6,512]{2,1,0:T(8,128)S(1)}, f32[6,6,512]{2,1,0:T(8,128)}, u32[]{:S(2)}, u32[]{:S(2)}) collective-permute-start(f32[6,6,512]{2,1,0:T(8,128)S(1)} %get-tuple-element.34), channel_id=1, source_target_pairs={{8,0},{16,8},{24,16},{32,24},{40,32},{48,40},{56,48},{64,56},{72,6... | collective-permute-start | bytes 221192 | tf_op jit(solution)/shard_map/ppermute | solution.py:125
  9.7 0.6 broadcast_in_dim.35
  10.4 12.7 %all-to-all-start = ((f32[32,1,132]{2,1,0:T(1,128)}), f32[32,1,132]{2,1,0:T(1,128)S(1)}, u32[]{:S(2)}, u32[]{:S(2)}) async-start(f32[32,1,132]{2,1,0:T(1,128)} %broadcast_in_dim.35), calls=%async_computation | async-start | bytes 65536 | tf_op jit(solution)/shard_map/all_to_all | solution.py:199
  23.2 1.3 %fusion.50 = s32[1,134,518]{2,1,0:T(8,128)S(1)} fusion(f32[140,524]{1,0:T(8,128)S(1)} %and_convert_fusion), kind=kLoop, calls=%fused_computation.129 | loop fusion | flops 2845892 | bytes 4164720 | tf_op jit(solution)/shard_map/stack | solution.py:185
  24.5 1.2 %fusion.78 = s32[1,134,518]{2,1,0:T(8,128)S(1)} fusion(f32[140,524]{1,0:T(8,128)S(1)} %and_convert_fusion), kind=kLoop, calls=%fused_computation.171 | loop fusion | flops 2845892 | bytes 4164720 | tf_op jit(solution)/shard_map/stack | solution.py:185
  25.8 0.8 slice_compare_fusion
  27.2 0.6 copy-done.4
  27.8 1.0 pad_maximum_fusion.5
  28.8 0.8 reshape.213
  29.7 2.3 %collective-permute-start.2 = (f32[5040]{0:T(1024)}, f32[5040]{0:T(1024)S(1)}, u32[]{:S(2)}, u32[]{:S(2)}) collective-permute-start(f32[5040]{0:T(1024)} %reshape.213), channel_id=1, source_target_pairs={{0,1},{1,2},{2,3},{3,4},{4,5},{5,6},{6,7},{8,9},{9,10},{10,11},{11... | collective-permute-start | bytes 60488 | tf_op jit(solution)/shard_map/ppermute | solution.py:124
  32.2 1.3 %collective-permute-start.3 = (f32[5040]{0:T(1024)S(1)}, f32[5040]{0:T(1024)}, u32[]{:S(2)}, u32[]{:S(2)}) collective-permute-start(f32[5040]{0:T(1024)S(1)} %reshape.215), channel_id=1, source_target_pairs={{1,0},{2,1},{3,2},{4,3},{5,4},{6,5},{7,6},{9,8},{10,9},{11,10},{12... | collective-permute-start | bytes 60488 | tf_op jit(solution)/shard_map/ppermute | solution.py:125
  34.9 2.5 %collective-permute-done.3 = f32[5040]{0:T(1024)} collective-permute-done((f32[5040]{0:T(1024)S(1)}, f32[5040]{0:T(1024)}, u32[]{:S(2)}, u32[]{:S(2)}) %collective-permute-start.3) | collective-permute-done | bytes 20192 | tf_op jit(solution)/shard_map/ppermute | solution.py:125
  37.4 0.9 reshape.216
  38.3 1.9 %pad_maximum_fusion = f32[6,140,524]{2,1,0:T(8,128)S(1)} fusion(f32[6,140,6]{2,1,0:T(8,128)S(1)} %reshape.216, f32[6,6,512]{2,1,0:T(8,128)} %collective-permute-done.1, f32[2,128,512]{2,1,0:T(8,128)S(1)} %convert_element_type.569, f32[2,128,512]{2,1,0:T(8,128)S(1)} %copy-done, f32[2,128,512]{2,1,0:T(8,128)S(1)} %copy-done.1, f32[6,6,512]{2,1,0:T(8,128)} %copy-done.4, ...), kind=kLoop, calls=%fused_computation | loop fusion | flops 2640960 | bytes 3521280 | tf_op jit(solution)/shard_map/concatenate | solution.py:126
  40.5 8.7 %multiply_add_fusion.1 = (f32[1,134,518]{2,1,0:T(8,128)S(1)}, f32[1,134,518]{2,1,0:T(8,128)S(1)}, f32[1,134,518]{2,1,0:T(8,128)S(1)}, f32[1,134,518]{2,1,0:T(8,128)S(1)}, f32[1,134,518]{2,1,0:T(8,128)S(1)}) fusion(s32[2,134,518]{2,1,0:T(8,128)S(1)} %fusion, f32[6,140,524]{2,1,0:T(8,128)S(1)} %pad_maximum_fusion, f32[6,6,512]{2,1,0:T(8,128)} %collective-permute-done.1, ...), kind=kLoop, calls=%fused_computation.212 | loop fusion | flops 27695388 | bytes 18697168 | tf_op jit(solution)/shard_map/add | solution.py:157
  49.2 6.1 %multiply_add_fusion = f32[1,134,518]{2,1,0:T(8,128)S(1)} fusion(f32[1,134,518]{2,1,0:T(8,128)S(1)} %get-tuple-element.30, f32[1,134,518]{2,1,0:T(8,128)S(1)} %get-tuple-element.29, f32[1,134,518]{2,1,0:T(8,128)S(1)} %get-tuple-element.28, f32[1,134,518]{2,1,0:T(8,128)S(1)} %get-tuple-element.27, s32[2,134,518]{2,1,0:T(8,128)S(1)} %fusion, ...), kind=kLoop, calls=%fused_computation.211 | loop fusion | flops 25890676 | bytes 16936528 | tf_op jit(solution)/shard_map/add | solution.py:158
  55.8 4.6 %multiply_add_fusion.3 = f32[1,128,512]{2,1,0:T(8,128)S(1)} fusion(s32[2,134,518]{2,1,0:T(8,128)S(1)} %fusion, f32[2,134,518]{2,1,0:T(8,128)S(1)} %get-tuple-element.24), kind=kLoop, calls=%fused_computation.433 | loop fusion | flops 24838144 | bytes 15990784 | tf_op jit(solution)/shard_map/add | solution.py:157
  60.4 4.5 %multiply_add_fusion.2 = f32[1,128,512]{2,1,0:T(8,128)S(1)} fusion(s32[2,134,518]{2,1,0:T(8,128)S(1)} %fusion, f32[2,134,518]{2,1,0:T(8,128)S(1)} %get-tuple-element.24), kind=kLoop, calls=%fused_computation.432 | loop fusion | flops 24838144 | bytes 15990784 | tf_op jit(solution)/shard_map/add | solution.py:158
  65.0 1.2 %slice_add_fusion.3 = (f32[2,128,512]{2,1,0:T(8,128)S(1)}, f32[2,128,512]{2,1,0:T(8,128)}) fusion(f32[2,134,518]{2,1,0:T(8,128)S(1)} %get-tuple-element.24, f32[1,128,512]{2,1,0:T(8,128)S(1)} %multiply_add_fusion.2, f32[1,128,512]{2,1,0:T(8,128)S(1)} %multiply_add_fusion.3, f32[2,134,518]{2,1,0:T(8,128)S(1)} %get-tuple-element.25), kind=kLoop, calls=%fused_computation.8 | loop fusion | flops 655360 | bytes 2621440 | tf_op jit(solution)/shard_map/add | solution.py:194
  66.1 1.6 %fusion.148 = (f32[]{:T(128)}, f32[]{:T(128)}, f32[128,512]{1,0:T(8,128)}, f32[128,512]{1,0:T(8,128)}) fusion(f32[2,128,512]{2,1,0:T(8,128)S(1)} %get-tuple-element.16, f32[512]{0:T(512)S(1)} %copy-done.8, f32[128]{0:T(128)S(1)} %copy-done.10), kind=kLoop, calls=%fused_computation.371 | loop fusion | flops 393214 | bytes 1051144 | tf_op jit(solution)/shard_map/reduce_max | solution.py:207
  69.0 0.7 reshape.217.pos_ref
  69.7 0.7 stack.47.geo_ref
  70.4 6.9 %shard_map.84 = f32[32,2,64,128]{3,2,1,0:T(8,128)} custom-call(f32[5]{0:T(128)} %stack.47.geo_ref, f32[4224]{0:T(1024)} %reshape.217.pos_ref, f32[128,512]{1,0:T(8,128)} %get-tuple-element.36.xr_ref, f32[128,512]{1,0:T(8,128)} %get-tuple-element.35.xc_ref), custom_call_target="tpu_custom_call" | custom-call | tf_op jit(solution)/shard_map/pallas_call | solution.py:105
  77.3 2.2 %reduce_sum.18 = f32[32,2,64]{2,1,0:T(2,128)S(1)} reduce(f32[32,2,64,128]{3,2,1,0:T(8,128)} %shard_map.84, f32[]{:T(128)} %constant.45.clone.1), dimensions={3}, to_apply=%region_2.3 | reduce | flops 520192 | bytes 2113540 | tf_op jit(solution)/shard_map/reduce_sum | solution.py:218
  79.7 0.7 broadcast_in_dim.39
  80.4 15.9 %all-to-all-start.1 = ((f32[256,1,128]{2,1,0:T(1,128)}), f32[256,1,128]{2,1,0:T(1,128)S(1)}, u32[]{:S(2)}, u32[]{:S(2)}) async-start(f32[256,1,128]{2,1,0:T(1,128)} %bitcast.40), calls=%async_computation.1 | async-start | bytes 262144 | tf_op jit(solution)/shard_map/all_to_all | solution.py:223
  96.3 2.7 %fusion.152 = f32[128,512]{1,0:T(8,128)} fusion(f32[140,524]{1,0:T(8,128)S(1)} %and_convert_fusion, s32[2,128,512]{2,1,0:T(8,128)S(1)} %copy-done.2), kind=kLoop, calls=%fused_computation.378 | loop fusion | flops 11010048 | bytes 8126464 | tf_op jit(solution)/shard_map/sub | solution.py:188
  98.9 10.1 %all-to-all-done.1 = f32[256,1,128]{2,1,0:T(1,128)S(1)} async-done(((f32[256,1,128]{2,1,0:T(1,128)}), f32[256,1,128]{2,1,0:T(1,128)S(1)}, u32[]{:S(2)}, u32[]{:S(2)}) %all-to-all-start.1) | async-done | bytes 131104 | tf_op jit(solution)/shard_map/all_to_all | solution.py:223
  109.4 0.6 copy.17
  (45 shorter events, 3.9 us)
Async XLA Ops:
  0.6 8.8 %copy-start.9 = (f32[64,2]{0,1:T(2,128)S(1)}, f32[64,2]{0,1:T(2,128)}, u32[]{:S(2)}) copy-start(f32[64,2]{0,1:T(2,128)} %param.8) | copy-start | bytes 1540
  0.6 9.1 %copy-start.11 = (s32[1,4]{1,0:T(1,128)S(1)}, s32[1,4]{1,0:T(1,128)}, u32[]{:S(2)}) copy-start(s32[1,4]{1,0:T(1,128)} %param.9) | copy-start | bytes 52
  2.6 24.6 %collective-permute-start = (f32[6,6,512]{2,1,0:T(8,128)S(1)}, f32[6,6,512]{2,1,0:T(8,128)S(1)}, u32[]{:S(2)}, u32[]{:S(2)}) collective-permute-start(f32[6,6,512]{2,1,0:T(8,128)S(1)} %get-tuple-element.33), channel_id=1, source_target_pairs={{0,8},{8,16},{16,24},{24,32},{32,40},{40,48},{48,56},{56,64},{64,7... | collective-permute-start | bytes 221192 | tf_op jit(solution)/shard_map/ppermute | solution.py:124
  7.5 20.3 %collective-permute-start.1 = (f32[6,6,512]{2,1,0:T(8,128)S(1)}, f32[6,6,512]{2,1,0:T(8,128)}, u32[]{:S(2)}, u32[]{:S(2)}) collective-permute-start(f32[6,6,512]{2,1,0:T(8,128)S(1)} %get-tuple-element.34), channel_id=1, source_target_pairs={{8,0},{16,8},{24,16},{32,24},{40,32},{48,40},{56,48},{64,56},{72,6... | collective-permute-start | bytes 221192 | tf_op jit(solution)/shard_map/ppermute | solution.py:125
  10.4 23.7 %all-to-all-start = ((f32[32,1,132]{2,1,0:T(1,128)}), f32[32,1,132]{2,1,0:T(1,128)S(1)}, u32[]{:S(2)}, u32[]{:S(2)}) async-start(f32[32,1,132]{2,1,0:T(1,128)} %broadcast_in_dim.35), calls=%async_computation | async-start | bytes 65536 | tf_op jit(solution)/shard_map/all_to_all | solution.py:199
  24.5 3.3 %copy-start = (f32[2,128,512]{2,1,0:T(8,128)S(1)}, f32[2,128,512]{2,1,0:T(8,128)}, u32[]{:S(2)}) copy-start(f32[2,128,512]{2,1,0:T(8,128)} %param.6) | copy-start | bytes 1572868
  24.5 3.3 %copy-start.1 = (f32[2,128,512]{2,1,0:T(8,128)S(1)}, f32[2,128,512]{2,1,0:T(8,128)}, u32[]{:S(2)}) copy-start(f32[2,128,512]{2,1,0:T(8,128)} %param.5) | copy-start | bytes 1572868
  27.2 0.6 copy-start.4
  29.7 5.0 %collective-permute-start.2 = (f32[5040]{0:T(1024)}, f32[5040]{0:T(1024)S(1)}, u32[]{:S(2)}, u32[]{:S(2)}) collective-permute-start(f32[5040]{0:T(1024)} %reshape.213), channel_id=1, source_target_pairs={{0,1},{1,2},{2,3},{3,4},{4,5},{5,6},{6,7},{8,9},{9,10},{10,11},{11... | collective-permute-start | bytes 60488 | tf_op jit(solution)/shard_map/ppermute | solution.py:124
  32.2 5.2 %collective-permute-start.3 = (f32[5040]{0:T(1024)S(1)}, f32[5040]{0:T(1024)}, u32[]{:S(2)}, u32[]{:S(2)}) collective-permute-start(f32[5040]{0:T(1024)S(1)} %reshape.215), channel_id=1, source_target_pairs={{1,0},{2,1},{3,2},{4,3},{5,4},{6,5},{7,6},{9,8},{10,9},{11,10},{12... | collective-permute-start | bytes 60488 | tf_op jit(solution)/shard_map/ppermute | solution.py:125
  38.3 2.2 %copy-start.5 = (f32[6,6,512]{2,1,0:T(8,128)S(1)}, f32[6,6,512]{2,1,0:T(8,128)}, u32[]{:S(2)}) copy-start(f32[6,6,512]{2,1,0:T(8,128)} %copy-done.4) | copy-start | bytes 221188
  49.2 6.1 %copy-start.6 = (pred[134,518]{1,0:T(8,128)(4,1)S(1)}, pred[134,518]{1,0:T(8,128)(4,1)}, u32[]{:S(2)}) copy-start(pred[134,518]{1,0:T(8,128)(4,1)} %slice_compare_fusion) | copy-start | bytes 208240
  64.9 1.2 %copy-start.8 = (f32[512]{0:T(512)S(1)}, f32[512]{0:T(512)}, u32[]{:S(2)}) copy-start(f32[512]{0:T(512)} %add_convert_fusion) | copy-start | bytes 6148
  64.9 1.2 %copy-start.10 = (f32[128]{0:T(128)S(1)}, f32[128]{0:T(128)}, u32[]{:S(2)}) copy-start(f32[128]{0:T(128)} %add_convert_fusion.1) | copy-start | bytes 1540
  65.0 4.0 %copy-start.7 = (f32[32,1,132]{2,0,1:T(8,128)S(1)}, f32[32,1,132]{2,0,1:T(8,128)}, u32[]{:S(2)}) copy-start(f32[32,1,132]{2,0,1:T(8,128)} %copy.20) | copy-start | bytes 50692
  66.1 13.4 %copy-start.3 = (f32[2,128,512]{2,1,0:T(8,128)}, f32[2,128,512]{2,1,0:T(8,128)S(1)}, u32[]{:S(2)}) copy-start(f32[2,128,512]{2,1,0:T(8,128)S(1)} %get-tuple-element.16) | copy-start | bytes 1572868
  70.4 25.8 %copy-start.2 = (s32[2,128,512]{2,1,0:T(8,128)S(1)}, s32[2,128,512]{2,1,0:T(8,128)}, u32[]{:S(2)}) copy-start(s32[2,128,512]{2,1,0:T(8,128)} %param.7) | copy-start | bytes 1572868
  80.4 28.6 %all-to-all-start.1 = ((f32[256,1,128]{2,1,0:T(1,128)}), f32[256,1,128]{2,1,0:T(1,128)S(1)}, u32[]{:S(2)}, u32[]{:S(2)}) async-start(f32[256,1,128]{2,1,0:T(1,128)} %bitcast.40), calls=%async_computation.1 | async-start | bytes 262144 | tf_op jit(solution)/shard_map/all_to_all | solution.py:223

commit v11 on v10

--- a/solution.py
+++ b/solution.py
@@ -176,13 +176,16 @@
     present_wide = (inside_row[:, None] & inside_col[None, :]).astype(jnp.float32)
     present_ring = present_wide[3:-3, 3:-3]
     ring_bits = ext[4:6, 3:-3, 3:-3].astype(jnp.int32)
-    words = [jnp.zeros((rows + 6, cols + 6), jnp.int32) for _ in range(2)]
+    row_words = [jnp.zeros((rows + 6,), jnp.int32) for _ in range(2)]
+    col_words = [jnp.zeros((cols + 6,), jnp.int32) for _ in range(2)]
     for index, (row_off, col_off) in enumerate(offsets):
-        inside = present_wide[3 + row_off : 3 + row_off + rows + 6, 3 + col_off : 3 + col_off + cols + 6]
-        words[index // 14] = words[index // 14] | jnp.left_shift(
-            inside.astype(jnp.int32), index % 14
-        )
-    ring_bits = jnp.bitwise_and(ring_bits, jnp.stack(words))
+        word, bit = index // 14, index % 14
+        row_in = inside_row[3 + row_off : 3 + row_off + rows + 6].astype(jnp.int32)
+        col_in = inside_col[3 + col_off : 3 + col_off + cols + 6].astype(jnp.int32)
+        row_words[word] = row_words[word] | jnp.left_shift(row_in, bit)
+        col_words[word] = col_words[word] | jnp.left_shift(col_in, bit)
+    words = jnp.stack([row_words[w][:, None] & col_words[w][None, :] for w in range(2)])
+    ring_bits = jnp.bitwise_and(ring_bits, words)
     force = forces(ext[0:2], ring_bits, rows + 6, cols + 6)
     kept_sum, exist_sum = bond_counts(bond_bits, present_ring, rows, cols)
     damage = 1.0 - kept_sum / exist_sum

time: 109 us -> 107 us (0.982); the launches traced: 110 us -> 105 us
  starting transfers between devices: 39 us -> 31.2 us
  Pallas kernels: 6.89 us -> 12.1 us
  other arithmetic: 42 us -> 39.7 us
    all_to_all x1, starting transfers between devices: 15.9 us -> 8.09 us  [body(): arrived = lax.all_to_all(spread, ('along', 'across'), 0, 0, tiled=True)]
    pallas_call x1, Pallas kernels: 6.89 us -> 12.1 us  [contact_sums(): pl.pallas_call(contact_kernel, out_shape=jax.ShapeDtypeStruct((blocks, 2,...]
    another operation x2 -> x0, other arithmetic: 2.56 us -> none  [body(): ring_bits = jnp.bitwise_and(ring_bits, jnp.stack(words))]
  transfers between devices with their start and end apart: 6 -> 6, of which waited for: 2 -> 3; matrix products, arithmetic and copies ran while one was open for 10% -> 8% of each run, Pallas kernels for 0% -> 0%
where the time goes in v11:
time: 107 us; the launch traced here: 105 us
  other arithmetic  39.7 us (37%)
  starting transfers between devices  31.2 us (29%)
  waiting for transfers between devices  12.6 us (12%)
  Pallas kernels  12.1 us (11%)
  local copies, waits for them, and re-layouts  7.39 us (7%)
  between operations  2.19 us (2%)
    add x2, other arithmetic, forces(): total_row = total_row + coeff * row_part  13.2 us
    all_to_all x1, starting transfers between devices, body(): lax.all_to_all(jnp.broadcast_to(packed[None], (block_count,) + packed.sha...  12.7 us
    pallas_call x1, Pallas kernels, contact_sums(): pl.pallas_call(contact_kernel, out_shape=jax.ShapeDtypeStruct((blocks, 2,...  12.1 us
    add x2, other arithmetic, forces(): total_col = total_col + coeff * col_part  10.6 us
    all_to_all x1, waiting for transfers between devices, body(): arrived = lax.all_to_all(spread, ('along', 'across'), 0, 0, tiled=True)  10 us
    all_to_all x1, starting transfers between devices, body(): arrived = lax.all_to_all(spread, ('along', 'across'), 0, 0, tiled=True)  8.09 us
    ppermute x2, starting transfers between devices, with_halo(): low = lax.ppermute(low, axis, forward).reshape(strip)  7.22 us
    ppermute x2, starting transfers between devices, with_halo(): high = lax.ppermute(high, axis, backward).reshape(strip)  3.21 us
  transfers between devices with their start and end apart: 6, of which 3 were waited for; matrix products, arithmetic and copies ran while one was open for 8% of the time, Pallas kernels for 0%

profile of v11, /device:TPU:1, one launch (start us, length us, event | category | flops | bytes accessed | tf_op | source)
XLA Modules:
  0.0 105.1 jit_solution(15691524230611832182)
XLA Ops:
  0.7 1.2 %convert_element_type.569 = f32[2,128,512]{2,1,0:T(8,128)S(1)} convert(s32[2,128,512]{2,1,0:T(8,128)} %param.7) | non-fusion elementwise | flops 131072 | bytes 1048576 | tf_op jit(solution)/shard_map/convert_element_type | solution.py:170
  1.8 0.8 pad_maximum_fusion.18
  2.7 4.9 %collective-permute-start = (f32[6,6,512]{2,1,0:T(8,128)S(1)}, f32[6,6,512]{2,1,0:T(8,128)S(1)}, u32[]{:S(2)}, u32[]{:S(2)}) collective-permute-start(f32[6,6,512]{2,1,0:T(8,128)S(1)} %get-tuple-element.33), channel_id=1, source_target_pairs={{0,8},{8,16},{16,24},{24,32},{32,40},{40,48},{48,56},{56,64},{64,7... | collective-permute-start | bytes 221192 | tf_op jit(solution)/shard_map/ppermute | solution.py:124
  7.6 1.9 %collective-permute-start.1 = (f32[6,6,512]{2,1,0:T(8,128)S(1)}, f32[6,6,512]{2,1,0:T(8,128)}, u32[]{:S(2)}, u32[]{:S(2)}) collective-permute-start(f32[6,6,512]{2,1,0:T(8,128)S(1)} %get-tuple-element.34), channel_id=1, source_target_pairs={{8,0},{16,8},{24,16},{32,24},{40,32},{48,40},{56,48},{64,56},{72,6... | collective-permute-start | bytes 221192 | tf_op jit(solution)/shard_map/ppermute | solution.py:125
  9.8 0.6 broadcast_in_dim.23
  10.5 12.7 %all-to-all-start = ((f32[32,1,132]{2,1,0:T(1,128)}), f32[32,1,132]{2,1,0:T(1,128)S(1)}, u32[]{:S(2)}, u32[]{:S(2)}) async-start(f32[32,1,132]{2,1,0:T(1,128)} %broadcast_in_dim.23), calls=%async_computation | async-start | bytes 65536 | tf_op jit(solution)/shard_map/all_to_all | solution.py:202
  23.5 0.8 slice_compare_fusion
  25.0 0.6 copy-done.4
  25.6 1.0 pad_maximum_fusion.5
  26.6 0.8 reshape.299
  27.5 2.3 %collective-permute-start.2 = (f32[5040]{0:T(1024)}, f32[5040]{0:T(1024)S(1)}, u32[]{:S(2)}, u32[]{:S(2)}) collective-permute-start(f32[5040]{0:T(1024)} %reshape.299), channel_id=1, source_target_pairs={{0,1},{1,2},{2,3},{3,4},{4,5},{5,6},{6,7},{8,9},{9,10},{10,11},{11... | collective-permute-start | bytes 60488 | tf_op jit(solution)/shard_map/ppermute | solution.py:124
  30.0 1.3 %collective-permute-start.3 = (f32[5040]{0:T(1024)S(1)}, f32[5040]{0:T(1024)}, u32[]{:S(2)}, u32[]{:S(2)}) collective-permute-start(f32[5040]{0:T(1024)S(1)} %reshape.301), channel_id=1, source_target_pairs={{1,0},{2,1},{3,2},{4,3},{5,4},{6,5},{7,6},{9,8},{10,9},{11,10},{12... | collective-permute-start | bytes 60488 | tf_op jit(solution)/shard_map/ppermute | solution.py:125
  31.8 0.7 all-to-all-done
  32.6 0.6 copy.20
  33.4 1.8 %collective-permute-done.3 = f32[5040]{0:T(1024)} collective-permute-done((f32[5040]{0:T(1024)S(1)}, f32[5040]{0:T(1024)}, u32[]{:S(2)}, u32[]{:S(2)}) %collective-permute-start.3) | collective-permute-done | bytes 20192 | tf_op jit(solution)/shard_map/ppermute | solution.py:125
  35.2 0.9 reshape.302
  36.1 1.9 %pad_maximum_fusion = f32[6,140,524]{2,1,0:T(8,128)S(1)} fusion(f32[6,140,6]{2,1,0:T(8,128)S(1)} %reshape.302, f32[6,6,512]{2,1,0:T(8,128)} %collective-permute-done.1, f32[2,128,512]{2,1,0:T(8,128)S(1)} %convert_element_type.569, f32[2,128,512]{2,1,0:T(8,128)S(1)} %copy-done, f32[2,128,512]{2,1,0:T(8,128)S(1)} %copy-done.1, f32[6,6,512]{2,1,0:T(8,128)} %copy-done.4, ...), kind=kLoop, calls=%fused_computation | loop fusion | flops 2640960 | bytes 3521280 | tf_op jit(solution)/shard_map/concatenate | solution.py:126
  38.3 8.7 %multiply_add_fusion.1 = (f32[1,134,518]{2,1,0:T(8,128)S(1)}, f32[1,134,518]{2,1,0:T(8,128)S(1)}, f32[1,134,518]{2,1,0:T(8,128)S(1)}, f32[1,134,518]{2,1,0:T(8,128)S(1)}, f32[1,134,518]{2,1,0:T(8,128)S(1)}) fusion(s32[2,134,518]{2,1,0:T(8,128)S(1)} %fusion, f32[6,140,524]{2,1,0:T(8,128)S(1)} %pad_maximum_fusion, f32[6,6,512]{2,1,0:T(8,128)} %collective-permute-done.1, ...), kind=kLoop, calls=%fused_computation.128 | loop fusion | flops 27695388 | bytes 18697168 | tf_op jit(solution)/shard_map/add | solution.py:157
  47.0 6.1 %multiply_add_fusion = f32[1,134,518]{2,1,0:T(8,128)S(1)} fusion(f32[1,134,518]{2,1,0:T(8,128)S(1)} %get-tuple-element.30, f32[1,134,518]{2,1,0:T(8,128)S(1)} %get-tuple-element.29, f32[1,134,518]{2,1,0:T(8,128)S(1)} %get-tuple-element.28, f32[1,134,518]{2,1,0:T(8,128)S(1)} %get-tuple-element.27, s32[2,134,518]{2,1,0:T(8,128)S(1)} %fusion, ...), kind=kLoop, calls=%fused_computation.127 | loop fusion | flops 25890676 | bytes 16936528 | tf_op jit(solution)/shard_map/add | solution.py:158
  53.6 4.5 %multiply_add_fusion.3 = f32[1,128,512]{2,1,0:T(8,128)S(1)} fusion(s32[2,134,518]{2,1,0:T(8,128)S(1)} %fusion, f32[2,134,518]{2,1,0:T(8,128)S(1)} %get-tuple-element.24), kind=kLoop, calls=%fused_computation.349 | loop fusion | flops 24838144 | bytes 15990784 | tf_op jit(solution)/shard_map/add | solution.py:157
  58.2 4.5 %multiply_add_fusion.2 = f32[1,128,512]{2,1,0:T(8,128)S(1)} fusion(s32[2,134,518]{2,1,0:T(8,128)S(1)} %fusion, f32[2,134,518]{2,1,0:T(8,128)S(1)} %get-tuple-element.24), kind=kLoop, calls=%fused_computation.348 | loop fusion | flops 24838144 | bytes 15990784 | tf_op jit(solution)/shard_map/add | solution.py:158
  62.7 1.2 %slice_add_fusion.3 = (f32[2,128,512]{2,1,0:T(8,128)S(1)}, f32[2,128,512]{2,1,0:T(8,128)}) fusion(f32[2,134,518]{2,1,0:T(8,128)S(1)} %get-tuple-element.24, f32[1,128,512]{2,1,0:T(8,128)S(1)} %multiply_add_fusion.2, f32[1,128,512]{2,1,0:T(8,128)S(1)} %multiply_add_fusion.3, f32[2,134,518]{2,1,0:T(8,128)S(1)} %get-tuple-element.25), kind=kLoop, calls=%fused_computation.8 | loop fusion | flops 655360 | bytes 2621440 | tf_op jit(solution)/shard_map/add | solution.py:197
  63.9 1.5 %fusion.92 = (f32[]{:T(128)}, f32[]{:T(128)}, f32[128,512]{1,0:T(8,128)}, f32[128,512]{1,0:T(8,128)}) fusion(f32[2,128,512]{2,1,0:T(8,128)S(1)} %get-tuple-element.16, f32[512]{0:T(512)S(1)} %copy-done.8, f32[128]{0:T(128)S(1)} %copy-done.10), kind=kLoop, calls=%fused_computation.287 | loop fusion | flops 393214 | bytes 1051144 | tf_op jit(solution)/shard_map/reduce_max | solution.py:210
  66.7 0.7 reshape.303.pos_ref
  67.4 0.7 stack.41.geo_ref
  68.1 12.1 %shard_map.84 = f32[32,2,64,128]{3,2,1,0:T(8,128)} custom-call(f32[5]{0:T(128)} %stack.41.geo_ref, f32[4224]{0:T(1024)} %reshape.303.pos_ref, f32[128,512]{1,0:T(8,128)} %get-tuple-element.36.xr_ref, f32[128,512]{1,0:T(8,128)} %get-tuple-element.35.xc_ref), custom_call_target="tpu_custom_call" | custom-call | tf_op jit(solution)/shard_map/pallas_call | solution.py:105
  80.1 2.2 %reduce_sum.18 = f32[32,2,64]{2,1,0:T(2,128)S(1)} reduce(f32[32,2,64,128]{3,2,1,0:T(8,128)} %shard_map.84, f32[]{:T(128)} %constant.45.clone.1), dimensions={3}, to_apply=%region_2.3 | reduce | flops 520192 | bytes 2113540 | tf_op jit(solution)/shard_map/reduce_sum | solution.py:221
  82.5 0.7 broadcast_in_dim.43
  83.2 8.1 %all-to-all-start.1 = ((f32[256,1,128]{2,1,0:T(1,128)}), f32[256,1,128]{2,1,0:T(1,128)S(1)}, u32[]{:S(2)}, u32[]{:S(2)}) async-start(f32[256,1,128]{2,1,0:T(1,128)} %bitcast.38), calls=%async_computation.1 | async-start | bytes 262144 | tf_op jit(solution)/shard_map/all_to_all | solution.py:226
  91.3 2.7 %fusion.96 = f32[128,512]{1,0:T(8,128)} fusion(f32[140,524]{1,0:T(8,128)S(1)} %and_convert_fusion, s32[2,128,512]{2,1,0:T(8,128)S(1)} %copy-done.2), kind=kLoop, calls=%fused_computation.294 | loop fusion | flops 11010048 | bytes 8126464 | tf_op jit(solution)/shard_map/sub | solution.py:191
  94.0 10.0 %all-to-all-done.1 = f32[256,1,128]{2,1,0:T(1,128)S(1)} async-done(((f32[256,1,128]{2,1,0:T(1,128)}), f32[256,1,128]{2,1,0:T(1,128)S(1)}, u32[]{:S(2)}, u32[]{:S(2)}) %all-to-all-start.1) | async-done | bytes 131104 | tf_op jit(solution)/shard_map/all_to_all | solution.py:226
  104.5 0.6 copy.17
  (46 shorter events, 3.6 us)
Async XLA Ops:
  0.6 25.0 %copy-start.1 = (f32[2,128,512]{2,1,0:T(8,128)S(1)}, f32[2,128,512]{2,1,0:T(8,128)}, u32[]{:S(2)}) copy-start(f32[2,128,512]{2,1,0:T(8,128)} %param.5) | copy-start | bytes 1572868
  0.6 25.0 %copy-start = (f32[2,128,512]{2,1,0:T(8,128)S(1)}, f32[2,128,512]{2,1,0:T(8,128)}, u32[]{:S(2)}) copy-start(f32[2,128,512]{2,1,0:T(8,128)} %param.6) | copy-start | bytes 1572868
  0.7 8.9 %copy-start.9 = (f32[64,2]{0,1:T(2,128)S(1)}, f32[64,2]{0,1:T(2,128)}, u32[]{:S(2)}) copy-start(f32[64,2]{0,1:T(2,128)} %param.8) | copy-start | bytes 1540
  0.7 9.1 %copy-start.11 = (s32[1,4]{1,0:T(1,128)S(1)}, s32[1,4]{1,0:T(1,128)}, u32[]{:S(2)}) copy-start(s32[1,4]{1,0:T(1,128)} %param.9) | copy-start | bytes 52
  2.7 22.3 %collective-permute-start = (f32[6,6,512]{2,1,0:T(8,128)S(1)}, f32[6,6,512]{2,1,0:T(8,128)S(1)}, u32[]{:S(2)}, u32[]{:S(2)}) collective-permute-start(f32[6,6,512]{2,1,0:T(8,128)S(1)} %get-tuple-element.33), channel_id=1, source_target_pairs={{0,8},{8,16},{16,24},{24,32},{32,40},{40,48},{48,56},{56,64},{64,7... | collective-permute-start | bytes 221192 | tf_op jit(solution)/shard_map/ppermute | solution.py:124
  7.6 18.0 %collective-permute-start.1 = (f32[6,6,512]{2,1,0:T(8,128)S(1)}, f32[6,6,512]{2,1,0:T(8,128)}, u32[]{:S(2)}, u32[]{:S(2)}) collective-permute-start(f32[6,6,512]{2,1,0:T(8,128)S(1)} %get-tuple-element.34), channel_id=1, source_target_pairs={{8,0},{16,8},{24,16},{32,24},{40,32},{48,40},{56,48},{64,56},{72,6... | collective-permute-start | bytes 221192 | tf_op jit(solution)/shard_map/ppermute | solution.py:125
  10.5 22.1 %all-to-all-start = ((f32[32,1,132]{2,1,0:T(1,128)}), f32[32,1,132]{2,1,0:T(1,128)S(1)}, u32[]{:S(2)}, u32[]{:S(2)}) async-start(f32[32,1,132]{2,1,0:T(1,128)} %broadcast_in_dim.23), calls=%async_computation | async-start | bytes 65536 | tf_op jit(solution)/shard_map/all_to_all | solution.py:202
  25.0 0.6 copy-start.4
  27.5 5.7 %collective-permute-start.2 = (f32[5040]{0:T(1024)}, f32[5040]{0:T(1024)S(1)}, u32[]{:S(2)}, u32[]{:S(2)}) collective-permute-start(f32[5040]{0:T(1024)} %reshape.299), channel_id=1, source_target_pairs={{0,1},{1,2},{2,3},{3,4},{4,5},{5,6},{6,7},{8,9},{9,10},{10,11},{11... | collective-permute-start | bytes 60488 | tf_op jit(solution)/shard_map/ppermute | solution.py:124
  30.0 5.2 %collective-permute-start.3 = (f32[5040]{0:T(1024)S(1)}, f32[5040]{0:T(1024)}, u32[]{:S(2)}, u32[]{:S(2)}) collective-permute-start(f32[5040]{0:T(1024)S(1)} %reshape.301), channel_id=1, source_target_pairs={{1,0},{2,1},{3,2},{4,3},{5,4},{6,5},{7,6},{9,8},{10,9},{11,10},{12... | collective-permute-start | bytes 60488 | tf_op jit(solution)/shard_map/ppermute | solution.py:125
  36.1 2.2 %copy-start.5 = (f32[6,6,512]{2,1,0:T(8,128)S(1)}, f32[6,6,512]{2,1,0:T(8,128)}, u32[]{:S(2)}) copy-start(f32[6,6,512]{2,1,0:T(8,128)} %copy-done.4) | copy-start | bytes 221188
  47.0 6.1 %copy-start.6 = (pred[134,518]{1,0:T(8,128)(4,1)S(1)}, pred[134,518]{1,0:T(8,128)(4,1)}, u32[]{:S(2)}) copy-start(pred[134,518]{1,0:T(8,128)(4,1)} %slice_compare_fusion) | copy-start | bytes 208240
  62.7 1.2 %copy-start.8 = (f32[512]{0:T(512)S(1)}, f32[512]{0:T(512)}, u32[]{:S(2)}) copy-start(f32[512]{0:T(512)} %add_convert_fusion) | copy-start | bytes 6148
  62.7 1.2 %copy-start.10 = (f32[128]{0:T(128)S(1)}, f32[128]{0:T(128)}, u32[]{:S(2)}) copy-start(f32[128]{0:T(128)} %add_convert_fusion.1) | copy-start | bytes 1540
  62.7 3.9 %copy-start.7 = (f32[32,1,132]{2,0,1:T(8,128)S(1)}, f32[32,1,132]{2,0,1:T(8,128)}, u32[]{:S(2)}) copy-start(f32[32,1,132]{2,0,1:T(8,128)} %copy.20) | copy-start | bytes 50692
  63.9 18.5 %copy-start.3 = (f32[2,128,512]{2,1,0:T(8,128)}, f32[2,128,512]{2,1,0:T(8,128)S(1)}, u32[]{:S(2)}) copy-start(f32[2,128,512]{2,1,0:T(8,128)S(1)} %get-tuple-element.16) | copy-start | bytes 1572868
  68.1 23.2 %copy-start.2 = (s32[2,128,512]{2,1,0:T(8,128)S(1)}, s32[2,128,512]{2,1,0:T(8,128)}, u32[]{:S(2)}) copy-start(s32[2,128,512]{2,1,0:T(8,128)} %param.7) | copy-start | bytes 1572868
  83.2 20.8 %all-to-all-start.1 = ((f32[256,1,128]{2,1,0:T(1,128)}), f32[256,1,128]{2,1,0:T(1,128)S(1)}, u32[]{:S(2)}, u32[]{:S(2)}) async-start(f32[256,1,128]{2,1,0:T(1,128)} %bitcast.38), calls=%async_computation.1 | async-start | bytes 262144 | tf_op jit(solution)/shard_map/all_to_all | solution.py:226

commit v12 on v10

--- a/solution.py
+++ b/solution.py
@@ -12,7 +12,6 @@
 
 
 def contact_kernel(geo_ref, pos_ref, xr_ref, xc_ref, out_ref):
-    out_ref[...] = jnp.zeros_like(out_ref)
     blocks, _, panels, _ = out_ref.shape
     rows, cols = xr_ref.shape
     row_tiles = rows // 8
@@ -84,6 +83,10 @@
         listed = pos_ref[block * stride + 2 * panels] == my_tile
         for slot in range(1, listing):
             listed = listed | (pos_ref[block * stride + 2 * panels + slot] == my_tile)
+
+        @pl.when(jnp.logical_not(listed))
+        def _():
+            out_ref[block] = jnp.zeros(out_ref.shape[1:], out_ref.dtype)
 
         @pl.when(listed & narrow)
         def _():

time: 109 us -> 110 us (level); the launches traced: 110 us -> 110 us
  no operation moved by 1% of the time
where the time goes in v12:
time: 110 us
  other arithmetic  42 us (38%)
  starting transfers between devices  38.3 us (35%)
  waiting for transfers between devices  12.7 us (12%)
  local copies, waits for them, and re-layouts  7.39 us (7%)
  Pallas kernels  6.94 us (6%)
  between operations  2.24 us (2%)
    all_to_all x1, starting transfers between devices, body(): arrived = lax.all_to_all(spread, ('along', 'across'), 0, 0, tiled=True)  15.2 us
    add x2, other arithmetic, forces(): total_row = total_row + coeff * row_part  13.2 us
    all_to_all x1, starting transfers between devices, body(): lax.all_to_all(jnp.broadcast_to(packed[None], (block_count,) + packed.sha...  12.7 us
    add x2, other arithmetic, forces(): total_col = total_col + coeff * col_part  10.6 us
    all_to_all x1, waiting for transfers between devices, body(): arrived = lax.all_to_all(spread, ('along', 'across'), 0, 0, tiled=True)  10.2 us
    ppermute x2, starting transfers between devices, with_halo(): low = lax.ppermute(low, axis, forward).reshape(strip)  7.22 us
    pallas_call x1, Pallas kernels, contact_sums(): pl.pallas_call(contact_kernel, out_shape=jax.ShapeDtypeStruct((blocks, 2,...  6.94 us
    ppermute x2, starting transfers between devices, with_halo(): high = lax.ppermute(high, axis, backward).reshape(strip)  3.21 us
  transfers between devices with their start and end apart: 6, of which 2 were waited for; matrix products, arithmetic and copies ran while one was open for 10% of the time, Pallas kernels for 0%

profile of v12, /device:TPU:1, one launch (start us, length us, event | category | flops | bytes accessed | tf_op | source)
XLA Modules:
  0.0 109.6 jit_solution(8714503285711947991)
XLA Ops:
  0.7 1.1 convert_element_type.569
  1.7 0.8 pad_maximum_fusion.18
  2.6 4.9 %collective-permute-start = (f32[6,6,512]{2,1,0:T(8,128)S(1)}, f32[6,6,512]{2,1,0:T(8,128)S(1)}, u32[]{:S(2)}, u32[]{:S(2)}) collective-permute-start(f32[6,6,512]{2,1,0:T(8,128)S(1)} %get-tuple-element.33), channel_id=1, source_target_pairs={{0,8},{8,16},{16,24},{24,32},{32,40},{40,48},{48,56},{56,64},{64,7... | collective-permute-start | bytes 221192 | tf_op jit(solution)/shard_map/ppermute | solution.py:127
  7.5 1.9 %collective-permute-start.1 = (f32[6,6,512]{2,1,0:T(8,128)S(1)}, f32[6,6,512]{2,1,0:T(8,128)}, u32[]{:S(2)}, u32[]{:S(2)}) collective-permute-start(f32[6,6,512]{2,1,0:T(8,128)S(1)} %get-tuple-element.34), channel_id=1, source_target_pairs={{8,0},{16,8},{24,16},{32,24},{40,32},{48,40},{56,48},{64,56},{72,6... | collective-permute-start | bytes 221192 | tf_op jit(solution)/shard_map/ppermute | solution.py:128
  9.7 0.6 broadcast_in_dim.35
  10.4 12.7 %all-to-all-start = ((f32[32,1,132]{2,1,0:T(1,128)}), f32[32,1,132]{2,1,0:T(1,128)S(1)}, u32[]{:S(2)}, u32[]{:S(2)}) async-start(f32[32,1,132]{2,1,0:T(1,128)} %broadcast_in_dim.35), calls=%async_computation | async-start | bytes 65536 | tf_op jit(solution)/shard_map/all_to_all | solution.py:202
  23.2 1.3 %fusion.50 = s32[1,134,518]{2,1,0:T(8,128)S(1)} fusion(f32[140,524]{1,0:T(8,128)S(1)} %and_convert_fusion), kind=kLoop, calls=%fused_computation.129 | loop fusion | flops 2845892 | bytes 4164720 | tf_op jit(solution)/shard_map/stack | solution.py:188
  24.5 1.2 %fusion.78 = s32[1,134,518]{2,1,0:T(8,128)S(1)} fusion(f32[140,524]{1,0:T(8,128)S(1)} %and_convert_fusion), kind=kLoop, calls=%fused_computation.171 | loop fusion | flops 2845892 | bytes 4164720 | tf_op jit(solution)/shard_map/stack | solution.py:188
  25.8 0.8 slice_compare_fusion
  27.2 0.6 copy-done.4
  27.8 1.0 pad_maximum_fusion.5
  28.8 0.8 reshape.213
  29.7 2.3 %collective-permute-start.2 = (f32[5040]{0:T(1024)}, f32[5040]{0:T(1024)S(1)}, u32[]{:S(2)}, u32[]{:S(2)}) collective-permute-start(f32[5040]{0:T(1024)} %reshape.213), channel_id=1, source_target_pairs={{0,1},{1,2},{2,3},{3,4},{4,5},{5,6},{6,7},{8,9},{9,10},{10,11},{11... | collective-permute-start | bytes 60488 | tf_op jit(solution)/shard_map/ppermute | solution.py:127
  32.2 1.3 %collective-permute-start.3 = (f32[5040]{0:T(1024)S(1)}, f32[5040]{0:T(1024)}, u32[]{:S(2)}, u32[]{:S(2)}) collective-permute-start(f32[5040]{0:T(1024)S(1)} %reshape.215), channel_id=1, source_target_pairs={{1,0},{2,1},{3,2},{4,3},{5,4},{6,5},{7,6},{9,8},{10,9},{11,10},{12... | collective-permute-start | bytes 60488 | tf_op jit(solution)/shard_map/ppermute | solution.py:128
  34.9 2.5 %collective-permute-done.3 = f32[5040]{0:T(1024)} collective-permute-done((f32[5040]{0:T(1024)S(1)}, f32[5040]{0:T(1024)}, u32[]{:S(2)}, u32[]{:S(2)}) %collective-permute-start.3) | collective-permute-done | bytes 20192 | tf_op jit(solution)/shard_map/ppermute | solution.py:128
  37.4 0.9 reshape.216
  38.3 1.9 %pad_maximum_fusion = f32[6,140,524]{2,1,0:T(8,128)S(1)} fusion(f32[6,140,6]{2,1,0:T(8,128)S(1)} %reshape.216, f32[6,6,512]{2,1,0:T(8,128)} %collective-permute-done.1, f32[2,128,512]{2,1,0:T(8,128)S(1)} %convert_element_type.569, f32[2,128,512]{2,1,0:T(8,128)S(1)} %copy-done, f32[2,128,512]{2,1,0:T(8,128)S(1)} %copy-done.1, f32[6,6,512]{2,1,0:T(8,128)} %copy-done.4, ...), kind=kLoop, calls=%fused_computation | loop fusion | flops 2640960 | bytes 3521280 | tf_op jit(solution)/shard_map/concatenate | solution.py:129
  40.5 8.7 %multiply_add_fusion.1 = (f32[1,134,518]{2,1,0:T(8,128)S(1)}, f32[1,134,518]{2,1,0:T(8,128)S(1)}, f32[1,134,518]{2,1,0:T(8,128)S(1)}, f32[1,134,518]{2,1,0:T(8,128)S(1)}, f32[1,134,518]{2,1,0:T(8,128)S(1)}) fusion(s32[2,134,518]{2,1,0:T(8,128)S(1)} %fusion, f32[6,140,524]{2,1,0:T(8,128)S(1)} %pad_maximum_fusion, f32[6,6,512]{2,1,0:T(8,128)} %collective-permute-done.1, ...), kind=kLoop, calls=%fused_computation.212 | loop fusion | flops 27695388 | bytes 18697168 | tf_op jit(solution)/shard_map/add | solution.py:160
  49.2 6.1 %multiply_add_fusion = f32[1,134,518]{2,1,0:T(8,128)S(1)} fusion(f32[1,134,518]{2,1,0:T(8,128)S(1)} %get-tuple-element.30, f32[1,134,518]{2,1,0:T(8,128)S(1)} %get-tuple-element.29, f32[1,134,518]{2,1,0:T(8,128)S(1)} %get-tuple-element.28, f32[1,134,518]{2,1,0:T(8,128)S(1)} %get-tuple-element.27, s32[2,134,518]{2,1,0:T(8,128)S(1)} %fusion, ...), kind=kLoop, calls=%fused_computation.211 | loop fusion | flops 25890676 | bytes 16936528 | tf_op jit(solution)/shard_map/add | solution.py:161
  55.8 4.6 %multiply_add_fusion.3 = f32[1,128,512]{2,1,0:T(8,128)S(1)} fusion(s32[2,134,518]{2,1,0:T(8,128)S(1)} %fusion, f32[2,134,518]{2,1,0:T(8,128)S(1)} %get-tuple-element.24), kind=kLoop, calls=%fused_computation.433 | loop fusion | flops 24838144 | bytes 15990784 | tf_op jit(solution)/shard_map/add | solution.py:160
  60.4 4.5 %multiply_add_fusion.2 = f32[1,128,512]{2,1,0:T(8,128)S(1)} fusion(s32[2,134,518]{2,1,0:T(8,128)S(1)} %fusion, f32[2,134,518]{2,1,0:T(8,128)S(1)} %get-tuple-element.24), kind=kLoop, calls=%fused_computation.432 | loop fusion | flops 24838144 | bytes 15990784 | tf_op jit(solution)/shard_map/add | solution.py:161
  65.0 1.2 %slice_add_fusion.3 = (f32[2,128,512]{2,1,0:T(8,128)S(1)}, f32[2,128,512]{2,1,0:T(8,128)}) fusion(f32[2,134,518]{2,1,0:T(8,128)S(1)} %get-tuple-element.24, f32[1,128,512]{2,1,0:T(8,128)S(1)} %multiply_add_fusion.2, f32[1,128,512]{2,1,0:T(8,128)S(1)} %multiply_add_fusion.3, f32[2,134,518]{2,1,0:T(8,128)S(1)} %get-tuple-element.25), kind=kLoop, calls=%fused_computation.8 | loop fusion | flops 655360 | bytes 2621440 | tf_op jit(solution)/shard_map/add | solution.py:197
  66.1 1.6 %fusion.148 = (f32[]{:T(128)}, f32[]{:T(128)}, f32[128,512]{1,0:T(8,128)}, f32[128,512]{1,0:T(8,128)}) fusion(f32[2,128,512]{2,1,0:T(8,128)S(1)} %get-tuple-element.16, f32[512]{0:T(512)S(1)} %copy-done.8, f32[128]{0:T(128)S(1)} %copy-done.10), kind=kLoop, calls=%fused_computation.371 | loop fusion | flops 393214 | bytes 1051144 | tf_op jit(solution)/shard_map/reduce_max | solution.py:210
  69.0 0.7 reshape.217.pos_ref
  69.7 0.7 stack.47.geo_ref
  70.4 6.9 %shard_map.84 = f32[32,2,64,128]{3,2,1,0:T(8,128)} custom-call(f32[5]{0:T(128)} %stack.47.geo_ref, f32[4224]{0:T(1024)} %reshape.217.pos_ref, f32[128,512]{1,0:T(8,128)} %get-tuple-element.36.xr_ref, f32[128,512]{1,0:T(8,128)} %get-tuple-element.35.xc_ref), custom_call_target="tpu_custom_call" | custom-call | tf_op jit(solution)/shard_map/pallas_call | solution.py:108
  77.3 2.2 %reduce_sum.18 = f32[32,2,64]{2,1,0:T(2,128)S(1)} reduce(f32[32,2,64,128]{3,2,1,0:T(8,128)} %shard_map.84, f32[]{:T(128)} %constant.45.clone.1), dimensions={3}, to_apply=%region_2.3 | reduce | flops 520192 | bytes 2113540 | tf_op jit(solution)/shard_map/reduce_sum | solution.py:221
  79.7 0.7 broadcast_in_dim.39
  80.4 15.2 %all-to-all-start.1 = ((f32[256,1,128]{2,1,0:T(1,128)}), f32[256,1,128]{2,1,0:T(1,128)S(1)}, u32[]{:S(2)}, u32[]{:S(2)}) async-start(f32[256,1,128]{2,1,0:T(1,128)} %bitcast.40), calls=%async_computation.1 | async-start | bytes 262144 | tf_op jit(solution)/shard_map/all_to_all | solution.py:226
  95.6 2.7 %fusion.152 = f32[128,512]{1,0:T(8,128)} fusion(f32[140,524]{1,0:T(8,128)S(1)} %and_convert_fusion, s32[2,128,512]{2,1,0:T(8,128)S(1)} %copy-done.2), kind=kLoop, calls=%fused_computation.378 | loop fusion | flops 11010048 | bytes 8126464 | tf_op jit(solution)/shard_map/sub | solution.py:191
  98.3 10.2 %all-to-all-done.1 = f32[256,1,128]{2,1,0:T(1,128)S(1)} async-done(((f32[256,1,128]{2,1,0:T(1,128)}), f32[256,1,128]{2,1,0:T(1,128)S(1)}, u32[]{:S(2)}, u32[]{:S(2)}) %all-to-all-start.1) | async-done | bytes 131104 | tf_op jit(solution)/shard_map/all_to_all | solution.py:226
  108.9 0.6 copy.17
  (45 shorter events, 3.9 us)
Async XLA Ops:
  0.6 8.8 %copy-start.9 = (f32[64,2]{0,1:T(2,128)S(1)}, f32[64,2]{0,1:T(2,128)}, u32[]{:S(2)}) copy-start(f32[64,2]{0,1:T(2,128)} %param.8) | copy-start | bytes 1540
  0.6 9.1 %copy-start.11 = (s32[1,4]{1,0:T(1,128)S(1)}, s32[1,4]{1,0:T(1,128)}, u32[]{:S(2)}) copy-start(s32[1,4]{1,0:T(1,128)} %param.9) | copy-start | bytes 52
  2.6 24.6 %collective-permute-start = (f32[6,6,512]{2,1,0:T(8,128)S(1)}, f32[6,6,512]{2,1,0:T(8,128)S(1)}, u32[]{:S(2)}, u32[]{:S(2)}) collective-permute-start(f32[6,6,512]{2,1,0:T(8,128)S(1)} %get-tuple-element.33), channel_id=1, source_target_pairs={{0,8},{8,16},{16,24},{24,32},{32,40},{40,48},{48,56},{56,64},{64,7... | collective-permute-start | bytes 221192 | tf_op jit(solution)/shard_map/ppermute | solution.py:127
  7.5 20.3 %collective-permute-start.1 = (f32[6,6,512]{2,1,0:T(8,128)S(1)}, f32[6,6,512]{2,1,0:T(8,128)}, u32[]{:S(2)}, u32[]{:S(2)}) collective-permute-start(f32[6,6,512]{2,1,0:T(8,128)S(1)} %get-tuple-element.34), channel_id=1, source_target_pairs={{8,0},{16,8},{24,16},{32,24},{40,32},{48,40},{56,48},{64,56},{72,6... | collective-permute-start | bytes 221192 | tf_op jit(solution)/shard_map/ppermute | solution.py:128
  10.4 23.7 %all-to-all-start = ((f32[32,1,132]{2,1,0:T(1,128)}), f32[32,1,132]{2,1,0:T(1,128)S(1)}, u32[]{:S(2)}, u32[]{:S(2)}) async-start(f32[32,1,132]{2,1,0:T(1,128)} %broadcast_in_dim.35), calls=%async_computation | async-start | bytes 65536 | tf_op jit(solution)/shard_map/all_to_all | solution.py:202
  24.5 3.3 %copy-start = (f32[2,128,512]{2,1,0:T(8,128)S(1)}, f32[2,128,512]{2,1,0:T(8,128)}, u32[]{:S(2)}) copy-start(f32[2,128,512]{2,1,0:T(8,128)} %param.6) | copy-start | bytes 1572868
  24.5 3.3 %copy-start.1 = (f32[2,128,512]{2,1,0:T(8,128)S(1)}, f32[2,128,512]{2,1,0:T(8,128)}, u32[]{:S(2)}) copy-start(f32[2,128,512]{2,1,0:T(8,128)} %param.5) | copy-start | bytes 1572868
  27.2 0.6 copy-start.4
  29.7 5.0 %collective-permute-start.2 = (f32[5040]{0:T(1024)}, f32[5040]{0:T(1024)S(1)}, u32[]{:S(2)}, u32[]{:S(2)}) collective-permute-start(f32[5040]{0:T(1024)} %reshape.213), channel_id=1, source_target_pairs={{0,1},{1,2},{2,3},{3,4},{4,5},{5,6},{6,7},{8,9},{9,10},{10,11},{11... | collective-permute-start | bytes 60488 | tf_op jit(solution)/shard_map/ppermute | solution.py:127
  32.2 5.2 %collective-permute-start.3 = (f32[5040]{0:T(1024)S(1)}, f32[5040]{0:T(1024)}, u32[]{:S(2)}, u32[]{:S(2)}) collective-permute-start(f32[5040]{0:T(1024)S(1)} %reshape.215), channel_id=1, source_target_pairs={{1,0},{2,1},{3,2},{4,3},{5,4},{6,5},{7,6},{9,8},{10,9},{11,10},{12... | collective-permute-start | bytes 60488 | tf_op jit(solution)/shard_map/ppermute | solution.py:128
  38.3 2.2 %copy-start.5 = (f32[6,6,512]{2,1,0:T(8,128)S(1)}, f32[6,6,512]{2,1,0:T(8,128)}, u32[]{:S(2)}) copy-start(f32[6,6,512]{2,1,0:T(8,128)} %copy-done.4) | copy-start | bytes 221188
  49.2 6.1 %copy-start.6 = (pred[134,518]{1,0:T(8,128)(4,1)S(1)}, pred[134,518]{1,0:T(8,128)(4,1)}, u32[]{:S(2)}) copy-start(pred[134,518]{1,0:T(8,128)(4,1)} %slice_compare_fusion) | copy-start | bytes 208240
  64.9 1.2 %copy-start.8 = (f32[512]{0:T(512)S(1)}, f32[512]{0:T(512)}, u32[]{:S(2)}) copy-start(f32[512]{0:T(512)} %add_convert_fusion) | copy-start | bytes 6148
  64.9 1.2 %copy-start.10 = (f32[128]{0:T(128)S(1)}, f32[128]{0:T(128)}, u32[]{:S(2)}) copy-start(f32[128]{0:T(128)} %add_convert_fusion.1) | copy-start | bytes 1540
  65.0 4.0 %copy-start.7 = (f32[32,1,132]{2,0,1:T(8,128)S(1)}, f32[32,1,132]{2,0,1:T(8,128)}, u32[]{:S(2)}) copy-start(f32[32,1,132]{2,0,1:T(8,128)} %copy.20) | copy-start | bytes 50692
  66.1 13.5 %copy-start.3 = (f32[2,128,512]{2,1,0:T(8,128)}, f32[2,128,512]{2,1,0:T(8,128)S(1)}, u32[]{:S(2)}) copy-start(f32[2,128,512]{2,1,0:T(8,128)S(1)} %get-tuple-element.16) | copy-start | bytes 1572868
  70.4 25.2 %copy-start.2 = (s32[2,128,512]{2,1,0:T(8,128)S(1)}, s32[2,128,512]{2,1,0:T(8,128)}, u32[]{:S(2)}) copy-start(s32[2,128,512]{2,1,0:T(8,128)} %param.7) | copy-start | bytes 1572868
  80.4 28.1 %all-to-all-start.1 = ((f32[256,1,128]{2,1,0:T(1,128)}), f32[256,1,128]{2,1,0:T(1,128)S(1)}, u32[]{:S(2)}, u32[]{:S(2)}) async-start(f32[256,1,128]{2,1,0:T(1,128)} %bitcast.40), calls=%async_computation.1 | async-start | bytes 262144 | tf_op jit(solution)/shard_map/all_to_all | solution.py:226

commit v13 on v10

--- a/solution.py
+++ b/solution.py
@@ -58,7 +58,7 @@
             store(block, j, accs)
             return carry
 
-        lax.fori_loop(0, panels, per_panel, 0, unroll=8)
+        lax.fori_loop(0, panels, per_panel, 0, unroll=16)
 
     def per_block_wide(block):
         def per_panel(j, carry):

time: 109 us -> 108 us (level); the launches traced: 110 us -> 108 us
  starting transfers between devices: 39 us -> 34.9 us
  Pallas kernels: 6.89 us -> 8.54 us
    all_to_all x1, starting transfers between devices: 15.9 us -> 11.8 us  [body(): arrived = lax.all_to_all(spread, ('along', 'across'), 0, 0, tiled=True)]
    pallas_call x1, Pallas kernels: 6.89 us -> 8.54 us  [contact_sums(): pl.pallas_call(contact_kernel, out_shape=jax.ShapeDtypeStruct((blocks, 2,...]
where the time goes in v13:
time: 108 us
  other arithmetic  42 us (39%)
  starting transfers between devices  34.9 us (32%)
  waiting for transfers between devices  12.6 us (12%)
  Pallas kernels  8.54 us (8%)
  local copies, waits for them, and re-layouts  7.39 us (7%)
  between operations  2.24 us (2%)
    add x2, other arithmetic, forces(): total_row = total_row + coeff * row_part  13.2 us
    all_to_all x1, starting transfers between devices, body(): lax.all_to_all(jnp.broadcast_to(packed[None], (block_count,) + packed.sha...  12.7 us
    all_to_all x1, starting transfers between devices, body(): arrived = lax.all_to_all(spread, ('along', 'across'), 0, 0, tiled=True)  11.8 us
    add x2, other arithmetic, forces(): total_col = total_col + coeff * col_part  10.6 us
    all_to_all x1, waiting for transfers between devices, body(): arrived = lax.all_to_all(spread, ('along', 'across'), 0, 0, tiled=True)  10.1 us
    pallas_call x1, Pallas kernels, contact_sums(): pl.pallas_call(contact_kernel, out_shape=jax.ShapeDtypeStruct((blocks, 2,...  8.54 us
    ppermute x2, starting transfers between devices, with_halo(): low = lax.ppermute(low, axis, forward).reshape(strip)  7.22 us
    ppermute x2, starting transfers between devices, with_halo(): high = lax.ppermute(high, axis, backward).reshape(strip)  3.21 us
  transfers between devices with their start and end apart: 6, of which 2 were waited for; matrix products, arithmetic and copies ran while one was open for 10% of the time, Pallas kernels for 0%

profile of v13, /device:TPU:1, one launch (start us, length us, event | category | flops | bytes accessed | tf_op | source)
XLA Modules:
  0.0 107.6 jit_solution(11677097931221923749)
XLA Ops:
  0.7 1.1 %convert_element_type.569 = f32[2,128,512]{2,1,0:T(8,128)S(1)} convert(s32[2,128,512]{2,1,0:T(8,128)} %param.7) | non-fusion elementwise | flops 131072 | bytes 1048576 | tf_op jit(solution)/shard_map/convert_element_type | solution.py:170
  1.7 0.8 pad_maximum_fusion.18
  2.6 4.9 %collective-permute-start = (f32[6,6,512]{2,1,0:T(8,128)S(1)}, f32[6,6,512]{2,1,0:T(8,128)S(1)}, u32[]{:S(2)}, u32[]{:S(2)}) collective-permute-start(f32[6,6,512]{2,1,0:T(8,128)S(1)} %get-tuple-element.33), channel_id=1, source_target_pairs={{0,8},{8,16},{16,24},{24,32},{32,40},{40,48},{48,56},{56,64},{64,7... | collective-permute-start | bytes 221192 | tf_op jit(solution)/shard_map/ppermute | solution.py:124
  7.5 1.9 %collective-permute-start.1 = (f32[6,6,512]{2,1,0:T(8,128)S(1)}, f32[6,6,512]{2,1,0:T(8,128)}, u32[]{:S(2)}, u32[]{:S(2)}) collective-permute-start(f32[6,6,512]{2,1,0:T(8,128)S(1)} %get-tuple-element.34), channel_id=1, source_target_pairs={{8,0},{16,8},{24,16},{32,24},{40,32},{48,40},{56,48},{64,56},{72,6... | collective-permute-start | bytes 221192 | tf_op jit(solution)/shard_map/ppermute | solution.py:125
  9.7 0.6 broadcast_in_dim.35
  10.4 12.7 %all-to-all-start = ((f32[32,1,132]{2,1,0:T(1,128)}), f32[32,1,132]{2,1,0:T(1,128)S(1)}, u32[]{:S(2)}, u32[]{:S(2)}) async-start(f32[32,1,132]{2,1,0:T(1,128)} %broadcast_in_dim.35), calls=%async_computation | async-start | bytes 65536 | tf_op jit(solution)/shard_map/all_to_all | solution.py:199
  23.2 1.3 %fusion.50 = s32[1,134,518]{2,1,0:T(8,128)S(1)} fusion(f32[140,524]{1,0:T(8,128)S(1)} %and_convert_fusion), kind=kLoop, calls=%fused_computation.129 | loop fusion | flops 2845892 | bytes 4164720 | tf_op jit(solution)/shard_map/stack | solution.py:185
  24.5 1.2 %fusion.78 = s32[1,134,518]{2,1,0:T(8,128)S(1)} fusion(f32[140,524]{1,0:T(8,128)S(1)} %and_convert_fusion), kind=kLoop, calls=%fused_computation.171 | loop fusion | flops 2845892 | bytes 4164720 | tf_op jit(solution)/shard_map/stack | solution.py:185
  25.8 0.8 slice_compare_fusion
  27.2 0.6 copy-done.4
  27.8 1.0 pad_maximum_fusion.5
  28.8 0.8 reshape.213
  29.7 2.3 %collective-permute-start.2 = (f32[5040]{0:T(1024)}, f32[5040]{0:T(1024)S(1)}, u32[]{:S(2)}, u32[]{:S(2)}) collective-permute-start(f32[5040]{0:T(1024)} %reshape.213), channel_id=1, source_target_pairs={{0,1},{1,2},{2,3},{3,4},{4,5},{5,6},{6,7},{8,9},{9,10},{10,11},{11... | collective-permute-start | bytes 60488 | tf_op jit(solution)/shard_map/ppermute | solution.py:124
  32.2 1.3 %collective-permute-start.3 = (f32[5040]{0:T(1024)S(1)}, f32[5040]{0:T(1024)}, u32[]{:S(2)}, u32[]{:S(2)}) collective-permute-start(f32[5040]{0:T(1024)S(1)} %reshape.215), channel_id=1, source_target_pairs={{1,0},{2,1},{3,2},{4,3},{5,4},{6,5},{7,6},{9,8},{10,9},{11,10},{12... | collective-permute-start | bytes 60488 | tf_op jit(solution)/shard_map/ppermute | solution.py:125
  34.9 2.5 %collective-permute-done.3 = f32[5040]{0:T(1024)} collective-permute-done((f32[5040]{0:T(1024)S(1)}, f32[5040]{0:T(1024)}, u32[]{:S(2)}, u32[]{:S(2)}) %collective-permute-start.3) | collective-permute-done | bytes 20192 | tf_op jit(solution)/shard_map/ppermute | solution.py:125
  37.4 0.9 reshape.216
  38.3 1.9 %pad_maximum_fusion = f32[6,140,524]{2,1,0:T(8,128)S(1)} fusion(f32[6,140,6]{2,1,0:T(8,128)S(1)} %reshape.216, f32[6,6,512]{2,1,0:T(8,128)} %collective-permute-done.1, f32[2,128,512]{2,1,0:T(8,128)S(1)} %convert_element_type.569, f32[2,128,512]{2,1,0:T(8,128)S(1)} %copy-done, f32[2,128,512]{2,1,0:T(8,128)S(1)} %copy-done.1, f32[6,6,512]{2,1,0:T(8,128)} %copy-done.4, ...), kind=kLoop, calls=%fused_computation | loop fusion | flops 2640960 | bytes 3521280 | tf_op jit(solution)/shard_map/concatenate | solution.py:126
  40.5 8.7 %multiply_add_fusion.1 = (f32[1,134,518]{2,1,0:T(8,128)S(1)}, f32[1,134,518]{2,1,0:T(8,128)S(1)}, f32[1,134,518]{2,1,0:T(8,128)S(1)}, f32[1,134,518]{2,1,0:T(8,128)S(1)}, f32[1,134,518]{2,1,0:T(8,128)S(1)}) fusion(s32[2,134,518]{2,1,0:T(8,128)S(1)} %fusion, f32[6,140,524]{2,1,0:T(8,128)S(1)} %pad_maximum_fusion, f32[6,6,512]{2,1,0:T(8,128)} %collective-permute-done.1, ...), kind=kLoop, calls=%fused_computation.212 | loop fusion | flops 27695388 | bytes 18697168 | tf_op jit(solution)/shard_map/add | solution.py:157
  49.2 6.1 %multiply_add_fusion = f32[1,134,518]{2,1,0:T(8,128)S(1)} fusion(f32[1,134,518]{2,1,0:T(8,128)S(1)} %get-tuple-element.30, f32[1,134,518]{2,1,0:T(8,128)S(1)} %get-tuple-element.29, f32[1,134,518]{2,1,0:T(8,128)S(1)} %get-tuple-element.28, f32[1,134,518]{2,1,0:T(8,128)S(1)} %get-tuple-element.27, s32[2,134,518]{2,1,0:T(8,128)S(1)} %fusion, ...), kind=kLoop, calls=%fused_computation.211 | loop fusion | flops 25890676 | bytes 16936528 | tf_op jit(solution)/shard_map/add | solution.py:158
  55.8 4.6 %multiply_add_fusion.3 = f32[1,128,512]{2,1,0:T(8,128)S(1)} fusion(s32[2,134,518]{2,1,0:T(8,128)S(1)} %fusion, f32[2,134,518]{2,1,0:T(8,128)S(1)} %get-tuple-element.24), kind=kLoop, calls=%fused_computation.433 | loop fusion | flops 24838144 | bytes 15990784 | tf_op jit(solution)/shard_map/add | solution.py:157
  60.4 4.5 %multiply_add_fusion.2 = f32[1,128,512]{2,1,0:T(8,128)S(1)} fusion(s32[2,134,518]{2,1,0:T(8,128)S(1)} %fusion, f32[2,134,518]{2,1,0:T(8,128)S(1)} %get-tuple-element.24), kind=kLoop, calls=%fused_computation.432 | loop fusion | flops 24838144 | bytes 15990784 | tf_op jit(solution)/shard_map/add | solution.py:158
  65.0 1.2 %slice_add_fusion.3 = (f32[2,128,512]{2,1,0:T(8,128)S(1)}, f32[2,128,512]{2,1,0:T(8,128)}) fusion(f32[2,134,518]{2,1,0:T(8,128)S(1)} %get-tuple-element.24, f32[1,128,512]{2,1,0:T(8,128)S(1)} %multiply_add_fusion.2, f32[1,128,512]{2,1,0:T(8,128)S(1)} %multiply_add_fusion.3, f32[2,134,518]{2,1,0:T(8,128)S(1)} %get-tuple-element.25), kind=kLoop, calls=%fused_computation.8 | loop fusion | flops 655360 | bytes 2621440 | tf_op jit(solution)/shard_map/add | solution.py:194
  66.1 1.6 %fusion.148 = (f32[]{:T(128)}, f32[]{:T(128)}, f32[128,512]{1,0:T(8,128)}, f32[128,512]{1,0:T(8,128)}) fusion(f32[2,128,512]{2,1,0:T(8,128)S(1)} %get-tuple-element.16, f32[512]{0:T(512)S(1)} %copy-done.8, f32[128]{0:T(128)S(1)} %copy-done.10), kind=kLoop, calls=%fused_computation.371 | loop fusion | flops 393214 | bytes 1051144 | tf_op jit(solution)/shard_map/reduce_max | solution.py:207
  69.0 0.7 reshape.217.pos_ref
  69.7 0.7 stack.47.geo_ref
  70.4 8.5 %shard_map.84 = f32[32,2,64,128]{3,2,1,0:T(8,128)} custom-call(f32[5]{0:T(128)} %stack.47.geo_ref, f32[4224]{0:T(1024)} %reshape.217.pos_ref, f32[128,512]{1,0:T(8,128)} %get-tuple-element.36.xr_ref, f32[128,512]{1,0:T(8,128)} %get-tuple-element.35.xc_ref), custom_call_target="tpu_custom_call" | custom-call | tf_op jit(solution)/shard_map/pallas_call | solution.py:105
  79.0 2.2 %reduce_sum.18 = f32[32,2,64]{2,1,0:T(2,128)S(1)} reduce(f32[32,2,64,128]{3,2,1,0:T(8,128)} %shard_map.84, f32[]{:T(128)} %constant.45.clone.1), dimensions={3}, to_apply=%region_2.3 | reduce | flops 520192 | bytes 2113540 | tf_op jit(solution)/shard_map/reduce_sum | solution.py:218
  81.3 0.7 broadcast_in_dim.39
  82.0 11.8 %all-to-all-start.1 = ((f32[256,1,128]{2,1,0:T(1,128)}), f32[256,1,128]{2,1,0:T(1,128)S(1)}, u32[]{:S(2)}, u32[]{:S(2)}) async-start(f32[256,1,128]{2,1,0:T(1,128)} %bitcast.40), calls=%async_computation.1 | async-start | bytes 262144 | tf_op jit(solution)/shard_map/all_to_all | solution.py:223
  93.8 2.7 %fusion.152 = f32[128,512]{1,0:T(8,128)} fusion(f32[140,524]{1,0:T(8,128)S(1)} %and_convert_fusion, s32[2,128,512]{2,1,0:T(8,128)S(1)} %copy-done.2), kind=kLoop, calls=%fused_computation.378 | loop fusion | flops 11010048 | bytes 8126464 | tf_op jit(solution)/shard_map/sub | solution.py:188
  96.5 10.1 %all-to-all-done.1 = f32[256,1,128]{2,1,0:T(1,128)S(1)} async-done(((f32[256,1,128]{2,1,0:T(1,128)}), f32[256,1,128]{2,1,0:T(1,128)S(1)}, u32[]{:S(2)}, u32[]{:S(2)}) %all-to-all-start.1) | async-done | bytes 131104 | tf_op jit(solution)/shard_map/all_to_all | solution.py:223
  107.0 0.6 copy.17
  (45 shorter events, 3.9 us)
Async XLA Ops:
  0.6 8.8 %copy-start.9 = (f32[64,2]{0,1:T(2,128)S(1)}, f32[64,2]{0,1:T(2,128)}, u32[]{:S(2)}) copy-start(f32[64,2]{0,1:T(2,128)} %param.8) | copy-start | bytes 1540
  0.6 9.1 %copy-start.11 = (s32[1,4]{1,0:T(1,128)S(1)}, s32[1,4]{1,0:T(1,128)}, u32[]{:S(2)}) copy-start(s32[1,4]{1,0:T(1,128)} %param.9) | copy-start | bytes 52
  2.6 24.6 %collective-permute-start = (f32[6,6,512]{2,1,0:T(8,128)S(1)}, f32[6,6,512]{2,1,0:T(8,128)S(1)}, u32[]{:S(2)}, u32[]{:S(2)}) collective-permute-start(f32[6,6,512]{2,1,0:T(8,128)S(1)} %get-tuple-element.33), channel_id=1, source_target_pairs={{0,8},{8,16},{16,24},{24,32},{32,40},{40,48},{48,56},{56,64},{64,7... | collective-permute-start | bytes 221192 | tf_op jit(solution)/shard_map/ppermute | solution.py:124
  7.5 20.3 %collective-permute-start.1 = (f32[6,6,512]{2,1,0:T(8,128)S(1)}, f32[6,6,512]{2,1,0:T(8,128)}, u32[]{:S(2)}, u32[]{:S(2)}) collective-permute-start(f32[6,6,512]{2,1,0:T(8,128)S(1)} %get-tuple-element.34), channel_id=1, source_target_pairs={{8,0},{16,8},{24,16},{32,24},{40,32},{48,40},{56,48},{64,56},{72,6... | collective-permute-start | bytes 221192 | tf_op jit(solution)/shard_map/ppermute | solution.py:125
  10.4 23.7 %all-to-all-start = ((f32[32,1,132]{2,1,0:T(1,128)}), f32[32,1,132]{2,1,0:T(1,128)S(1)}, u32[]{:S(2)}, u32[]{:S(2)}) async-start(f32[32,1,132]{2,1,0:T(1,128)} %broadcast_in_dim.35), calls=%async_computation | async-start | bytes 65536 | tf_op jit(solution)/shard_map/all_to_all | solution.py:199
  24.5 3.3 %copy-start = (f32[2,128,512]{2,1,0:T(8,128)S(1)}, f32[2,128,512]{2,1,0:T(8,128)}, u32[]{:S(2)}) copy-start(f32[2,128,512]{2,1,0:T(8,128)} %param.6) | copy-start | bytes 1572868
  24.5 3.3 %copy-start.1 = (f32[2,128,512]{2,1,0:T(8,128)S(1)}, f32[2,128,512]{2,1,0:T(8,128)}, u32[]{:S(2)}) copy-start(f32[2,128,512]{2,1,0:T(8,128)} %param.5) | copy-start | bytes 1572868
  27.2 0.6 copy-start.4
  29.7 5.0 %collective-permute-start.2 = (f32[5040]{0:T(1024)}, f32[5040]{0:T(1024)S(1)}, u32[]{:S(2)}, u32[]{:S(2)}) collective-permute-start(f32[5040]{0:T(1024)} %reshape.213), channel_id=1, source_target_pairs={{0,1},{1,2},{2,3},{3,4},{4,5},{5,6},{6,7},{8,9},{9,10},{10,11},{11... | collective-permute-start | bytes 60488 | tf_op jit(solution)/shard_map/ppermute | solution.py:124
  32.2 5.2 %collective-permute-start.3 = (f32[5040]{0:T(1024)S(1)}, f32[5040]{0:T(1024)}, u32[]{:S(2)}, u32[]{:S(2)}) collective-permute-start(f32[5040]{0:T(1024)S(1)} %reshape.215), channel_id=1, source_target_pairs={{1,0},{2,1},{3,2},{4,3},{5,4},{6,5},{7,6},{9,8},{10,9},{11,10},{12... | collective-permute-start | bytes 60488 | tf_op jit(solution)/shard_map/ppermute | solution.py:125
  38.3 2.2 %copy-start.5 = (f32[6,6,512]{2,1,0:T(8,128)S(1)}, f32[6,6,512]{2,1,0:T(8,128)}, u32[]{:S(2)}) copy-start(f32[6,6,512]{2,1,0:T(8,128)} %copy-done.4) | copy-start | bytes 221188
  49.2 6.1 %copy-start.6 = (pred[134,518]{1,0:T(8,128)(4,1)S(1)}, pred[134,518]{1,0:T(8,128)(4,1)}, u32[]{:S(2)}) copy-start(pred[134,518]{1,0:T(8,128)(4,1)} %slice_compare_fusion) | copy-start | bytes 208240
  64.9 1.2 %copy-start.8 = (f32[512]{0:T(512)S(1)}, f32[512]{0:T(512)}, u32[]{:S(2)}) copy-start(f32[512]{0:T(512)} %add_convert_fusion) | copy-start | bytes 6148
  64.9 1.2 %copy-start.10 = (f32[128]{0:T(128)S(1)}, f32[128]{0:T(128)}, u32[]{:S(2)}) copy-start(f32[128]{0:T(128)} %add_convert_fusion.1) | copy-start | bytes 1540
  65.0 4.0 %copy-start.7 = (f32[32,1,132]{2,0,1:T(8,128)S(1)}, f32[32,1,132]{2,0,1:T(8,128)}, u32[]{:S(2)}) copy-start(f32[32,1,132]{2,0,1:T(8,128)} %copy.20) | copy-start | bytes 50692
  66.1 15.1 %copy-start.3 = (f32[2,128,512]{2,1,0:T(8,128)}, f32[2,128,512]{2,1,0:T(8,128)S(1)}, u32[]{:S(2)}) copy-start(f32[2,128,512]{2,1,0:T(8,128)S(1)} %get-tuple-element.16) | copy-start | bytes 1572868
  70.4 23.4 %copy-start.2 = (s32[2,128,512]{2,1,0:T(8,128)S(1)}, s32[2,128,512]{2,1,0:T(8,128)}, u32[]{:S(2)}) copy-start(s32[2,128,512]{2,1,0:T(8,128)} %param.7) | copy-start | bytes 1572868
  82.0 24.5 %all-to-all-start.1 = ((f32[256,1,128]{2,1,0:T(1,128)}), f32[256,1,128]{2,1,0:T(1,128)S(1)}, u32[]{:S(2)}, u32[]{:S(2)}) async-start(f32[256,1,128]{2,1,0:T(1,128)} %bitcast.40), calls=%async_computation.1 | async-start | bytes 262144 | tf_op jit(solution)/shard_map/all_to_all | solution.py:223
